TPU v7x, 256 devices: a whole 4x4x8 slice. The times are simulated.
256 devices in a mesh: snap: 4 (over x), line: 64 (over z, y, core).
Axes of the slice: x: 4, y: 4, z: 8, core: 2. Of those that a mesh axis runs over, the one named last changes fastest.
Arguments:
- ptdf_rows: float32 [8192, 20480], P('line'), may hold values from -4 to 4
- plan: float32 [5120, 2048], P(('snap', 'line')), may hold values from 0 to 0.15
- unit_bus: int32 [5120], replicated, may hold values from 0 to 20479
- min_up: int32 [5120], P(('snap', 'line')), may hold values from 1 to 24, as said below
- ramp_lag: int32 [5120], P(('snap', 'line')), may hold values from 1 to 6, as said below
- load_share: float32 [20480], replicated, may hold values from 0.004 to 0.04
- system_load: float32 [2048], P('snap'), may hold values from 0.6 to 1.4
- corridor_order: int32 [4], replicated, may hold values from 0 to 3, each once
- corridor_buses: int32 [4, 2], replicated, may hold values from 0 to 20479, as said below
- corridor_owner: int32 [4], replicated, may hold values from 0 to 63
- corridor_row: int32 [4], replicated, may hold values from 0 to 127
- corridor_ratio: float32 [4], replicated, may hold values from 0.5 to 2
Outputs:
- flows: float32 [8192, 2048], P('line', 'snap')
- corridor_sens: float32 [4, 20480], replicated
Inputs may be any that keep to these rules, and one draw needn't show every extreme that they name: `min_up`: some unit has a window of exactly 24. `ramp_lag`: some unit has a lag of exactly 6. `corridor_buses`: the two buses of a corridor differ.
All inputs are finite; a program needn't handle non-finite values.
Results may differ from a plain program's by a relative error of at most 0.000098.
Values sent between devices are 32-bit elements; how exact they have to be, the bound alone decides.
No kernel may reach another device: no remote copies, remote signals or barrier semaphores. Data moves between devices by JAX's collectives and lax.ppermute only.
A program may use at most 128 MiB of HBM per device.

v0:
```python
import jax
import jax.numpy as jnp
from jax import lax
from jax.sharding import Mesh
from jax.sharding import PartitionSpec as P

WMAX = 24
NC = 4
LINE = ("line_0", "line_1", "line_2")
SNAP_LINE = ("snap", "line_0", "line_1", "line_2")


ramp_gain = 0.5


def in_blocks(x, dim, peers):
    before, after = (x.shape[:dim], x.shape[dim + 1 :])
    return jnp.moveaxis(x.reshape(*before, peers, -1, *after), dim, 0)


def sum_at_owner(x, axis, dim):
    tiles = in_blocks(x, dim, lax.axis_size(axis))
    arrived = lax.all_to_all(tiles, axis, split_axis=0, concat_axis=0, tiled=True)
    return arrived.sum(axis=0)


def summed_rows(x, axes, dim):
    far, near = axes
    tiles = in_blocks(x, dim, lax.axis_size(far))
    nearer = sum_at_owner(tiles, near, dim + 1)
    arrived = lax.all_to_all(nearer, far, split_axis=0, concat_axis=0, tiled=True)
    return arrived.sum(axis=0)


def padded_to(lines, peers):
    spare = -len(lines) % peers
    return jnp.pad(lines, [(0, spare)] + [(0, 0)] * (lines.ndim - 1))


def copy_for_each(x, axis):
    peers = lax.axis_size(axis)
    return lax.all_to_all(jnp.broadcast_to(x[None], (peers, *x.shape)), axis, 0, 0, tiled=True)


def joined_along(tiles, dim):
    lengths = list(tiles.shape[1:])
    lengths[dim] *= tiles.shape[0]
    return jnp.moveaxis(tiles, 0, dim).reshape(lengths)


def gathered_by_axis(x, axes, dim):
    far, near = axes
    leading = copy_for_each(x, far)
    tiles = jnp.swapaxes(copy_for_each(leading, near), 0, 1)
    return joined_along(tiles.reshape(-1, *x.shape), dim)


def total_of(x, axes):
    own = summed_rows(padded_to(x, lax.axis_size(axes[0]) * lax.axis_size(axes[1])), axes, 0)
    whole = gathered_by_axis(own, axes, 0)
    return whole[: len(x)].reshape(x.shape)


def together(arrays, axis):
    ends = [0]
    for a in arrays:
        ends.append(ends[-1] + a.size)
    subtotal = total_of(jnp.concatenate([a.ravel() for a in arrays]), axis)
    return tuple((subtotal[b:e].reshape(a.shape) for a, b, e in zip(arrays, ends, ends[1:])))


def body(
    ptdf_rows,
    plan,
    unit_bus,
    min_up,
    ramp_lag,
    load_share,
    system_load,
    corridor_order,
    corridor_buses,
    corridor_owner,
    corridor_row,
    corridor_ratio,
):
    unit_count, horizon = plan.shape
    snap_count = lax.axis_size("snap")
    line_count = lax.axis_size(LINE)
    padded = jnp.pad(plan, ((0, 0), (WMAX, 0)))
    inverse = 1.0 / min_up.astype(jnp.float32)
    held_mean = jnp.zeros(plan.shape, jnp.float32)
    lagged = jnp.zeros(plan.shape, jnp.float32)
    for offset in range(WMAX):
        shifted = padded[:, WMAX - offset : WMAX - offset + horizon]
        held_mean = held_mean + shifted * jnp.where(offset < min_up, inverse, 0.0)[:, None]
        lagged = lagged + shifted * (ramp_lag == offset).astype(jnp.float32)[:, None]
    dispatch = held_mean + ramp_gain * (plan - lagged)
    unit_blocks = lax.all_to_all(dispatch, "snap", split_axis=1, concat_axis=0, tiled=True)
    order_ids = unit_bus.reshape(snap_count, line_count, unit_count).transpose(1, 0, 2).reshape(-1)
    columns = jnp.take(ptdf_rows, order_ids, axis=1)
    gen_flows = jnp.dot(
        columns,
        lax.all_gather(unit_blocks, LINE, axis=0, tiled=True),
        preferred_element_type=jnp.float32,
        precision=lax.Precision.HIGHEST,
    )
    load_flows = jnp.dot(
        ptdf_rows, load_share, preferred_element_type=jnp.float32, precision=lax.Precision.HIGHEST
    )
    base = gen_flows - load_flows[:, None] * system_load[None, :]
    here = lax.axis_index(LINE)
    picked_rows = []
    picked_flows = []
    for step in range(NC):
        chosen = corridor_order[step]
        local_row = corridor_row[chosen]
        mine = corridor_owner[chosen] == here
        picked_rows.append(jnp.where(mine, ptdf_rows[local_row], 0.0))
        picked_flows.append(jnp.where(mine, base[local_row], 0.0))
    all_rows, all_flows = together(
        (jnp.stack(picked_rows), jnp.stack(picked_flows)), (("line_0", "line_1"), "line_2")
    )
    coeff_list = []
    sens_list = []
    shift_list = []
    ends_list = []
    for step in range(NC):
        chosen = corridor_order[step]
        bus_from = corridor_buses[chosen, 0]
        bus_to = corridor_buses[chosen, 1]
        ratio = corridor_ratio[chosen]
        coefficient = ptdf_rows[:, bus_from] - ptdf_rows[:, bus_to]
        for prior in range(step):
            coefficient = coefficient - coeff_list[prior] * (
                sens_list[prior][bus_from] - sens_list[prior][bus_to]
            )
        initial = all_rows[step]
        current = initial
        line_flow = all_flows[step]
        row_coeffs = []
        for prior in range(step):
            prior_from, prior_to = ends_list[prior]
            value = initial[prior_from] - initial[prior_to]
            for earlier in range(prior):
                value = value - row_coeffs[earlier] * (
                    sens_list[earlier][prior_from] - sens_list[earlier][prior_to]
                )
            row_coeffs.append(value)
        for prior in range(step):
            current = current - row_coeffs[prior] * sens_list[prior]
            line_flow = line_flow - row_coeffs[prior] * shift_list[prior]
        weight = ratio / (1.0 + ratio * jnp.abs(current[bus_from] - current[bus_to]))
        coeff_list.append(coefficient)
        sens_list.append(weight * current)
        shift_list.append(weight * line_flow)
        ends_list.append((bus_from, bus_to))
    flows = base
    for step in range(NC):
        flows = flows - coeff_list[step][:, None] * shift_list[step][None, :]
    return (flows, jnp.stack(sens_list))


def solution(mesh):
    torus = Mesh(
        mesh.devices.reshape(mesh.shape["snap"], 8, 4, 2), ("snap", "line_0", "line_1", "line_2")
    )
    in_specs = (
        P(LINE, None),
        P(SNAP_LINE, None),
        P(),
        P(SNAP_LINE),
        P(SNAP_LINE),
        P(),
        P("snap"),
        P(),
        P(),
        P(),
        P(),
        P(),
    )
    out_specs = (P(LINE, "snap"), P())
    return jax.shard_map(body, mesh=torus, in_specs=in_specs, out_specs=out_specs, check_vma=False)
```

profile of v0, /device:TPU:2, one launch (start us, length us, event | category | flops | bytes accessed | tf_op | source)
XLA Modules:
  0.0 216.5 jit_solution(7106054973172409046)
XLA Ops:
  7.2 0.7 compare_select_fusion.25
  9.3 6.7 %multiply_add_fusion = f32[20,2048]{1,0:T(8,128)S(1)} fusion(f32[20,2048]{1,0:T(8,128)} %param.13, f32[20]{0:T(128)S(1)} %get-tuple-element.133, f32[20]{0:T(128)S(1)} %get-tuple-element.134, f32[20]{0:T(128)S(1)} %get-tuple-element.112, f32[20]{0:T(128)S(1)} %get-tuple-element.113, f32[20]{0:T(128)S(1)} %get-tuple-element.114, ...), kind=kLoop, calls=%fused_computation.11 | loop fusion | flops 3973120 | bytes 331520 | tf_op jit(solution)/shard_map/add | solution.py:97
  16.2 9.5 %all_to_all.44 = f32[20,4,512]{2,0,1:T(8,128)S(1)} all-to-all(f32[20,4,512]{2,0,1:T(8,128)S(1)} %copy.27), channel_id=1, replica_groups=mesh['snap'=4,'line_0'=8,'line_1'=4,'line_2'=2] {'snap'}, dimensions={1} | all-to-all | bytes 327680 | tf_op jit(solution)/shard_map/all_to_all | solution.py:98
  25.7 0.7 all_to_all.33
  26.4 0.9 reshape.185
  27.7 1.4 fusion.31
  36.5 1.5 fusion.29
  43.1 11.8 %copy.26 = f32[128,20480]{0,1:T(8,128)} copy(f32[128,20480]{1,0:T(8,128)} %param.12) | data formatting | bytes 20971520 | tf_op args[0]
  59.9 2.0 broadcast_select_fusion.3
  62.3 17.4 %gather_fusion = f32[5120,128]{1,0:T(8,128)S(1)} fusion(f32[128,20480]{0,1:T(8,128)} %copy.26, s32[5120]{0:T(1024)S(1)} %broadcast_clamp_fusion), kind=kCustom, calls=%fused_computation | custom fusion | bytes 5263360 | tf_op jit(solution)/shard_map/jit(_take)/gather | solution.py:100
  79.8 10.9 %convolution_bitcast_fusion = f32[128]{0:T(128)S(1)} fusion(f32[128,20480]{1,0:T(8,128)} %param.12, f32[20480,1]{0,1:T(1,128)S(1)} %bitcast.64), kind=kOutput, calls=%fused_computation.6 | convolution fusion | flops 31457280 | bytes 10568192 | tf_op jit(solution)/shard_map/dot_general | solution.py:107
  90.7 23.9 %all-gather.2.cloned.1.call-done = f32[5120,512]{1,0:T(8,128)} async-done(((f32[80,512]{1,0:T(8,128)}), f32[5120,512]{1,0:T(8,128)}) %all-gather.2.cloned.1.call-update) | async-done | bytes 10485776 | tf_op jit(solution)/shard_map/all_gather | solution.py:103
  114.6 10.9 %fusion.4 = f32[128,512]{1,0:T(8,128)S(1)} fusion(f32[5120,512]{1,0:T(8,128)} %all-gather.2.cloned.1.call-done, f32[5120,128]{1,0:T(8,128)S(1)} %gather_fusion, pred[5120]{0:T(1024)(128)(4,1)S(1)} %compare_and_fusion, f32[512]{0:T(512)S(1)} %copy-done.3, f32[128]{0:T(128)S(1)} %convolution_bitcast_fusion), kind=kOutput, calls=%fused_computation.5 | convolution fusion | flops 4027318272 | bytes 13377024 | tf_op jit(solution)/shard_map/dot_general | solution.py:101
  126.0 4.0 %all_to_all.45 = f32[2,32,1312]{2,1,0:T(8,128)S(1)} all-to-all(f32[2,32,1312]{2,1,0:T(8,128)S(1)} %copy.28), channel_id=1, replica_groups=mesh['snap'=4,'line_0'=8,'line_1'=4,'line_2'=2] {'line_2'}, dimensions={0} | all-to-all | bytes 671744 | tf_op jit(solution)/shard_map/all_to_all | solution.py:23
  130.2 17.1 %all_to_all.46 = f32[32,1,1312]{2,1,0:T(1,128)S(1)} all-to-all(f32[32,1,1312]{2,1,0:T(1,128)S(1)} %all_to_all.35), channel_id=1, replica_groups=mesh['snap'=4,'line_0'=8,'line_1'=4,'line_2'=2] {'line_0','line_1'}, dimensions={0} | all-to-all | bytes 335872 | tf_op jit(solution)/shard_map/all_to_all | solution.py:31
  147.4 0.8 broadcast_in_dim.62
  148.1 3.9 %all-to-all-start.3 = ((f32[32,1,1312]{2,1,0:T(1,128)}), f32[32,1,1312]{2,1,0:T(1,128)S(1)}, u32[]{:S(2)}, u32[]{:S(2)}) async-start(f32[32,1,1312]{2,1,0:T(1,128)} %broadcast_in_dim.62), calls=%async_computation.3 | async-start | bytes 360448 | tf_op jit(solution)/shard_map/all_to_all | solution.py:42
  152.0 0.7 constant_dynamic-slice_fusion.8
  168.4 4.0 %all_to_all.47 = f32[2,32,1312]{2,1,0:T(8,128)S(1)} all-to-all(f32[2,32,1312]{2,1,0:T(8,128)S(1)} %broadcast_in_dim.64), channel_id=1, replica_groups=mesh['snap'=4,'line_0'=8,'line_1'=4,'line_2'=2] {'line_2'}, dimensions={0} | all-to-all | bytes 671744 | tf_op jit(solution)/shard_map/all_to_all | solution.py:42
  184.4 1.1 multiply_subtract_fusion.5
  191.2 0.7 fusion.19
  206.6 1.0 pad_maximum_fusion.1
  207.6 1.2 fusion.7
  208.8 0.9 multiply_subtract_fusion
  (52 shorter events, 10.4 us)
Async XLA Ops:
  7.2 72.6 %copy-start = (f32[20480]{0:T(1024)S(1)}, f32[20480]{0:T(1024)}, u32[]{:S(2)}) copy-start(f32[20480]{0:T(1024)} %param.17) | copy-start | bytes 245764
  7.2 107.4 %all-gather.2.cloned.1.call-start = ((), (), s32[]{:S(2)}) async-start(), calls=%async_computation.5 | async-start | bytes 10649600 | tf_op jit(solution)/shard_map/all_gather | solution.py:103
  79.7 34.9 %copy-start.3 = (f32[512]{0:T(512)S(1)}, f32[512]{0:T(512)}, u32[]{:S(2)}) copy-start(f32[512]{0:T(512)} %param.18) | copy-start | bytes 6148
  90.7 61.3 %copy-start.1 = (s32[4,2]{0,1:T(2,128)S(1)}, s32[4,2]{0,1:T(2,128)}, u32[]{:S(2)}) copy-start(s32[4,2]{0,1:T(2,128)} %param.20) | copy-start | bytes 100
  90.7 77.0 %copy-start.2 = (f32[4]{0:T(128)S(1)}, f32[4]{0:T(128)}, u32[]{:S(2)}) copy-start(f32[4]{0:T(128)} %param.23) | copy-start | bytes 52
  148.1 20.3 %all-to-all-start.3 = ((f32[32,1,1312]{2,1,0:T(1,128)}), f32[32,1,1312]{2,1,0:T(1,128)S(1)}, u32[]{:S(2)}, u32[]{:S(2)}) async-start(f32[32,1,1312]{2,1,0:T(1,128)} %broadcast_in_dim.62), calls=%async_computation.3 | async-start | bytes 360448 | tf_op jit(solution)/shard_map/all_to_all | solution.py:42
Sparse Core Ops, SparseCore 0:
  26.5 88.0 all-gather.1
where the time goes:
time: 219 us; the launch traced here: 216 us
  between operations  72.5 us (33%)
  local copies, waits for them, and re-layouts  44.2 us (20%)
  blocking collectives  34.6 us (16%)
  waiting for transfers between devices  23.9 us (11%)
  matrix products  21.8 us (10%)
  other arithmetic  15.6 us (7%)
  starting transfers between devices  3.9 us (2%)
    all_gather x1, waiting for transfers between devices, body(): lax.all_gather(unit_blocks, LINE, axis=0, tiled=True)  23.9 us
    gather x1, local copies, waits for them, and re-layouts, body(): columns = jnp.take(ptdf_rows, order_ids, axis=1)  17.4 us
    all_to_all x1, blocking collectives, summed_rows(): lax.all_to_all(nearer, far, split_axis=0, concat_axis=0, tiled=True)  17.1 us
    unnamed x12, local copies, waits for them, and re-layouts  11.9 us
    dot_general x1, matrix products, body(): jnp.dot(columns, lax.all_gather(unit_blocks, LINE, axis=0, tiled=True), p...  10.9 us
    dot_general x1, matrix products, body(): jnp.dot(ptdf_rows, load_share, preferred_element_type=jnp.float32, precis...  10.9 us
    all_to_all x1, blocking collectives, body(): lax.all_to_all(dispatch, 'snap', split_axis=1, concat_axis=0, tiled=True)  9.5 us
    add x1, other arithmetic, body(): dispatch = held_mean + ramp_gain * (plan - lagged)  6.69 us
  transfers between devices with their start and end apart: 2, of which 1 were waited for; matrix products, arithmetic and copies ran while one was open for 22% of the time, Pallas kernels for 0%

commit v1 on v0

v1 whole, which is shorter than its diff:
```python
import jax
import jax.numpy as jnp
from jax import lax
from jax.sharding import Mesh
from jax.sharding import PartitionSpec as P

WMAX = 24
NC = 4
LINE = ("line_0", "line_1", "line_2")
SNAP_LINE = ("snap", "line_0", "line_1", "line_2")


ramp_gain = 0.5


def body(
    ptdf_rows,
    plan,
    unit_bus,
    min_up,
    ramp_lag,
    load_share,
    system_load,
    corridor_order,
    corridor_buses,
    corridor_owner,
    corridor_row,
    corridor_ratio,
):
    unit_count, horizon = plan.shape
    snap_count = lax.axis_size("snap")
    line_count = lax.axis_size(LINE)
    here = lax.axis_index(LINE)

    picked_rows = []
    for step in range(NC):
        chosen = corridor_order[step]
        row = lax.dynamic_index_in_dim(ptdf_rows, corridor_row[chosen], 0, keepdims=False)
        picked_rows.append(jnp.where(corridor_owner[chosen] == here, row, 0.0))
    all_rows = lax.psum(jnp.stack(picked_rows), LINE)

    padded = jnp.pad(plan, ((0, 0), (WMAX, 0)))
    inverse = 1.0 / min_up.astype(jnp.float32)
    held_mean = jnp.zeros(plan.shape, jnp.float32)
    lagged = jnp.zeros(plan.shape, jnp.float32)
    for offset in range(WMAX):
        shifted = padded[:, WMAX - offset : WMAX - offset + horizon]
        held_mean = held_mean + shifted * jnp.where(offset < min_up, inverse, 0.0)[:, None]
        lagged = lagged + shifted * (ramp_lag == offset).astype(jnp.float32)[:, None]
    dispatch = held_mean + ramp_gain * (plan - lagged)
    unit_blocks = lax.all_to_all(dispatch, "snap", split_axis=1, concat_axis=0, tiled=True)
    everyone = lax.all_gather(unit_blocks, LINE, axis=0, tiled=True)

    order_ids = unit_bus.reshape(snap_count, line_count, unit_count).transpose(1, 0, 2).reshape(-1)
    columns = jnp.concatenate(
        [jnp.take(ptdf_rows, order_ids, axis=1), jnp.take(all_rows, order_ids, axis=1)], axis=0
    )
    load_flows = jnp.dot(
        ptdf_rows, load_share, preferred_element_type=jnp.float32, precision=lax.Precision.HIGHEST
    )
    row_load_flows = jnp.dot(
        all_rows, load_share, preferred_element_type=jnp.float32, precision=lax.Precision.HIGHEST
    )

    sens_list = []
    weights = []
    row_coeff_list = []
    ends_list = []
    for step in range(NC):
        chosen = corridor_order[step]
        bus_from = corridor_buses[chosen, 0]
        bus_to = corridor_buses[chosen, 1]
        ratio = corridor_ratio[chosen]
        initial = all_rows[step]
        row_coeffs = []
        for prior in range(step):
            prior_from, prior_to = ends_list[prior]
            value = initial[prior_from] - initial[prior_to]
            for earlier in range(prior):
                value = value - row_coeffs[earlier] * (
                    sens_list[earlier][prior_from] - sens_list[earlier][prior_to]
                )
            row_coeffs.append(value)
        current = initial
        for prior in range(step):
            current = current - row_coeffs[prior] * sens_list[prior]
        weight = ratio / (1.0 + ratio * jnp.abs(current[bus_from] - current[bus_to]))
        sens_list.append(weight * current)
        weights.append(weight)
        row_coeff_list.append(row_coeffs)
        ends_list.append((bus_from, bus_to))

    coeff_list = []
    for step in range(NC):
        bus_from, bus_to = ends_list[step]
        coefficient = ptdf_rows[:, bus_from] - ptdf_rows[:, bus_to]
        for prior in range(step):
            coefficient = coefficient - coeff_list[prior] * (
                sens_list[prior][bus_from] - sens_list[prior][bus_to]
            )
        coeff_list.append(coefficient)

    flows_all = jnp.dot(
        columns,
        everyone,
        preferred_element_type=jnp.float32,
        precision=lax.Precision.HIGHEST,
    )
    lines_here = ptdf_rows.shape[0]
    base = flows_all[:lines_here] - load_flows[:, None] * system_load[None, :]
    row_base = flows_all[lines_here:] - row_load_flows[:, None] * system_load[None, :]

    shift_list = []
    for step in range(NC):
        line_flow = row_base[step]
        for prior in range(step):
            line_flow = line_flow - row_coeff_list[step][prior] * shift_list[prior]
        shift_list.append(weights[step] * line_flow)
    flows = base
    for step in range(NC):
        flows = flows - coeff_list[step][:, None] * shift_list[step][None, :]
    return (flows, jnp.stack(sens_list))


def solution(mesh):
    torus = Mesh(
        mesh.devices.reshape(mesh.shape["snap"], 8, 4, 2), ("snap", "line_0", "line_1", "line_2")
    )
    in_specs = (
        P(LINE, None),
        P(SNAP_LINE, None),
        P(),
        P(SNAP_LINE),
        P(SNAP_LINE),
        P(),
        P("snap"),
        P(),
        P(),
        P(),
        P(),
        P(),
    )
    out_specs = (P(LINE, "snap"), P())
    return jax.shard_map(body, mesh=torus, in_specs=in_specs, out_specs=out_specs, check_vma=False)
```

time: 219 us -> 348 us (1.59)
  waiting for transfers between devices: 23.9 us -> 132 us
  blocking collectives: 34.6 us -> 0 us
  local copies, waits for them, and re-layouts: 44.2 us -> 75.6 us
  matrix products: 21.8 us -> 32.7 us
  other arithmetic: 15.6 us -> 26.4 us
    psum x0 -> x1, waiting for transfers between devices: none -> 115 us  [body(): all_rows = lax.psum(jnp.stack(picked_rows), LINE)]
    all_to_all x4 -> x0, blocking collectives: 34.6 us -> none  [the longest x1 17.1 us: summed_rows(): lax.all_to_all(nearer, far, split_axis=0, concat_axis=0, tiled=True)]
    gather x1 -> x2, local copies, waits for them, and re-layouts: 17.4 us -> 43.2 us  [the longest x1 21.6 us: body(): jnp.take(ptdf_rows, order_ids, axis=1)]
    dot_general x1 -> x2, matrix products: 10.9 us -> 21.9 us  [the longest x1 20.4 us: body(): jnp.dot(columns, everyone, preferred_element_type=jnp.float32, precision=...]
    select_n x3 -> x4, other arithmetic: 2.03 us -> 11.5 us  [the longest x1 5.29 us: body(): jnp.take(all_rows, order_ids, axis=1)]
    all_gather x1, waiting for transfers between devices: 23.9 us -> 16.4 us  [body(): everyone = lax.all_gather(unit_blocks, LINE, axis=0, tiled=True)]
    psum x0 -> x1, local copies, waits for them, and re-layouts: none -> 6.55 us  [body(): all_rows = lax.psum(jnp.stack(picked_rows), LINE)]
    unnamed x12 -> x11, local copies, waits for them, and re-layouts: 11.9 us -> 11.8 us
  transfers between devices with their start and end apart: 2 -> 3, of which waited for: 1 -> 2; matrix products, arithmetic and copies ran while one was open for 22% -> 30% of each run, Pallas kernels for 0% -> 0%
where the time goes in v1:
time: 348 us; the launch traced here: 345 us
  waiting for transfers between devices  132 us (38%)
  local copies, waits for them, and re-layouts  75.6 us (22%)
  between operations  72.9 us (21%)
  matrix products  32.7 us (9%)
  other arithmetic  26.4 us (8%)
  starting transfers between devices  5.8 us (2%)
    psum x1, waiting for transfers between devices, body(): all_rows = lax.psum(jnp.stack(picked_rows), LINE)  115 us
    gather x1, local copies, waits for them, and re-layouts, body(): jnp.take(ptdf_rows, order_ids, axis=1)  21.6 us
    gather x1, local copies, waits for them, and re-layouts, body(): jnp.take(all_rows, order_ids, axis=1)  21.6 us
    dot_general x1, matrix products, body(): jnp.dot(columns, everyone, preferred_element_type=jnp.float32, precision=...  20.4 us
    all_gather x1, waiting for transfers between devices, body(): everyone = lax.all_gather(unit_blocks, LINE, axis=0, tiled=True)  16.4 us
    unnamed x11, local copies, waits for them, and re-layouts  11.8 us
    dot_general x1, matrix products, body(): jnp.dot(ptdf_rows, load_share, preferred_element_type=jnp.float32, precis...  10.8 us
  transfers between devices with their start and end apart: 3, of which 2 were waited for; matrix products, arithmetic and copies ran while one was open for 30% of the time, Pallas kernels for 0%

profile of v1, /device:TPU:2, one launch (start us, length us, event | category | flops | bytes accessed | tf_op | source)
XLA Modules:
  0.0 344.9 jit_solution(17711845217591911878)
XLA Ops:
  7.9 0.7 compare_select_fusion.25
  9.3 6.7 %multiply_add_fusion = f32[20,2048]{1,0:T(8,128)S(1)} fusion(f32[20,2048]{1,0:T(8,128)} %param.13, f32[20]{0:T(128)S(1)} %get-tuple-element.133, f32[20]{0:T(128)S(1)} %get-tuple-element.134, f32[20]{0:T(128)S(1)} %get-tuple-element.112, f32[20]{0:T(128)S(1)} %get-tuple-element.113, f32[20]{0:T(128)S(1)} %get-tuple-element.114, ...), kind=kLoop, calls=%fused_computation.17 | loop fusion | flops 3973120 | bytes 331520 | tf_op jit(solution)/shard_map/add | solution.py:50
  16.1 0.7 copy.43
  16.8 5.6 %all-to-all-start = ((f32[20,4,512]{2,0,1:T(8,128)}), f32[20,4,512]{2,0,1:T(8,128)S(1)}, u32[]{:S(2)}, u32[]{:S(2)}) async-start(f32[20,4,512]{2,0,1:T(8,128)} %copy.43), calls=%async_computation | async-start | bytes 393216 | tf_op jit(solution)/shard_map/all_to_all | solution.py:51
  22.4 1.5 fusion.22
  31.6 1.5 fusion.20
  43.5 2.0 broadcast_select_fusion.3
  45.4 1.0 pad_maximum_fusion
  46.7 0.9 reshape.180
  48.1 11.8 %copy.41 = f32[128,20480]{0,1:T(8,128)} copy(f32[128,20480]{1,0:T(8,128)} %param.12) | data formatting | bytes 20971520 | tf_op args[0]
  59.9 21.6 %gather_fusion = f32[5120,128]{1,0:T(8,128)} fusion(f32[128,20480]{0,1:T(8,128)} %copy.41, s32[5120]{0:T(1024)S(1)} %broadcast_clamp_fusion), kind=kCustom, calls=%fused_computation | custom fusion | bytes 5263360 | tf_op jit(solution)/shard_map/jit(_take)/gather | solution.py:56
  81.5 4.2 %select_bitcast_fusion.1 = f32[128,5120]{0,1:T(8,128)S(1)} fusion(f32[5120,128]{1,0:T(8,128)} %gather_fusion, pred[5120]{0:T(1024)(128)(4,1)S(1)} %compare_and_fusion), kind=kLoop, calls=%fused_computation.7 | loop fusion | flops 655360 | bytes 5248000 | tf_op jit(solution)/shard_map/jit(_take)/select_n | solution.py:56
  85.8 10.8 %convolution_bitcast_fusion.1 = f32[128]{0:T(128)S(1)} fusion(f32[128,20480]{1,0:T(8,128)} %param.12, f32[20480,1]{0,1:T(1,128)S(1)} %bitcast.62), kind=kOutput, calls=%fused_computation.9 | convolution fusion | flops 31457280 | bytes 10568192 | tf_op jit(solution)/shard_map/dot_general | solution.py:58
  114.0 115.1 %all-reduce.3.cloned.1.call-done = f32[4,20480]{1,0:T(4,128)} async-done(((f32[4,20480]{1,0:T(4,128)}), f32[4,20480]{1,0:T(4,128)}) %all-reduce.3.cloned.1.call-update) | async-done | bytes 327696 | tf_op jit(solution)/shard_map/psum | solution.py:40
  229.1 6.5 %copy.42 = f32[4,20480]{0,1:T(8,128)} copy(f32[4,20480]{1,0:T(4,128)} %all-reduce.3.cloned.1.call-done) | data formatting | bytes 655360 | tf_op jit(solution)/shard_map/psum | solution.py:40
  235.7 21.6 %gather_fusion.1 = f32[5120,4]{1,0:T(8,128)} fusion(f32[4,20480]{0,1:T(8,128)} %copy.42, s32[5120]{0:T(1024)S(1)} %broadcast_clamp_fusion), kind=kCustom, calls=%fused_computation.1 | custom fusion | bytes 184320 | tf_op jit(solution)/shard_map/jit(_take)/gather | solution.py:56
  290.0 1.1 multiply_subtract_fusion.4
  291.1 1.3 fusion.8
  292.4 1.5 convolution_bitcast_fusion
  293.9 5.3 %select_bitcast_fusion = f32[4,5120]{0,1:T(8,128)} fusion(f32[5120,4]{1,0:T(8,128)} %gather_fusion.1, pred[5120]{0:T(1024)(128)(4,1)S(1)} %compare_and_fusion), kind=kLoop, calls=%fused_computation.6 | loop fusion | flops 20480 | bytes 168960 | tf_op jit(solution)/shard_map/jit(_take)/select_n | solution.py:56
  299.2 1.0 pad_maximum_fusion.1
  300.3 16.4 %all-gather.2.cloned.1.call-done = f32[5120,512]{1,0:T(8,128)} async-done(((f32[80,512]{1,0:T(8,128)}), f32[5120,512]{1,0:T(8,128)}) %all-gather.2.cloned.1.call-update) | async-done | bytes 10485776 | tf_op jit(solution)/shard_map/all_gather | solution.py:52
  316.7 20.4 %fusion = f32[132,512]{1,0:T(8,128)S(1)} fusion(f32[5120,512]{1,0:T(8,128)} %all-gather.2.cloned.1.call-done, f32[4,5120]{0,1:T(8,128)} %select_bitcast_fusion, f32[128,5120]{0,1:T(8,128)S(1)} %select_bitcast_fusion.1), kind=kOutput, calls=%fused_computation.2 | convolution fusion | flops 4153036800 | bytes 13459456 | tf_op jit(solution)/shard_map/dot_general | solution.py:103
  337.1 0.9 fusion.7
  (44 shorter events, 11.9 us)
Async XLA Ops:
  7.2 78.6 %copy-start = (f32[20480]{0:T(1024)S(1)}, f32[20480]{0:T(1024)}, u32[]{:S(2)}) copy-start(f32[20480]{0:T(1024)} %param.17) | copy-start | bytes 245764
  16.8 96.5 %all-to-all-start = ((f32[20,4,512]{2,0,1:T(8,128)}), f32[20,4,512]{2,0,1:T(8,128)S(1)}, u32[]{:S(2)}, u32[]{:S(2)}) async-start(f32[20,4,512]{2,0,1:T(8,128)} %copy.43), calls=%async_computation | async-start | bytes 393216 | tf_op jit(solution)/shard_map/all_to_all | solution.py:51
  22.4 206.7 %all-reduce.3.cloned.1.call-start = ((), (), s32[]{:S(2)}) async-start(), calls=%async_computation.1 | async-start | bytes 655360 | tf_op jit(solution)/shard_map/psum | solution.py:40
  46.5 270.2 %all-gather.2.cloned.1.call-start = ((), (), s32[]{:S(2)}) async-start(), calls=%async_computation.2 | async-start | bytes 10649600 | tf_op jit(solution)/shard_map/all_gather | solution.py:52
  85.7 10.9 %copy-start.2 = (s32[4,2]{0,1:T(2,128)S(1)}, s32[4,2]{0,1:T(2,128)}, u32[]{:S(2)}) copy-start(s32[4,2]{0,1:T(2,128)} %param.20) | copy-start | bytes 100
  85.7 26.9 %copy-start.4 = (f32[4]{0:T(128)S(1)}, f32[4]{0:T(128)}, u32[]{:S(2)}) copy-start(f32[4]{0:T(128)} %param.23) | copy-start | bytes 52
  229.1 28.2 %copy-start.1 = (f32[4,20480]{1,0:T(4,128)S(1)}, f32[4,20480]{1,0:T(4,128)}, u32[]{:S(2)}) copy-start(f32[4,20480]{1,0:T(4,128)} %all-reduce.3.cloned.1.call-done) | copy-start | bytes 983044
  300.3 36.8 %copy-start.3 = (f32[512]{0:T(512)S(1)}, f32[512]{0:T(512)}, u32[]{:S(2)}) copy-start(f32[512]{0:T(512)} %param.18) | copy-start | bytes 6148
Sparse Core Ops, SparseCore 0:
  46.6 182.4 all-reduce.2
  232.5 84.1 all-gather.1

commit v2 on v1

v2 whole, which is shorter than its diff:
```python
import jax
import jax.numpy as jnp
from jax import lax
from jax.sharding import Mesh
from jax.sharding import PartitionSpec as P

WMAX = 24
NC = 4
LINE = ("line_0", "line_1", "line_2")
SNAP_LINE = ("snap", "line_0", "line_1", "line_2")
HI = lax.Precision.HIGHEST


ramp_gain = 0.5


def line_total(x):
    for axis in ("line_2", "line_1", "line_0"):
        size = lax.axis_size(axis)
        step = 1
        while step < size:
            x = x + lax.ppermute(x, axis, [(i, i ^ step) for i in range(size)])
            step *= 2
    return x


def body(
    ptdf_rows,
    plan,
    unit_bus,
    min_up,
    ramp_lag,
    load_share,
    system_load,
    corridor_order,
    corridor_buses,
    corridor_owner,
    corridor_row,
    corridor_ratio,
):
    unit_count, horizon = plan.shape
    lines_here, buses = ptdf_rows.shape
    snap_count = lax.axis_size("snap")
    line_count = lax.axis_size(LINE)
    here = lax.axis_index(LINE)

    rows_of = corridor_row[corridor_order]
    mine = corridor_owner[corridor_order] == here
    ends = corridor_buses[corridor_order].reshape(-1)
    ratios = corridor_ratio[corridor_order]
    pick = jnp.where(
        mine[:, None] & (rows_of[:, None] == jnp.arange(lines_here)[None, :]), 1.0, 0.0
    )

    all_rows = line_total(jnp.dot(pick, ptdf_rows, precision=HI))

    padded = jnp.pad(plan, ((0, 0), (WMAX, 0)))
    inverse = 1.0 / min_up.astype(jnp.float32)
    held_mean = jnp.zeros(plan.shape, jnp.float32)
    lagged = jnp.zeros(plan.shape, jnp.float32)
    for offset in range(WMAX):
        shifted = padded[:, WMAX - offset : WMAX - offset + horizon]
        held_mean = held_mean + shifted * jnp.where(offset < min_up, inverse, 0.0)[:, None]
        lagged = lagged + shifted * (ramp_lag == offset).astype(jnp.float32)[:, None]
    dispatch = held_mean + ramp_gain * (plan - lagged)
    unit_blocks = lax.all_to_all(dispatch, "snap", split_axis=1, concat_axis=0, tiled=True)
    everyone = lax.all_gather(unit_blocks, LINE, axis=0, tiled=True)

    order_ids = unit_bus.reshape(snap_count, line_count, unit_count).transpose(1, 0, 2).reshape(-1)
    columns = jnp.take(ptdf_rows, order_ids, axis=1)
    row_columns = line_total(jnp.dot(pick, columns, precision=HI))

    probes = jnp.concatenate(
        [
            load_share[:, None],
            jnp.where(jnp.arange(buses)[:, None] == ends[None, :], 1.0, 0.0),
        ],
        axis=1,
    )
    local_probe = jnp.dot(ptdf_rows, probes, preferred_element_type=jnp.float32, precision=HI)
    row_probe = jnp.dot(all_rows, probes, preferred_element_type=jnp.float32, precision=HI)
    load_flows = local_probe[:, 0]
    at_ends = local_probe[:, 1:]
    row_load_flows = row_probe[:, 0]
    row_at_ends = row_probe[:, 1:]

    sens_ends = []
    weights = []
    row_coeff_list = []
    for step in range(NC):
        initial = row_at_ends[step]
        row_coeffs = []
        for prior in range(step):
            value = initial[2 * prior] - initial[2 * prior + 1]
            for earlier in range(prior):
                value = value - row_coeffs[earlier] * (
                    sens_ends[earlier][2 * prior] - sens_ends[earlier][2 * prior + 1]
                )
            row_coeffs.append(value)
        current = initial
        for prior in range(step):
            current = current - row_coeffs[prior] * sens_ends[prior]
        ratio = ratios[step]
        weight = ratio / (1.0 + ratio * jnp.abs(current[2 * step] - current[2 * step + 1]))
        sens_ends.append(weight * current)
        weights.append(weight)
        row_coeff_list.append(row_coeffs)

    sens_list = []
    for step in range(NC):
        current = all_rows[step]
        for prior in range(step):
            current = current - row_coeff_list[step][prior] * sens_list[prior]
        sens_list.append(weights[step] * current)

    coeff_list = []
    for step in range(NC):
        coefficient = at_ends[:, 2 * step] - at_ends[:, 2 * step + 1]
        for prior in range(step):
            coefficient = coefficient - coeff_list[prior] * (
                sens_ends[prior][2 * step] - sens_ends[prior][2 * step + 1]
            )
        coeff_list.append(coefficient)

    flows_all = jnp.dot(
        jnp.concatenate([columns, row_columns], axis=0),
        everyone,
        preferred_element_type=jnp.float32,
        precision=HI,
    )
    base = flows_all[:lines_here] - load_flows[:, None] * system_load[None, :]
    row_base = flows_all[lines_here:] - row_load_flows[:, None] * system_load[None, :]

    shift_list = []
    for step in range(NC):
        line_flow = row_base[step]
        for prior in range(step):
            line_flow = line_flow - row_coeff_list[step][prior] * shift_list[prior]
        shift_list.append(weights[step] * line_flow)
    flows = base
    for step in range(NC):
        flows = flows - coeff_list[step][:, None] * shift_list[step][None, :]
    return (flows, jnp.stack(sens_list))


def solution(mesh):
    torus = Mesh(
        mesh.devices.reshape(mesh.shape["snap"], 8, 4, 2), ("snap", "line_0", "line_1", "line_2")
    )
    in_specs = (
        P(LINE, None),
        P(SNAP_LINE, None),
        P(),
        P(SNAP_LINE),
        P(SNAP_LINE),
        P(),
        P("snap"),
        P(),
        P(),
        P(),
        P(),
        P(),
    )
    out_specs = (P(LINE, "snap"), P())
    return jax.shard_map(body, mesh=torus, in_specs=in_specs, out_specs=out_specs, check_vma=False)
```

time: 348 us -> 240 us (0.69)
  the two profiles are of different devices: /device:TPU:2 before, /device:TPU:120 now
where the time goes in v2:
time: 240 us; the launch traced here: 239 us
  waiting for transfers between devices  53.8 us (22%)
  matrix products  45.2 us (19%)
  local copies, waits for them, and re-layouts  40.5 us (17%)
  between operations  39.7 us (17%)
  starting transfers between devices  28.3 us (12%)
  other arithmetic  21.2 us (9%)
  blocking collectives  10.4 us (4%)
    ppermute x12, waiting for transfers between devices, line_total(): x = x + lax.ppermute(x, axis, [(i, i ^ step) for i in range(size)])  53.8 us
    ppermute x12, starting transfers between devices, line_total(): x = x + lax.ppermute(x, axis, [(i, i ^ step) for i in range(size)])  28.3 us
    dot_general x1, matrix products, body(): jnp.dot(jnp.concatenate([columns, row_columns], axis=0), everyone, prefer...  20.8 us
    gather x1, local copies, waits for them, and re-layouts, body(): columns = jnp.take(ptdf_rows, order_ids, axis=1)  17.4 us
    unnamed x20, local copies, waits for them, and re-layouts  12 us
    dot_general x1, matrix products, body(): jnp.dot(ptdf_rows, probes, preferred_element_type=jnp.float32, precision=HI)  10.8 us
    all_to_all x1, blocking collectives, body(): lax.all_to_all(dispatch, 'snap', split_axis=1, concat_axis=0, tiled=True)  10.4 us
    dot_general x1, matrix products, body(): all_rows = line_total(jnp.dot(pick, ptdf_rows, precision=HI))  7.63 us
  transfers between devices with their start and end apart: 13, of which 7 were waited for; matrix products, arithmetic and copies ran while one was open for 32% of the time, Pallas kernels for 0%

profile of v2, /device:TPU:120, one launch (start us, length us, event | category | flops | bytes accessed | tf_op | source)
XLA Modules:
  0.0 239.2 jit_solution(9855642005362963659)
XLA Ops:
  9.3 6.7 %multiply_add_fusion = f32[20,2048]{1,0:T(8,128)S(1)} fusion(f32[20,2048]{1,0:T(8,128)} %param.13, f32[20]{0:T(128)S(1)} %get-tuple-element.104, f32[20]{0:T(128)S(1)} %get-tuple-element.105, f32[20]{0:T(128)S(1)} %get-tuple-element.83, f32[20]{0:T(128)S(1)} %get-tuple-element.84, f32[20]{0:T(128)S(1)} %get-tuple-element.85, f32[20]{0:T(128)S(1)} %get-tuple-element.86, ...), kind=kLoop, calls=%fused_computation.26 | loop fusion | flops 3973120 | bytes 331520 | tf_op jit(solution)/shard_map/add | solution.py:65
  16.2 10.4 %all_to_all.19 = f32[20,4,512]{2,0,1:T(8,128)S(1)} all-to-all(f32[20,4,512]{2,0,1:T(8,128)S(1)} %copy.28), channel_id=1, replica_groups=mesh['snap'=4,'line_0'=8,'line_1'=4,'line_2'=2] {'snap'}, dimensions={1} | all-to-all | bytes 327680 | tf_op jit(solution)/shard_map/all_to_all | solution.py:66
  29.3 7.6 %fusion.22 = f32[4,20480]{1,0:T(4,128)S(1)} fusion(f32[128,20480]{1,0:T(8,128)} %param.12, s32[4]{0:T(128)S(1)} %gather_fusion.2, pred[4]{0:T(512)(128)(4,1)S(1)} %broadcast_compare_fusion), kind=kOutput, calls=%fused_computation.61 | convolution fusion | flops 125830656 | bytes 10813460 | tf_op jit(solution)/shard_map/dot_general | solution.py:55
  37.5 1.1 collective-permute-done.6
  39.6 11.8 %copy.26 = f32[128,20480]{0,1:T(8,128)} copy(f32[128,20480]{1,0:T(8,128)} %param.12) | data formatting | bytes 20971520 | tf_op args[0]
  51.6 17.4 %gather_fusion = f32[5120,128]{1,0:T(8,128)S(1)} fusion(f32[128,20480]{0,1:T(8,128)} %copy.26, s32[5120]{0:T(1024)S(1)} %broadcast_clamp_fusion), kind=kCustom, calls=%fused_computation | custom fusion | bytes 5263360 | tf_op jit(solution)/shard_map/jit(_take)/gather | solution.py:70
  69.0 1.1 add.285
  71.2 4.4 %fusion.4 = f32[4,5120]{1,0:T(4,128)S(1)} fusion(f32[5120,128]{1,0:T(8,128)S(1)} %gather_fusion, pred[5120]{0:T(1024)(128)(4,1)S(1)} %compare_and_fusion, s32[4]{0:T(128)S(1)} %gather_fusion.2, pred[4]{0:T(512)(128)(4,1)S(1)} %broadcast_compare_fusion), kind=kOutput, calls=%fused_computation.9 | convolution fusion | flops 32114176 | bytes 2708500 | tf_op jit(solution)/shard_map/dot_general | solution.py:71
  75.7 1.3 collective-permute-done
  78.8 6.7 %collective-permute-done.1 = f32[4,5120]{1,0:T(4,128)S(1)} collective-permute-done((f32[4,5120]{1,0:T(4,128)S(1)}, f32[4,5120]{1,0:T(4,128)S(1)}, u32[]{:S(2)}, u32[]{:S(2)}) %collective-permute-start.1) | collective-permute-done | bytes 81952 | tf_op jit(solution)/shard_map/ppermute | solution.py:22
  85.5 6.7 %collective-permute-start.2 = (f32[4,5120]{1,0:T(4,128)S(1)}, f32[4,5120]{1,0:T(4,128)S(1)}, u32[]{:S(2)}, u32[]{:S(2)}) collective-permute-start(f32[4,5120]{1,0:T(4,128)S(1)} %add.232), channel_id=1, source_target_pairs={{0,4},{2,6},{4,0},{6,2},{1,5},{3,7},{5,1},{7,3},{8,12},{10,14},{12... | collective-permute-start | bytes 245768 | tf_op jit(solution)/shard_map/ppermute | solution.py:22
  92.7 3.8 %collective-permute-done.2 = f32[4,5120]{1,0:T(4,128)S(1)} collective-permute-done((f32[4,5120]{1,0:T(4,128)S(1)}, f32[4,5120]{1,0:T(4,128)S(1)}, u32[]{:S(2)}, u32[]{:S(2)}) %collective-permute-start.2) | collective-permute-done | bytes 81952 | tf_op jit(solution)/shard_map/ppermute | solution.py:22
  96.7 13.5 %collective-permute-done.9 = f32[4,20480]{1,0:T(4,128)S(1)} collective-permute-done((f32[4,20480]{1,0:T(4,128)S(1)}, f32[4,20480]{1,0:T(4,128)S(1)}, u32[]{:S(2)}, u32[]{:S(2)}) %collective-permute-start.9) | collective-permute-done | bytes 327712 | tf_op jit(solution)/shard_map/ppermute | solution.py:22
  110.4 3.7 %select_bitcast_fusion = f32[128,5120]{0,1:T(8,128)} fusion(f32[5120,128]{1,0:T(8,128)S(1)} %gather_fusion, pred[5120]{0:T(1024)(128)(4,1)S(1)} %compare_and_fusion), kind=kLoop, calls=%fused_computation.11 | loop fusion | flops 655360 | bytes 5248000 | tf_op jit(solution)/shard_map/jit(_take)/select_n | solution.py:70
  114.1 3.0 %collective-permute-start.4 = (f32[4,5120]{1,0:T(4,128)S(1)}, f32[4,5120]{1,0:T(4,128)S(1)}, u32[]{:S(2)}, u32[]{:S(2)}) collective-permute-start(f32[4,5120]{1,0:T(4,128)S(1)} %add.234), channel_id=1, source_target_pairs={{0,16},{8,24},{16,0},{24,8},{32,48},{40,56},{48,32},{56,40},{1,17}... | collective-permute-start | bytes 245768 | tf_op jit(solution)/shard_map/ppermute | solution.py:22
  117.1 19.7 %collective-permute-done.10 = f32[4,20480]{1,0:T(4,128)S(1)} collective-permute-done((f32[4,20480]{1,0:T(4,128)S(1)}, f32[4,20480]{1,0:T(4,128)S(1)}, u32[]{:S(2)}, u32[]{:S(2)}) %collective-permute-start.10) | collective-permute-done | bytes 327712 | tf_op jit(solution)/shard_map/ppermute | solution.py:22
  137.6 14.8 %collective-permute-start.11 = (f32[4,20480]{1,0:T(4,128)}, f32[4,20480]{1,0:T(4,128)}, u32[]{:S(2)}, u32[]{:S(2)}) collective-permute-start(f32[4,20480]{1,0:T(4,128)} %add.288), channel_id=1, source_target_pairs={{0,32},{8,40},{16,48},{24,56},{32,0},{40,8},{48,16},{56,24},{1,33}... | collective-permute-start | bytes 983048 | tf_op jit(solution)/shard_map/ppermute | solution.py:22
  152.4 10.8 %fusion.10 = f32[128,9]{0,1:T(8,128)S(1)} fusion(f32[128,20480]{1,0:T(8,128)} %param.12, f32[20480,8]{0,1:T(8,128)S(1)} %fusion.11, f32[20480,1]{0,1:T(1,128)S(1)} %bitcast.45), kind=kOutput, calls=%fused_computation.17 | convolution fusion | flops 283299840 | bytes 11227648 | tf_op jit(solution)/shard_map/dot_general | solution.py:80
  164.9 7.7 %collective-permute-done.5 = f32[4,5120]{1,0:T(4,128)S(1)} collective-permute-done((f32[4,5120]{1,0:T(4,128)S(1)}, f32[4,5120]{1,0:T(4,128)S(1)}, u32[]{:S(2)}, u32[]{:S(2)}) %collective-permute-start.5) | collective-permute-done | bytes 81952 | tf_op jit(solution)/shard_map/ppermute | solution.py:22
  172.6 2.3 copy.27
  174.9 1.2 add.289
  176.0 1.6 fusion.6
  207.4 2.1 fusion.21
  210.6 20.8 %fusion = f32[132,512]{1,0:T(8,128)S(1)} fusion(f32[5120,512]{1,0:T(8,128)} %all-gather.2.cloned.1.call-done, f32[4,5120]{0,1:T(8,128)} %copy.27, f32[128,5120]{0,1:T(8,128)S(1)} %copy-done.3), kind=kOutput, calls=%fused_computation.5 | convolution fusion | flops 4153036800 | bytes 13459456 | tf_op jit(solution)/shard_map/dot_general | solution.py:125
  (84 shorter events, 19.2 us)
Async XLA Ops:
  7.2 20.8 %copy-start = (s32[4]{0:T(128)S(1)}, s32[4]{0:T(128)}, u32[]{:S(2)}) copy-start(s32[4]{0:T(128)} %param.21) | copy-start | bytes 52
  7.2 21.5 %copy-start.1 = (s32[4]{0:T(128)S(1)}, s32[4]{0:T(128)}, u32[]{:S(2)}) copy-start(s32[4]{0:T(128)} %param.22) | copy-start | bytes 52
  7.2 203.4 %all-gather.2.cloned.1.call-start = ((), (), s32[]{:S(2)}) async-start(), calls=%async_computation.1 | async-start | bytes 10649600 | tf_op jit(solution)/shard_map/all_gather | solution.py:67
  29.3 7.7 %copy-start.6 = (s32[5120]{0:T(1024)S(1)}, s32[5120]{0:T(1024)}, u32[]{:S(2)}) copy-start(s32[5120]{0:T(1024)} %param.14) | copy-start | bytes 61444
  36.9 1.7 collective-permute-start.6
  38.7 30.3 %collective-permute-start.7 = (f32[4,20480]{1,0:T(4,128)S(1)}, f32[4,20480]{1,0:T(4,128)}, u32[]{:S(2)}, u32[]{:S(2)}) collective-permute-start(f32[4,20480]{1,0:T(4,128)S(1)} %add.284), channel_id=1, source_target_pairs={{0,2},{2,0},{4,6},{6,4},{1,3},{3,1},{5,7},{7,5},{8,10},{10,8},{12,... | collective-permute-start | bytes 983048 | tf_op jit(solution)/shard_map/ppermute | solution.py:22
  69.0 9.0 %copy-start.8 = (s32[4,2]{0,1:T(2,128)S(1)}, s32[4,2]{0,1:T(2,128)}, u32[]{:S(2)}) copy-start(s32[4,2]{0,1:T(2,128)} %param.20) | copy-start | bytes 100
  70.2 22.1 %collective-permute-start.8 = (f32[4,20480]{1,0:T(4,128)S(1)}, f32[4,20480]{1,0:T(4,128)S(1)}, u32[]{:S(2)}, u32[]{:S(2)}) collective-permute-start(f32[4,20480]{1,0:T(4,128)S(1)} %add.285), channel_id=1, source_target_pairs={{0,4},{2,6},{4,0},{6,2},{1,5},{3,7},{5,1},{7,3},{8,12},{10,14},{12... | collective-permute-start | bytes 983048 | tf_op jit(solution)/shard_map/ppermute | solution.py:22
  75.6 1.4 collective-permute-start
  77.0 8.5 %collective-permute-start.1 = (f32[4,5120]{1,0:T(4,128)S(1)}, f32[4,5120]{1,0:T(4,128)S(1)}, u32[]{:S(2)}, u32[]{:S(2)}) collective-permute-start(f32[4,5120]{1,0:T(4,128)S(1)} %add.231), channel_id=1, source_target_pairs={{0,2},{2,0},{4,6},{6,4},{1,3},{3,1},{5,7},{7,5},{8,10},{10,8},{12,... | collective-permute-start | bytes 245768 | tf_op jit(solution)/shard_map/ppermute | solution.py:22
  85.5 11.0 %collective-permute-start.2 = (f32[4,5120]{1,0:T(4,128)S(1)}, f32[4,5120]{1,0:T(4,128)S(1)}, u32[]{:S(2)}, u32[]{:S(2)}) collective-permute-start(f32[4,5120]{1,0:T(4,128)S(1)} %add.232), channel_id=1, source_target_pairs={{0,4},{2,6},{4,0},{6,2},{1,5},{3,7},{5,1},{7,3},{8,12},{10,14},{12... | collective-permute-start | bytes 245768 | tf_op jit(solution)/shard_map/ppermute | solution.py:22
  92.3 17.8 %collective-permute-start.9 = (f32[4,20480]{1,0:T(4,128)S(1)}, f32[4,20480]{1,0:T(4,128)S(1)}, u32[]{:S(2)}, u32[]{:S(2)}) collective-permute-start(f32[4,20480]{1,0:T(4,128)S(1)} %add.286), channel_id=1, source_target_pairs={{0,8},{8,0},{16,24},{24,16},{32,40},{40,32},{48,56},{56,48},{1,9},... | collective-permute-start | bytes 983048 | tf_op jit(solution)/shard_map/ppermute | solution.py:22
  96.6 17.5 %collective-permute-start.3 = (f32[4,5120]{1,0:T(4,128)S(1)}, f32[4,5120]{1,0:T(4,128)S(1)}, u32[]{:S(2)}, u32[]{:S(2)}) collective-permute-start(f32[4,5120]{1,0:T(4,128)S(1)} %add.233), channel_id=1, source_target_pairs={{0,8},{8,0},{16,24},{24,16},{32,40},{40,32},{48,56},{56,48},{1,9},... | collective-permute-start | bytes 245768 | tf_op jit(solution)/shard_map/ppermute | solution.py:22
  110.2 42.1 %copy-start.5 = (f32[20480]{0:T(1024)S(1)}, f32[20480]{0:T(1024)}, u32[]{:S(2)}) copy-start(f32[20480]{0:T(1024)} %param.17) | copy-start | bytes 245764
  110.3 26.5 %collective-permute-start.10 = (f32[4,20480]{1,0:T(4,128)S(1)}, f32[4,20480]{1,0:T(4,128)S(1)}, u32[]{:S(2)}, u32[]{:S(2)}) collective-permute-start(f32[4,20480]{1,0:T(4,128)S(1)} %add.287), channel_id=1, source_target_pairs={{0,16},{8,24},{16,0},{24,8},{32,48},{40,56},{48,32},{56,40},{1,17}... | collective-permute-start | bytes 983048 | tf_op jit(solution)/shard_map/ppermute | solution.py:22
  114.1 49.7 %collective-permute-start.4 = (f32[4,5120]{1,0:T(4,128)S(1)}, f32[4,5120]{1,0:T(4,128)S(1)}, u32[]{:S(2)}, u32[]{:S(2)}) collective-permute-start(f32[4,5120]{1,0:T(4,128)S(1)} %add.234), channel_id=1, source_target_pairs={{0,16},{8,24},{16,0},{24,8},{32,48},{40,56},{48,32},{56,40},{1,17}... | collective-permute-start | bytes 245768 | tf_op jit(solution)/shard_map/ppermute | solution.py:22
  137.6 37.3 %collective-permute-start.11 = (f32[4,20480]{1,0:T(4,128)}, f32[4,20480]{1,0:T(4,128)}, u32[]{:S(2)}, u32[]{:S(2)}) collective-permute-start(f32[4,20480]{1,0:T(4,128)} %add.288), channel_id=1, source_target_pairs={{0,32},{8,40},{16,48},{24,56},{32,0},{40,8},{48,16},{56,24},{1,33}... | collective-permute-start | bytes 983048 | tf_op jit(solution)/shard_map/ppermute | solution.py:22
  152.4 10.8 %copy-start.2 = (f32[4]{0:T(128)S(1)}, f32[4]{0:T(128)}, u32[]{:S(2)}) copy-start(f32[4]{0:T(128)} %param.23) | copy-start | bytes 52
  163.9 8.7 %collective-permute-start.5 = (f32[4,5120]{1,0:T(4,128)S(1)}, f32[4,5120]{1,0:T(4,128)S(1)}, u32[]{:S(2)}, u32[]{:S(2)}) collective-permute-start(f32[4,5120]{1,0:T(4,128)S(1)} %add.235), channel_id=1, source_target_pairs={{0,32},{8,40},{16,48},{24,56},{32,0},{40,8},{48,16},{56,24},{1,33}... | collective-permute-start | bytes 245768 | tf_op jit(solution)/shard_map/ppermute | solution.py:22
  172.6 38.0 %copy-start.3 = (f32[128,5120]{0,1:T(8,128)S(1)}, f32[128,5120]{0,1:T(8,128)}, u32[]{:S(2)}) copy-start(f32[128,5120]{0,1:T(8,128)} %select_bitcast_fusion) | copy-start | bytes 7864324
  176.0 1.6 copy-start.4
  210.6 20.8 %copy-start.7 = (f32[512]{0:T(512)S(1)}, f32[512]{0:T(512)}, u32[]{:S(2)}) copy-start(f32[512]{0:T(512)} %param.18) | copy-start | bytes 6148
Sparse Core Ops, SparseCore 0:
  27.4 96.8 all-gather.1

commit v3 on v2

--- a/solution.py
+++ b/solution.py
@@ -9,19 +9,43 @@
 LINE = ("line_0", "line_1", "line_2")
 SNAP_LINE = ("snap", "line_0", "line_1", "line_2")
 HI = lax.Precision.HIGHEST
+STAGES = (("line_2", 1), ("line_1", 1), ("line_1", 2), ("line_0", 1), ("line_0", 2), ("line_0", 4))
 
 
 ramp_gain = 0.5
 
 
 def line_total(x):
-    for axis in ("line_2", "line_1", "line_0"):
+    for axis, step in STAGES:
         size = lax.axis_size(axis)
-        step = 1
-        while step < size:
-            x = x + lax.ppermute(x, axis, [(i, i ^ step) for i in range(size)])
-            step *= 2
+        x = x + lax.ppermute(x, axis, [(i, i ^ step) for i in range(size)])
     return x
+
+
+def line_scatter(x):
+    for axis, step in STAGES:
+        size = lax.axis_size(axis)
+        upper = (lax.axis_index(axis) // step) % 2 == 1
+        half = x.shape[1] // 2
+        keep = jnp.where(upper, x[:, half:], x[:, :half])
+        give = jnp.where(upper, x[:, :half], x[:, half:])
+        x = keep + lax.ppermute(give, axis, [(i, i ^ step) for i in range(size)])
+    return x
+
+
+def piece_order(sizes):
+    line_0, line_1, line_2 = sizes
+    slice_of = []
+    for i in range(line_0 * line_1 * line_2):
+        digits = {"line_0": i // (line_1 * line_2), "line_1": (i // line_2) % line_1, "line_2": i % line_2}
+        s = 0
+        for axis, step in STAGES:
+            s = s * 2 + (digits[axis] // step) % 2
+        slice_of.append(s)
+    owner_of = [0] * len(slice_of)
+    for i, s in enumerate(slice_of):
+        owner_of[s] = i
+    return owner_of
 
 
 def body(
@@ -52,7 +76,13 @@
         mine[:, None] & (rows_of[:, None] == jnp.arange(lines_here)[None, :]), 1.0, 0.0
     )
 
-    all_rows = line_total(jnp.dot(pick, ptdf_rows, precision=HI))
+    row_piece = line_scatter(jnp.dot(pick, ptdf_rows, precision=HI))
+    piece_width = row_piece.shape[1]
+    packed = row_piece.reshape(-1)
+    block_width = horizon // snap_count
+    extra_rows = -(-packed.shape[0] // block_width)
+    extra_rows += -(unit_count * snap_count + extra_rows) % 8
+    packed = jnp.pad(packed, (0, extra_rows * block_width - packed.shape[0])).reshape(extra_rows, block_width)
 
     padded = jnp.pad(plan, ((0, 0), (WMAX, 0)))
     inverse = 1.0 / min_up.astype(jnp.float32)
@@ -64,11 +94,14 @@
         lagged = lagged + shifted * (ramp_lag == offset).astype(jnp.float32)[:, None]
     dispatch = held_mean + ramp_gain * (plan - lagged)
     unit_blocks = lax.all_to_all(dispatch, "snap", split_axis=1, concat_axis=0, tiled=True)
-    everyone = lax.all_gather(unit_blocks, LINE, axis=0, tiled=True)
+    block_units = unit_blocks.shape[0]
+    everyone = lax.all_gather(
+        jnp.concatenate([unit_blocks, packed], axis=0), LINE, axis=0, tiled=True
+    )
 
     order_ids = unit_bus.reshape(snap_count, line_count, unit_count).transpose(1, 0, 2).reshape(-1)
-    columns = jnp.take(ptdf_rows, order_ids, axis=1)
-    row_columns = line_total(jnp.dot(pick, columns, precision=HI))
+    columns = jnp.take(ptdf_rows, order_ids, axis=1).reshape(lines_here, line_count, block_units)
+    columns = jnp.pad(columns, ((0, 0), (0, 0), (0, extra_rows))).reshape(lines_here, -1)
 
     probes = jnp.concatenate(
         [
@@ -78,10 +111,9 @@
         axis=1,
     )
     local_probe = jnp.dot(ptdf_rows, probes, preferred_element_type=jnp.float32, precision=HI)
-    row_probe = jnp.dot(all_rows, probes, preferred_element_type=jnp.float32, precision=HI)
+    row_probe = line_total(jnp.dot(pick, local_probe, precision=HI))
     load_flows = local_probe[:, 0]
     at_ends = local_probe[:, 1:]
-    row_load_flows = row_probe[:, 0]
     row_at_ends = row_probe[:, 1:]
 
     sens_ends = []
@@ -106,13 +138,6 @@
         weights.append(weight)
         row_coeff_list.append(row_coeffs)
 
-    sens_list = []
-    for step in range(NC):
-        current = all_rows[step]
-        for prior in range(step):
-            current = current - row_coeff_list[step][prior] * sens_list[prior]
-        sens_list.append(weights[step] * current)
-
     coeff_list = []
     for step in range(NC):
         coefficient = at_ends[:, 2 * step] - at_ends[:, 2 * step + 1]
@@ -122,14 +147,21 @@
             )
         coeff_list.append(coefficient)
 
-    flows_all = jnp.dot(
-        jnp.concatenate([columns, row_columns], axis=0),
-        everyone,
-        preferred_element_type=jnp.float32,
-        precision=HI,
-    )
-    base = flows_all[:lines_here] - load_flows[:, None] * system_load[None, :]
-    row_base = flows_all[lines_here:] - row_load_flows[:, None] * system_load[None, :]
+    gen_flows = jnp.dot(columns, everyone, preferred_element_type=jnp.float32, precision=HI)
+    base = gen_flows - load_flows[:, None] * system_load[None, :]
+    row_base = line_total(jnp.dot(pick, base, precision=HI))
+
+    pieces = everyone.reshape(line_count, block_units + extra_rows, block_width)[:, block_units:]
+    pieces = pieces.reshape(line_count, -1)[:, : NC * piece_width].reshape(line_count, NC, piece_width)
+    pieces = jnp.take(pieces, jnp.array(piece_order([lax.axis_size(a) for a in LINE])), axis=0)
+    all_rows = pieces.transpose(1, 0, 2).reshape(NC, buses)
+
+    sens_list = []
+    for step in range(NC):
+        current = all_rows[step]
+        for prior in range(step):
+            current = current - row_coeff_list[step][prior] * sens_list[prior]
+        sens_list.append(weights[step] * current)
 
     shift_list = []
     for step in range(NC):

time: 240 us -> 192 us (0.80)
  the two profiles are of different devices: /device:TPU:120 before, /device:TPU:2 now
where the time goes in v3:
time: 192 us; the launch traced here: 191 us
  local copies, waits for them, and re-layouts  44.2 us (23%)
  starting transfers between devices  40.7 us (21%)
  between operations  39.6 us (21%)
  matrix products  32.1 us (17%)
  waiting for transfers between devices  25.1 us (13%)
  other arithmetic  9.59 us (5%)
    ppermute x12, starting transfers between devices, line_total(): x = x + lax.ppermute(x, axis, [(i, i ^ step) for i in range(size)])  19.8 us
    gather x1, local copies, waits for them, and re-layouts, body(): jnp.take(ptdf_rows, order_ids, axis=1)  17.4 us
    ppermute x6, starting transfers between devices, line_scatter(): x = keep + lax.ppermute(give, axis, [(i, i ^ step) for i in range(size)])  16 us
    ppermute x12, waiting for transfers between devices, line_total(): x = x + lax.ppermute(x, axis, [(i, i ^ step) for i in range(size)])  14.4 us
    dot_general x1, matrix products, body(): jnp.dot(columns, everyone, preferred_element_type=jnp.float32, precision=HI)  13.1 us
    unnamed x23, local copies, waits for them, and re-layouts  12.6 us
    dot_general x1, matrix products, body(): jnp.dot(ptdf_rows, probes, preferred_element_type=jnp.float32, precision=HI)  10.8 us
    ppermute x6, waiting for transfers between devices, line_scatter(): x = keep + lax.ppermute(give, axis, [(i, i ^ step) for i in range(size)])  10.6 us
  transfers between devices with their start and end apart: 20, of which 13 were waited for; matrix products, arithmetic and copies ran while one was open for 31% of the time, Pallas kernels for 0%

profile of v3, /device:TPU:2, one launch (start us, length us, event | category | flops | bytes accessed | tf_op | source)
XLA Modules:
  0.0 191.2 jit_solution(9067945301560081246)
XLA Ops:
  9.8 7.7 %fusion.10 = f32[4,20480]{1,0:T(4,128)S(1)} fusion(f32[128,20480]{1,0:T(8,128)} %param.13, s32[4]{0:T(128)S(1)} %gather_fusion.2, pred[4]{0:T(512)(128)(4,1)S(1)} %broadcast_compare_fusion), kind=kOutput, calls=%fused_computation.65 | convolution fusion | flops 125830656 | bytes 10813460 | tf_op jit(solution)/shard_map/dot_general | solution.py:79
  20.9 2.9 %collective-permute-done.1 = f32[4,5120]{1,0:T(4,128)S(1)} collective-permute-done((f32[4,5120]{1,0:T(4,128)S(1)}, f32[4,5120]{1,0:T(4,128)S(1)}, u32[]{:S(2)}, u32[]{:S(2)}) %collective-permute-start.1) | collective-permute-done | bytes 81952 | tf_op jit(solution)/shard_map/ppermute | solution.py:32
  23.8 3.3 %collective-permute-start.2 = (f32[4,2560]{1,0:T(4,128)S(1)}, f32[4,2560]{1,0:T(4,128)S(1)}, u32[]{:S(2)}, u32[]{:S(2)}) collective-permute-start(f32[4,2560]{1,0:T(4,128)S(1)} %slice_select_fusion.2), channel_id=1, source_target_pairs={{0,4},{2,6},{4,0},{6,2},{1,5},{3,7},{5,1},{7,3},{8,12},{10,14},{12... | collective-permute-start | bytes 122888 | tf_op jit(solution)/shard_map/ppermute | solution.py:32
  27.1 2.3 %collective-permute-done.2 = f32[4,2560]{1,0:T(4,128)S(1)} collective-permute-done((f32[4,2560]{1,0:T(4,128)S(1)}, f32[4,2560]{1,0:T(4,128)S(1)}, u32[]{:S(2)}, u32[]{:S(2)}) %collective-permute-start.2) | collective-permute-done | bytes 40992 | tf_op jit(solution)/shard_map/ppermute | solution.py:32
  29.4 2.0 %collective-permute-start.3 = (f32[4,1280]{1,0:T(4,128)S(1)}, f32[4,1280]{1,0:T(4,128)S(1)}, u32[]{:S(2)}, u32[]{:S(2)}) collective-permute-start(f32[4,1280]{1,0:T(4,128)S(1)} %slice_select_fusion.3), channel_id=1, source_target_pairs={{0,8},{8,0},{16,24},{24,16},{32,40},{40,32},{48,56},{56,48},{1,9},... | collective-permute-start | bytes 61448 | tf_op jit(solution)/shard_map/ppermute | solution.py:32
  31.5 1.8 collective-permute-done.3
  33.3 3.5 %collective-permute-start.4 = (f32[4,640]{1,0:T(4,128)S(1)}, f32[4,640]{1,0:T(4,128)S(1)}, u32[]{:S(2)}, u32[]{:S(2)}) collective-permute-start(f32[4,640]{1,0:T(4,128)S(1)} %slice_select_fusion.4), channel_id=1, source_target_pairs={{0,16},{8,24},{16,0},{24,8},{32,48},{40,56},{48,32},{56,40},{1,17}... | collective-permute-start | bytes 30728 | tf_op jit(solution)/shard_map/ppermute | solution.py:32
  39.2 4.8 %all-to-all-start = ((f32[20,4,512]{2,0,1:T(8,128)}), f32[20,4,512]{2,0,1:T(8,128)S(1)}, u32[]{:S(2)}, u32[]{:S(2)}) async-start(f32[20,4,512]{2,0,1:T(8,128)} %copy.28), calls=%async_computation | async-start | bytes 393216 | tf_op jit(solution)/shard_map/all_to_all | solution.py:96
  44.1 5.5 %collective-permute-start.5 = (f32[4,320]{1,0:T(4,128)S(1)}, f32[4,320]{1,0:T(4,128)S(1)}, u32[]{:S(2)}, u32[]{:S(2)}) collective-permute-start(f32[4,320]{1,0:T(4,128)S(1)} %slice_select_fusion.5), channel_id=1, source_target_pairs={{0,32},{8,40},{16,48},{24,56},{32,0},{40,8},{48,16},{56,24},{1,33}... | collective-permute-start | bytes 15368 | tf_op jit(solution)/shard_map/ppermute | solution.py:32
  49.6 2.2 %collective-permute-done.5 = f32[4,320]{1,0:T(4,128)S(1)} collective-permute-done((f32[4,320]{1,0:T(4,128)S(1)}, f32[4,320]{1,0:T(4,128)S(1)}, u32[]{:S(2)}, u32[]{:S(2)}) %collective-permute-start.5) | collective-permute-done | bytes 5152 | tf_op jit(solution)/shard_map/ppermute | solution.py:32
  53.6 10.8 %fusion = f32[9,128]{1,0:T(8,128)S(1)} fusion(f32[128,20480]{1,0:T(8,128)} %param.13, f32[20480,8]{0,1:T(8,128)S(1)} %fusion.4, f32[20480,1]{0,1:T(1,128)S(1)} %bitcast.61), kind=kOutput, calls=%fused_computation.6 | convolution fusion | flops 283299840 | bytes 11227648 | tf_op jit(solution)/shard_map/dot_general | solution.py:113
  67.4 11.8 %copy.27 = f32[128,20480]{0,1:T(8,128)} copy(f32[128,20480]{1,0:T(8,128)} %param.13) | data formatting | bytes 20971520 | tf_op args[0]
  79.2 3.0 %collective-permute-start.8 = (f32[4,9]{1,0:T(4,128)S(1)}, f32[4,9]{1,0:T(4,128)S(1)}, u32[]{:S(2)}, u32[]{:S(2)}) collective-permute-start(f32[4,9]{1,0:T(4,128)S(1)} %add.347), channel_id=1, source_target_pairs={{0,4},{2,6},{4,0},{6,2},{1,5},{3,7},{5,1},{7,3},{8,12},{10,14},{12... | collective-permute-start | bytes 440 | tf_op jit(solution)/shard_map/ppermute | solution.py:21
  82.3 17.4 %gather_fusion = f32[5120,128]{1,0:T(8,128)S(1)} fusion(f32[128,20480]{0,1:T(8,128)} %copy.27, s32[5120]{0:T(1024)S(1)} %broadcast_clamp_fusion), kind=kCustom, calls=%fused_computation | custom fusion | bytes 5263360 | tf_op jit(solution)/shard_map/jit(_take)/gather | solution.py:103
  99.8 1.8 collective-permute-start.9
  101.7 2.5 %broadcast_select_fusion = f32[128,64,80]{0,2,1:T(8,128)} fusion(f32[128,64,80]{0,2,1:T(8,128)S(1)} %bitcast.54, pred[64,80]{1,0:T(8,128)(4,1)S(1)} %copy.25), kind=kLoop, calls=%fused_computation.10 | loop fusion | flops 655360 | bytes 5248000 | tf_op jit(solution)/shard_map/jit(_take)/select_n | solution.py:103
  105.0 3.8 %collective-permute-done.10 = f32[4,9]{1,0:T(4,128)S(1)} collective-permute-done((f32[4,9]{1,0:T(4,128)S(1)}, f32[4,9]{1,0:T(4,128)S(1)}, u32[]{:S(2)}, u32[]{:S(2)}) %collective-permute-start.10) | collective-permute-done | bytes 176 | tf_op jit(solution)/shard_map/ppermute | solution.py:21
  108.8 4.7 %collective-permute-start.11 = (f32[4,9]{1,0:T(4,128)S(1)}, f32[4,9]{1,0:T(4,128)S(1)}, u32[]{:S(2)}, u32[]{:S(2)}) collective-permute-start(f32[4,9]{1,0:T(4,128)S(1)} %add.350), channel_id=1, source_target_pairs={{0,32},{8,40},{16,48},{24,56},{32,0},{40,8},{48,16},{56,24},{1,33}... | collective-permute-start | bytes 440 | tf_op jit(solution)/shard_map/ppermute | solution.py:21
  114.1 1.9 %pad.12 = f32[128,64,88]{0,2,1:T(8,128)S(1)} pad(f32[128,64,80]{0,2,1:T(8,128)} %broadcast_select_fusion, f32[]{:T(128)} %constant.151.clone.1), padding=0_0x0_0x0_8 | pad | bytes 5505028 | tf_op jit(solution)/shard_map/jit(_pad)/pad | solution.py:104
  142.5 13.1 %convolution_subtract_fusion = f32[128,512]{1,0:T(8,128)S(1)} fusion(f32[128,5632]{0,1:T(8,128)S(1)} %bitcast.53, f32[5632,512]{1,0:T(8,128)} %all-gather.2.cloned.1.call-done, f32[512]{0:T(512)S(1)} %copy-done.5, f32[128]{0:T(128)S(1)} %get-tuple-element.25), kind=kOutput, calls=%fused_computation.11 | convolution fusion | flops 4429316096 | bytes 14682624 | tf_op jit(solution)/shard_map/dot_general | solution.py:150
  157.3 3.5 %collective-permute-done.13 = f32[4,512]{1,0:T(4,128)S(1)} collective-permute-done((f32[4,512]{1,0:T(4,128)S(1)}, f32[4,512]{1,0:T(4,128)S(1)}, u32[]{:S(2)}, u32[]{:S(2)}) %collective-permute-start.13) | collective-permute-done | bytes 8224 | tf_op jit(solution)/shard_map/ppermute | solution.py:21
  173.5 2.4 %collective-permute-done.16 = f32[4,512]{1,0:T(4,128)S(1)} collective-permute-done((f32[4,512]{1,0:T(4,128)S(1)}, f32[4,512]{1,0:T(4,128)S(1)}, u32[]{:S(2)}, u32[]{:S(2)}) %collective-permute-start.16) | collective-permute-done | bytes 8224 | tf_op jit(solution)/shard_map/ppermute | solution.py:21
  175.9 4.6 %collective-permute-start.17 = (f32[4,512]{1,0:T(4,128)S(1)}, f32[4,512]{1,0:T(4,128)S(1)}, u32[]{:S(2)}, u32[]{:S(2)}) collective-permute-start(f32[4,512]{1,0:T(4,128)S(1)} %add.357), channel_id=1, source_target_pairs={{0,32},{8,40},{16,48},{24,56},{32,0},{40,8},{48,16},{56,24},{1,33}... | collective-permute-start | bytes 24584 | tf_op jit(solution)/shard_map/ppermute | solution.py:21
  181.6 2.0 %collective-permute-done.17 = f32[4,512]{1,0:T(4,128)S(1)} collective-permute-done((f32[4,512]{1,0:T(4,128)S(1)}, f32[4,512]{1,0:T(4,128)S(1)}, u32[]{:S(2)}, u32[]{:S(2)}) %collective-permute-start.17) | collective-permute-done | bytes 8224 | tf_op jit(solution)/shard_map/ppermute | solution.py:21
  (126 shorter events, 32.3 us)
Async XLA Ops:
  9.8 27.0 %copy-start.2 = (f32[20,2048]{1,0:T(8,128)S(1)}, f32[20,2048]{1,0:T(8,128)}, u32[]{:S(2)}) copy-start(f32[20,2048]{1,0:T(8,128)} %param.14) | copy-start | bytes 491524
  17.5 35.2 %copy-start.6 = (s32[4,2]{0,1:T(2,128)S(1)}, s32[4,2]{0,1:T(2,128)}, u32[]{:S(2)}) copy-start(s32[4,2]{0,1:T(2,128)} %param.21) | copy-start | bytes 100
  17.5 36.1 %copy-start.3 = (f32[20480]{0:T(1024)S(1)}, f32[20480]{0:T(1024)}, u32[]{:S(2)}) copy-start(f32[20480]{0:T(1024)} %param.18) | copy-start | bytes 245764
  17.6 1.5 collective-permute-start
  19.2 4.6 %collective-permute-start.1 = (f32[4,5120]{1,0:T(4,128)S(1)}, f32[4,5120]{1,0:T(4,128)S(1)}, u32[]{:S(2)}, u32[]{:S(2)}) collective-permute-start(f32[4,5120]{1,0:T(4,128)S(1)} %slice_select_fusion.1), channel_id=1, source_target_pairs={{0,2},{2,0},{4,6},{6,4},{1,3},{3,1},{5,7},{7,5},{8,10},{10,8},{12,... | collective-permute-start | bytes 245768 | tf_op jit(solution)/shard_map/ppermute | solution.py:32
  23.8 5.6 %collective-permute-start.2 = (f32[4,2560]{1,0:T(4,128)S(1)}, f32[4,2560]{1,0:T(4,128)S(1)}, u32[]{:S(2)}, u32[]{:S(2)}) collective-permute-start(f32[4,2560]{1,0:T(4,128)S(1)} %slice_select_fusion.2), channel_id=1, source_target_pairs={{0,4},{2,6},{4,0},{6,2},{1,5},{3,7},{5,1},{7,3},{8,12},{10,14},{12... | collective-permute-start | bytes 122888 | tf_op jit(solution)/shard_map/ppermute | solution.py:32
  29.4 3.9 %collective-permute-start.3 = (f32[4,1280]{1,0:T(4,128)S(1)}, f32[4,1280]{1,0:T(4,128)S(1)}, u32[]{:S(2)}, u32[]{:S(2)}) collective-permute-start(f32[4,1280]{1,0:T(4,128)S(1)} %slice_select_fusion.3), channel_id=1, source_target_pairs={{0,8},{8,0},{16,24},{24,16},{32,40},{40,32},{48,56},{56,48},{1,9},... | collective-permute-start | bytes 61448 | tf_op jit(solution)/shard_map/ppermute | solution.py:32
  33.3 10.7 %collective-permute-start.4 = (f32[4,640]{1,0:T(4,128)S(1)}, f32[4,640]{1,0:T(4,128)S(1)}, u32[]{:S(2)}, u32[]{:S(2)}) collective-permute-start(f32[4,640]{1,0:T(4,128)S(1)} %slice_select_fusion.4), channel_id=1, source_target_pairs={{0,16},{8,24},{16,0},{24,8},{32,48},{40,56},{48,32},{56,40},{1,17}... | collective-permute-start | bytes 30728 | tf_op jit(solution)/shard_map/ppermute | solution.py:32
  39.2 10.4 %all-to-all-start = ((f32[20,4,512]{2,0,1:T(8,128)}), f32[20,4,512]{2,0,1:T(8,128)S(1)}, u32[]{:S(2)}, u32[]{:S(2)}) async-start(f32[20,4,512]{2,0,1:T(8,128)} %copy.28), calls=%async_computation | async-start | bytes 393216 | tf_op jit(solution)/shard_map/all_to_all | solution.py:96
  44.0 98.5 %all-gather.2.cloned.1.call-start = ((), (), s32[]{:S(2)}) async-start(), calls=%async_computation.1 | async-start | bytes 11714560 | tf_op jit(solution)/shard_map/all_gather | solution.py:98
  44.1 7.7 %collective-permute-start.5 = (f32[4,320]{1,0:T(4,128)S(1)}, f32[4,320]{1,0:T(4,128)S(1)}, u32[]{:S(2)}, u32[]{:S(2)}) collective-permute-start(f32[4,320]{1,0:T(4,128)S(1)} %slice_select_fusion.5), channel_id=1, source_target_pairs={{0,32},{8,40},{16,48},{24,56},{32,0},{40,8},{48,16},{56,24},{1,33}... | collective-permute-start | bytes 15368 | tf_op jit(solution)/shard_map/ppermute | solution.py:32
  64.7 1.2 collective-permute-start.6
  65.8 13.4 %collective-permute-start.7 = (f32[4,9]{1,0:T(4,128)S(1)}, f32[4,9]{1,0:T(4,128)S(1)}, u32[]{:S(2)}, u32[]{:S(2)}) collective-permute-start(f32[4,9]{1,0:T(4,128)S(1)} %add.346), channel_id=1, source_target_pairs={{0,2},{2,0},{4,6},{6,4},{1,3},{3,1},{5,7},{7,5},{8,10},{10,8},{12,... | collective-permute-start | bytes 440 | tf_op jit(solution)/shard_map/ppermute | solution.py:21
  79.2 20.5 %collective-permute-start.8 = (f32[4,9]{1,0:T(4,128)S(1)}, f32[4,9]{1,0:T(4,128)S(1)}, u32[]{:S(2)}, u32[]{:S(2)}) collective-permute-start(f32[4,9]{1,0:T(4,128)S(1)} %add.347), channel_id=1, source_target_pairs={{0,4},{2,6},{4,0},{6,2},{1,5},{3,7},{5,1},{7,3},{8,12},{10,14},{12... | collective-permute-start | bytes 440 | tf_op jit(solution)/shard_map/ppermute | solution.py:21
  99.8 4.3 %collective-permute-start.9 = (f32[4,9]{1,0:T(4,128)S(1)}, f32[4,9]{1,0:T(4,128)S(1)}, u32[]{:S(2)}, u32[]{:S(2)}) collective-permute-start(f32[4,9]{1,0:T(4,128)S(1)} %add.348), channel_id=1, source_target_pairs={{0,8},{8,0},{16,24},{24,16},{32,40},{40,32},{48,56},{56,48},{1,9},... | collective-permute-start | bytes 440 | tf_op jit(solution)/shard_map/ppermute | solution.py:21
  104.1 4.7 %collective-permute-start.10 = (f32[4,9]{1,0:T(4,128)S(1)}, f32[4,9]{1,0:T(4,128)S(1)}, u32[]{:S(2)}, u32[]{:S(2)}) collective-permute-start(f32[4,9]{1,0:T(4,128)S(1)} %add.349), channel_id=1, source_target_pairs={{0,16},{8,24},{16,0},{24,8},{32,48},{40,56},{48,32},{56,40},{1,17}... | collective-permute-start | bytes 440 | tf_op jit(solution)/shard_map/ppermute | solution.py:21
  105.0 37.6 %copy-start.5 = (f32[512]{0:T(512)S(1)}, f32[512]{0:T(512)}, u32[]{:S(2)}) copy-start(f32[512]{0:T(512)} %param.19) | copy-start | bytes 6148
  108.8 7.6 %collective-permute-start.11 = (f32[4,9]{1,0:T(4,128)S(1)}, f32[4,9]{1,0:T(4,128)S(1)}, u32[]{:S(2)}, u32[]{:S(2)}) collective-permute-start(f32[4,9]{1,0:T(4,128)S(1)} %add.350), channel_id=1, source_target_pairs={{0,32},{8,40},{16,48},{24,56},{32,0},{40,8},{48,16},{56,24},{1,33}... | collective-permute-start | bytes 440 | tf_op jit(solution)/shard_map/ppermute | solution.py:21
  155.9 1.2 collective-permute-start.12
  157.1 3.7 %collective-permute-start.13 = (f32[4,512]{1,0:T(4,128)S(1)}, f32[4,512]{1,0:T(4,128)S(1)}, u32[]{:S(2)}, u32[]{:S(2)}) collective-permute-start(f32[4,512]{1,0:T(4,128)S(1)} %add.353), channel_id=1, source_target_pairs={{0,2},{2,0},{4,6},{6,4},{1,3},{3,1},{5,7},{7,5},{8,10},{10,8},{12,... | collective-permute-start | bytes 24584 | tf_op jit(solution)/shard_map/ppermute | solution.py:21
  160.8 6.9 %collective-permute-start.14 = (f32[4,512]{1,0:T(4,128)S(1)}, f32[4,512]{1,0:T(4,128)S(1)}, u32[]{:S(2)}, u32[]{:S(2)}) collective-permute-start(f32[4,512]{1,0:T(4,128)S(1)} %add.354), channel_id=1, source_target_pairs={{0,4},{2,6},{4,0},{6,2},{1,5},{3,7},{5,1},{7,3},{8,12},{10,14},{12... | collective-permute-start | bytes 24584 | tf_op jit(solution)/shard_map/ppermute | solution.py:21
  167.6 3.7 %collective-permute-start.15 = (f32[4,512]{1,0:T(4,128)S(1)}, f32[4,512]{1,0:T(4,128)S(1)}, u32[]{:S(2)}, u32[]{:S(2)}) collective-permute-start(f32[4,512]{1,0:T(4,128)S(1)} %add.355), channel_id=1, source_target_pairs={{0,8},{8,0},{16,24},{24,16},{32,40},{40,32},{48,56},{56,48},{1,9},... | collective-permute-start | bytes 24584 | tf_op jit(solution)/shard_map/ppermute | solution.py:21
  171.4 4.5 %collective-permute-start.16 = (f32[4,512]{1,0:T(4,128)S(1)}, f32[4,512]{1,0:T(4,128)S(1)}, u32[]{:S(2)}, u32[]{:S(2)}) collective-permute-start(f32[4,512]{1,0:T(4,128)S(1)} %add.356), channel_id=1, source_target_pairs={{0,16},{8,24},{16,0},{24,8},{32,48},{40,56},{48,32},{56,40},{1,17}... | collective-permute-start | bytes 24584 | tf_op jit(solution)/shard_map/ppermute | solution.py:21
  175.9 7.6 %collective-permute-start.17 = (f32[4,512]{1,0:T(4,128)S(1)}, f32[4,512]{1,0:T(4,128)S(1)}, u32[]{:S(2)}, u32[]{:S(2)}) collective-permute-start(f32[4,512]{1,0:T(4,128)S(1)} %add.357), channel_id=1, source_target_pairs={{0,32},{8,40},{16,48},{24,56},{32,0},{40,8},{48,16},{56,24},{1,33}... | collective-permute-start | bytes 24584 | tf_op jit(solution)/shard_map/ppermute | solution.py:21
  (6 other events, 59.4 us)
Sparse Core Ops, SparseCore 0:
  52.9 88.8 all-gather.1

commit v4 on v3

--- a/solution.py
+++ b/solution.py
@@ -76,14 +76,6 @@
         mine[:, None] & (rows_of[:, None] == jnp.arange(lines_here)[None, :]), 1.0, 0.0
     )
 
-    row_piece = line_scatter(jnp.dot(pick, ptdf_rows, precision=HI))
-    piece_width = row_piece.shape[1]
-    packed = row_piece.reshape(-1)
-    block_width = horizon // snap_count
-    extra_rows = -(-packed.shape[0] // block_width)
-    extra_rows += -(unit_count * snap_count + extra_rows) % 8
-    packed = jnp.pad(packed, (0, extra_rows * block_width - packed.shape[0])).reshape(extra_rows, block_width)
-
     padded = jnp.pad(plan, ((0, 0), (WMAX, 0)))
     inverse = 1.0 / min_up.astype(jnp.float32)
     held_mean = jnp.zeros(plan.shape, jnp.float32)
@@ -94,6 +86,15 @@
         lagged = lagged + shifted * (ramp_lag == offset).astype(jnp.float32)[:, None]
     dispatch = held_mean + ramp_gain * (plan - lagged)
     unit_blocks = lax.all_to_all(dispatch, "snap", split_axis=1, concat_axis=0, tiled=True)
+
+    dispatch, pick = lax.optimization_barrier((dispatch, pick))
+    row_piece = line_scatter(jnp.dot(pick, ptdf_rows, precision=HI))
+    piece_width = row_piece.shape[1]
+    packed = row_piece.reshape(-1)
+    block_width = horizon // snap_count
+    extra_rows = -(-packed.shape[0] // block_width)
+    extra_rows += -(unit_count * snap_count + extra_rows) % 8
+    packed = jnp.pad(packed, (0, extra_rows * block_width - packed.shape[0])).reshape(extra_rows, block_width)
     block_units = unit_blocks.shape[0]
     everyone = lax.all_gather(
         jnp.concatenate([unit_blocks, packed], axis=0), LINE, axis=0, tiled=True

time: 192 us -> 200 us (1.042)
  other arithmetic: 9.59 us -> 16.9 us
    add x1, other arithmetic: 1.54 us -> 6.7 us  [body(): dispatch = held_mean + ramp_gain * (plan - lagged)]
    unnamed x23 -> x17, local copies, waits for them, and re-layouts: 12.6 us -> 12.6 us
  transfers between devices with their start and end apart: 20 -> 20, of which waited for: 13 -> 13; matrix products, arithmetic and copies ran while one was open for 31% -> 29% of each run, Pallas kernels for 0% -> 0%
where the time goes in v4:
time: 200 us; the launch traced here: 199 us
  local copies, waits for them, and re-layouts  44.3 us (22%)
  starting transfers between devices  40.3 us (20%)
  between operations  40 us (20%)
  matrix products  31.9 us (16%)
  waiting for transfers between devices  25.5 us (13%)
  other arithmetic  16.9 us (8%)
    ppermute x12, starting transfers between devices, line_total(): x = x + lax.ppermute(x, axis, [(i, i ^ step) for i in range(size)])  19.5 us
    gather x1, local copies, waits for them, and re-layouts, body(): jnp.take(ptdf_rows, order_ids, axis=1)  17.4 us
    ppermute x6, starting transfers between devices, line_scatter(): x = keep + lax.ppermute(give, axis, [(i, i ^ step) for i in range(size)])  16 us
    ppermute x12, waiting for transfers between devices, line_total(): x = x + lax.ppermute(x, axis, [(i, i ^ step) for i in range(size)])  14.7 us
    dot_general x1, matrix products, body(): jnp.dot(columns, everyone, preferred_element_type=jnp.float32, precision=HI)  13.1 us
    unnamed x17, local copies, waits for them, and re-layouts  12.6 us
    dot_general x1, matrix products, body(): jnp.dot(ptdf_rows, probes, preferred_element_type=jnp.float32, precision=HI)  10.8 us
    ppermute x6, waiting for transfers between devices, line_scatter(): x = keep + lax.ppermute(give, axis, [(i, i ^ step) for i in range(size)])  10.7 us
  transfers between devices with their start and end apart: 20, of which 13 were waited for; matrix products, arithmetic and copies ran while one was open for 29% of the time, Pallas kernels for 0%

profile of v4, /device:TPU:2, one launch (start us, length us, event | category | flops | bytes accessed | tf_op | source)
XLA Modules:
  0.0 198.9 jit_solution(11118435700842984069)
XLA Ops:
  11.9 6.7 %multiply_add_fusion = f32[20,2048]{1,0:T(8,128)S(1)} fusion(f32[20,2048]{1,0:T(8,128)} %param.14, f32[20]{0:T(128)S(1)} %get-tuple-element.109, f32[20]{0:T(128)S(1)} %get-tuple-element.110, f32[20]{0:T(128)S(1)} %get-tuple-element.88, f32[20]{0:T(128)S(1)} %get-tuple-element.89, f32[20]{0:T(128)S(1)} %get-tuple-element.90, f32[20]{0:T(128)S(1)} %get-tuple-element.91, ...), kind=kLoop, calls=%fused_computation.16 | loop fusion | flops 3973120 | bytes 331520 | tf_op jit(solution)/shard_map/add | solution.py:87
  18.7 7.6 %fusion.32 = f32[4,20480]{1,0:T(4,128)S(1)} fusion(f32[4,128]{1,0:T(4,128)S(1)} %fusion.11, f32[128,20480]{1,0:T(8,128)} %param.13), kind=kOutput, calls=%fused_computation.151 | convolution fusion | flops 125829120 | bytes 10815488 | tf_op jit(solution)/shard_map/dot_general | solution.py:91
  29.6 2.9 %collective-permute-done.1 = f32[4,5120]{1,0:T(4,128)S(1)} collective-permute-done((f32[4,5120]{1,0:T(4,128)S(1)}, f32[4,5120]{1,0:T(4,128)S(1)}, u32[]{:S(2)}, u32[]{:S(2)}) %collective-permute-start.1) | collective-permute-done | bytes 81952 | tf_op jit(solution)/shard_map/ppermute | solution.py:32
  32.6 3.3 %collective-permute-start.2 = (f32[4,2560]{1,0:T(4,128)S(1)}, f32[4,2560]{1,0:T(4,128)S(1)}, u32[]{:S(2)}, u32[]{:S(2)}) collective-permute-start(f32[4,2560]{1,0:T(4,128)S(1)} %slice_select_fusion.2), channel_id=1, source_target_pairs={{0,4},{2,6},{4,0},{6,2},{1,5},{3,7},{5,1},{7,3},{8,12},{10,14},{12... | collective-permute-start | bytes 122888 | tf_op jit(solution)/shard_map/ppermute | solution.py:32
  35.8 2.3 %collective-permute-done.2 = f32[4,2560]{1,0:T(4,128)S(1)} collective-permute-done((f32[4,2560]{1,0:T(4,128)S(1)}, f32[4,2560]{1,0:T(4,128)S(1)}, u32[]{:S(2)}, u32[]{:S(2)}) %collective-permute-start.2) | collective-permute-done | bytes 40992 | tf_op jit(solution)/shard_map/ppermute | solution.py:32
  38.2 2.0 %collective-permute-start.3 = (f32[4,1280]{1,0:T(4,128)S(1)}, f32[4,1280]{1,0:T(4,128)S(1)}, u32[]{:S(2)}, u32[]{:S(2)}) collective-permute-start(f32[4,1280]{1,0:T(4,128)S(1)} %slice_select_fusion.3), channel_id=1, source_target_pairs={{0,8},{8,0},{16,24},{24,16},{32,40},{40,32},{48,56},{56,48},{1,9},... | collective-permute-start | bytes 61448 | tf_op jit(solution)/shard_map/ppermute | solution.py:32
  42.1 3.5 %collective-permute-start.4 = (f32[4,640]{1,0:T(4,128)S(1)}, f32[4,640]{1,0:T(4,128)S(1)}, u32[]{:S(2)}, u32[]{:S(2)}) collective-permute-start(f32[4,640]{1,0:T(4,128)S(1)} %slice_select_fusion.4), channel_id=1, source_target_pairs={{0,16},{8,24},{16,0},{24,8},{32,48},{40,56},{48,32},{56,40},{1,17}... | collective-permute-start | bytes 30728 | tf_op jit(solution)/shard_map/ppermute | solution.py:32
  46.4 4.8 %all-to-all-start = ((f32[20,4,512]{2,0,1:T(8,128)}), f32[20,4,512]{2,0,1:T(8,128)S(1)}, u32[]{:S(2)}, u32[]{:S(2)}) async-start(f32[20,4,512]{2,0,1:T(8,128)} %copy.28), calls=%async_computation | async-start | bytes 393216 | tf_op jit(solution)/shard_map/all_to_all | solution.py:88
  51.3 5.5 %collective-permute-start.5 = (f32[4,320]{1,0:T(4,128)S(1)}, f32[4,320]{1,0:T(4,128)S(1)}, u32[]{:S(2)}, u32[]{:S(2)}) collective-permute-start(f32[4,320]{1,0:T(4,128)S(1)} %slice_select_fusion.5), channel_id=1, source_target_pairs={{0,32},{8,40},{16,48},{24,56},{32,0},{40,8},{48,16},{56,24},{1,33}... | collective-permute-start | bytes 15368 | tf_op jit(solution)/shard_map/ppermute | solution.py:32
  56.8 2.2 %collective-permute-done.5 = f32[4,320]{1,0:T(4,128)S(1)} collective-permute-done((f32[4,320]{1,0:T(4,128)S(1)}, f32[4,320]{1,0:T(4,128)S(1)}, u32[]{:S(2)}, u32[]{:S(2)}) %collective-permute-start.5) | collective-permute-done | bytes 5152 | tf_op jit(solution)/shard_map/ppermute | solution.py:32
  60.9 10.8 %fusion = f32[9,128]{1,0:T(8,128)S(1)} fusion(f32[128,20480]{1,0:T(8,128)} %param.13, f32[20480,8]{0,1:T(8,128)S(1)} %fusion.4, f32[20480,1]{0,1:T(1,128)S(1)} %bitcast.64), kind=kOutput, calls=%fused_computation.6 | convolution fusion | flops 283299840 | bytes 11227648 | tf_op jit(solution)/shard_map/dot_general | solution.py:114
  74.6 11.8 %copy.27 = f32[128,20480]{0,1:T(8,128)} copy(f32[128,20480]{1,0:T(8,128)} %param.13) | data formatting | bytes 20971520 | tf_op args[0]
  86.4 3.0 %collective-permute-start.8 = (f32[4,9]{1,0:T(4,128)S(1)}, f32[4,9]{1,0:T(4,128)S(1)}, u32[]{:S(2)}, u32[]{:S(2)}) collective-permute-start(f32[4,9]{1,0:T(4,128)S(1)} %add.347), channel_id=1, source_target_pairs={{0,4},{2,6},{4,0},{6,2},{1,5},{3,7},{5,1},{7,3},{8,12},{10,14},{12... | collective-permute-start | bytes 440 | tf_op jit(solution)/shard_map/ppermute | solution.py:21
  89.5 17.4 %gather_fusion = f32[5120,128]{1,0:T(8,128)S(1)} fusion(f32[128,20480]{0,1:T(8,128)} %copy.27, s32[5120]{0:T(1024)S(1)} %broadcast_clamp_fusion), kind=kCustom, calls=%fused_computation | custom fusion | bytes 5263360 | tf_op jit(solution)/shard_map/jit(_take)/gather | solution.py:104
  106.9 1.9 collective-permute-start.9
  108.8 2.4 %broadcast_select_fusion = f32[128,64,80]{0,2,1:T(8,128)} fusion(f32[128,64,80]{0,2,1:T(8,128)S(1)} %bitcast.57, pred[64,80]{1,0:T(8,128)(4,1)S(1)} %copy.25), kind=kLoop, calls=%fused_computation.10 | loop fusion | flops 655360 | bytes 5248000 | tf_op jit(solution)/shard_map/jit(_take)/select_n | solution.py:104
  112.1 3.8 %collective-permute-done.10 = f32[4,9]{1,0:T(4,128)S(1)} collective-permute-done((f32[4,9]{1,0:T(4,128)S(1)}, f32[4,9]{1,0:T(4,128)S(1)}, u32[]{:S(2)}, u32[]{:S(2)}) %collective-permute-start.10) | collective-permute-done | bytes 176 | tf_op jit(solution)/shard_map/ppermute | solution.py:21
  115.9 4.7 %collective-permute-start.11 = (f32[4,9]{1,0:T(4,128)S(1)}, f32[4,9]{1,0:T(4,128)S(1)}, u32[]{:S(2)}, u32[]{:S(2)}) collective-permute-start(f32[4,9]{1,0:T(4,128)S(1)} %add.350), channel_id=1, source_target_pairs={{0,32},{8,40},{16,48},{24,56},{32,0},{40,8},{48,16},{56,24},{1,33}... | collective-permute-start | bytes 440 | tf_op jit(solution)/shard_map/ppermute | solution.py:21
  121.3 1.9 pad.12
  150.0 13.1 %convolution_subtract_fusion = f32[128,512]{1,0:T(8,128)S(1)} fusion(f32[128,5632]{0,1:T(8,128)S(1)} %bitcast.56, f32[5632,512]{1,0:T(8,128)} %all-gather.2.cloned.1.call-done, f32[512]{0:T(512)S(1)} %copy-done.4, f32[128]{0:T(128)S(1)} %get-tuple-element.27), kind=kOutput, calls=%fused_computation.11 | convolution fusion | flops 4429316096 | bytes 14682624 | tf_op jit(solution)/shard_map/dot_general | solution.py:151
  164.9 3.3 %collective-permute-done.13 = f32[4,512]{1,0:T(4,128)S(1)} collective-permute-done((f32[4,512]{1,0:T(4,128)S(1)}, f32[4,512]{1,0:T(4,128)S(1)}, u32[]{:S(2)}, u32[]{:S(2)}) %collective-permute-start.13) | collective-permute-done | bytes 8224 | tf_op jit(solution)/shard_map/ppermute | solution.py:21
  180.8 2.8 %collective-permute-done.16 = f32[4,512]{1,0:T(4,128)S(1)} collective-permute-done((f32[4,512]{1,0:T(4,128)S(1)}, f32[4,512]{1,0:T(4,128)S(1)}, u32[]{:S(2)}, u32[]{:S(2)}) %collective-permute-start.16) | collective-permute-done | bytes 8224 | tf_op jit(solution)/shard_map/ppermute | solution.py:21
  183.6 4.6 %collective-permute-start.17 = (f32[4,512]{1,0:T(4,128)S(1)}, f32[4,512]{1,0:T(4,128)S(1)}, u32[]{:S(2)}, u32[]{:S(2)}) collective-permute-start(f32[4,512]{1,0:T(4,128)S(1)} %add.357), channel_id=1, source_target_pairs={{0,32},{8,40},{16,48},{24,56},{32,0},{40,8},{48,16},{56,24},{1,33}... | collective-permute-start | bytes 24584 | tf_op jit(solution)/shard_map/ppermute | solution.py:21
  189.2 2.0 collective-permute-done.17
  (121 shorter events, 34.6 us)
Async XLA Ops:
  26.3 33.7 %copy-start.5 = (s32[4,2]{0,1:T(2,128)S(1)}, s32[4,2]{0,1:T(2,128)}, u32[]{:S(2)}) copy-start(s32[4,2]{0,1:T(2,128)} %param.21) | copy-start | bytes 100
  26.3 34.6 %copy-start.2 = (f32[20480]{0:T(1024)S(1)}, f32[20480]{0:T(1024)}, u32[]{:S(2)}) copy-start(f32[20480]{0:T(1024)} %param.18) | copy-start | bytes 245764
  26.4 1.5 collective-permute-start
  27.9 4.6 %collective-permute-start.1 = (f32[4,5120]{1,0:T(4,128)S(1)}, f32[4,5120]{1,0:T(4,128)S(1)}, u32[]{:S(2)}, u32[]{:S(2)}) collective-permute-start(f32[4,5120]{1,0:T(4,128)S(1)} %slice_select_fusion.1), channel_id=1, source_target_pairs={{0,2},{2,0},{4,6},{6,4},{1,3},{3,1},{5,7},{7,5},{8,10},{10,8},{12,... | collective-permute-start | bytes 245768 | tf_op jit(solution)/shard_map/ppermute | solution.py:32
  32.6 5.6 %collective-permute-start.2 = (f32[4,2560]{1,0:T(4,128)S(1)}, f32[4,2560]{1,0:T(4,128)S(1)}, u32[]{:S(2)}, u32[]{:S(2)}) collective-permute-start(f32[4,2560]{1,0:T(4,128)S(1)} %slice_select_fusion.2), channel_id=1, source_target_pairs={{0,4},{2,6},{4,0},{6,2},{1,5},{3,7},{5,1},{7,3},{8,12},{10,14},{12... | collective-permute-start | bytes 122888 | tf_op jit(solution)/shard_map/ppermute | solution.py:32
  38.2 3.9 %collective-permute-start.3 = (f32[4,1280]{1,0:T(4,128)S(1)}, f32[4,1280]{1,0:T(4,128)S(1)}, u32[]{:S(2)}, u32[]{:S(2)}) collective-permute-start(f32[4,1280]{1,0:T(4,128)S(1)} %slice_select_fusion.3), channel_id=1, source_target_pairs={{0,8},{8,0},{16,24},{24,16},{32,40},{40,32},{48,56},{56,48},{1,9},... | collective-permute-start | bytes 61448 | tf_op jit(solution)/shard_map/ppermute | solution.py:32
  42.1 9.1 %collective-permute-start.4 = (f32[4,640]{1,0:T(4,128)S(1)}, f32[4,640]{1,0:T(4,128)S(1)}, u32[]{:S(2)}, u32[]{:S(2)}) collective-permute-start(f32[4,640]{1,0:T(4,128)S(1)} %slice_select_fusion.4), channel_id=1, source_target_pairs={{0,16},{8,24},{16,0},{24,8},{32,48},{40,56},{48,32},{56,40},{1,17}... | collective-permute-start | bytes 30728 | tf_op jit(solution)/shard_map/ppermute | solution.py:32
  46.4 10.4 %all-to-all-start = ((f32[20,4,512]{2,0,1:T(8,128)}), f32[20,4,512]{2,0,1:T(8,128)S(1)}, u32[]{:S(2)}, u32[]{:S(2)}) async-start(f32[20,4,512]{2,0,1:T(8,128)} %copy.28), calls=%async_computation | async-start | bytes 393216 | tf_op jit(solution)/shard_map/all_to_all | solution.py:88
  51.2 98.8 %all-gather.2.cloned.1.call-start = ((), (), s32[]{:S(2)}) async-start(), calls=%async_computation.1 | async-start | bytes 11714560 | tf_op jit(solution)/shard_map/all_gather | solution.py:99
  51.3 7.7 %collective-permute-start.5 = (f32[4,320]{1,0:T(4,128)S(1)}, f32[4,320]{1,0:T(4,128)S(1)}, u32[]{:S(2)}, u32[]{:S(2)}) collective-permute-start(f32[4,320]{1,0:T(4,128)S(1)} %slice_select_fusion.5), channel_id=1, source_target_pairs={{0,32},{8,40},{16,48},{24,56},{32,0},{40,8},{48,16},{56,24},{1,33}... | collective-permute-start | bytes 15368 | tf_op jit(solution)/shard_map/ppermute | solution.py:32
  71.8 1.2 collective-permute-start.6
  73.0 13.4 %collective-permute-start.7 = (f32[4,9]{1,0:T(4,128)S(1)}, f32[4,9]{1,0:T(4,128)S(1)}, u32[]{:S(2)}, u32[]{:S(2)}) collective-permute-start(f32[4,9]{1,0:T(4,128)S(1)} %add.346), channel_id=1, source_target_pairs={{0,2},{2,0},{4,6},{6,4},{1,3},{3,1},{5,7},{7,5},{8,10},{10,8},{12,... | collective-permute-start | bytes 440 | tf_op jit(solution)/shard_map/ppermute | solution.py:21
  86.4 20.5 %collective-permute-start.8 = (f32[4,9]{1,0:T(4,128)S(1)}, f32[4,9]{1,0:T(4,128)S(1)}, u32[]{:S(2)}, u32[]{:S(2)}) collective-permute-start(f32[4,9]{1,0:T(4,128)S(1)} %add.347), channel_id=1, source_target_pairs={{0,4},{2,6},{4,0},{6,2},{1,5},{3,7},{5,1},{7,3},{8,12},{10,14},{12... | collective-permute-start | bytes 440 | tf_op jit(solution)/shard_map/ppermute | solution.py:21
  106.9 4.3 %collective-permute-start.9 = (f32[4,9]{1,0:T(4,128)S(1)}, f32[4,9]{1,0:T(4,128)S(1)}, u32[]{:S(2)}, u32[]{:S(2)}) collective-permute-start(f32[4,9]{1,0:T(4,128)S(1)} %add.348), channel_id=1, source_target_pairs={{0,8},{8,0},{16,24},{24,16},{32,40},{40,32},{48,56},{56,48},{1,9},... | collective-permute-start | bytes 440 | tf_op jit(solution)/shard_map/ppermute | solution.py:21
  111.3 4.6 %collective-permute-start.10 = (f32[4,9]{1,0:T(4,128)S(1)}, f32[4,9]{1,0:T(4,128)S(1)}, u32[]{:S(2)}, u32[]{:S(2)}) collective-permute-start(f32[4,9]{1,0:T(4,128)S(1)} %add.349), channel_id=1, source_target_pairs={{0,16},{8,24},{16,0},{24,8},{32,48},{40,56},{48,32},{56,40},{1,17}... | collective-permute-start | bytes 440 | tf_op jit(solution)/shard_map/ppermute | solution.py:21
  112.1 37.9 %copy-start.4 = (f32[512]{0:T(512)S(1)}, f32[512]{0:T(512)}, u32[]{:S(2)}) copy-start(f32[512]{0:T(512)} %param.19) | copy-start | bytes 6148
  115.9 7.6 %collective-permute-start.11 = (f32[4,9]{1,0:T(4,128)S(1)}, f32[4,9]{1,0:T(4,128)S(1)}, u32[]{:S(2)}, u32[]{:S(2)}) collective-permute-start(f32[4,9]{1,0:T(4,128)S(1)} %add.350), channel_id=1, source_target_pairs={{0,32},{8,40},{16,48},{24,56},{32,0},{40,8},{48,16},{56,24},{1,33}... | collective-permute-start | bytes 440 | tf_op jit(solution)/shard_map/ppermute | solution.py:21
  150.0 14.9 %copy-start.6 = (s32[64]{0:T(128)S(1)}, s32[64]{0:T(128)}, u32[]{:S(2)}) copy-start(s32[64]{0:T(128)} %constant.201) | copy-start | bytes 772
  163.4 1.2 collective-permute-start.12
  164.6 3.7 %collective-permute-start.13 = (f32[4,512]{1,0:T(4,128)S(1)}, f32[4,512]{1,0:T(4,128)S(1)}, u32[]{:S(2)}, u32[]{:S(2)}) collective-permute-start(f32[4,512]{1,0:T(4,128)S(1)} %add.353), channel_id=1, source_target_pairs={{0,2},{2,0},{4,6},{6,4},{1,3},{3,1},{5,7},{7,5},{8,10},{10,8},{12,... | collective-permute-start | bytes 24584 | tf_op jit(solution)/shard_map/ppermute | solution.py:21
  168.3 7.0 %collective-permute-start.14 = (f32[4,512]{1,0:T(4,128)S(1)}, f32[4,512]{1,0:T(4,128)S(1)}, u32[]{:S(2)}, u32[]{:S(2)}) collective-permute-start(f32[4,512]{1,0:T(4,128)S(1)} %add.354), channel_id=1, source_target_pairs={{0,4},{2,6},{4,0},{6,2},{1,5},{3,7},{5,1},{7,3},{8,12},{10,14},{12... | collective-permute-start | bytes 24584 | tf_op jit(solution)/shard_map/ppermute | solution.py:21
  175.3 3.7 %collective-permute-start.15 = (f32[4,512]{1,0:T(4,128)S(1)}, f32[4,512]{1,0:T(4,128)S(1)}, u32[]{:S(2)}, u32[]{:S(2)}) collective-permute-start(f32[4,512]{1,0:T(4,128)S(1)} %add.355), channel_id=1, source_target_pairs={{0,8},{8,0},{16,24},{24,16},{32,40},{40,32},{48,56},{56,48},{1,9},... | collective-permute-start | bytes 24584 | tf_op jit(solution)/shard_map/ppermute | solution.py:21
  179.0 4.5 %collective-permute-start.16 = (f32[4,512]{1,0:T(4,128)S(1)}, f32[4,512]{1,0:T(4,128)S(1)}, u32[]{:S(2)}, u32[]{:S(2)}) collective-permute-start(f32[4,512]{1,0:T(4,128)S(1)} %add.356), channel_id=1, source_target_pairs={{0,16},{8,24},{16,0},{24,8},{32,48},{40,56},{48,32},{56,40},{1,17}... | collective-permute-start | bytes 24584 | tf_op jit(solution)/shard_map/ppermute | solution.py:21
  183.6 7.6 %collective-permute-start.17 = (f32[4,512]{1,0:T(4,128)S(1)}, f32[4,512]{1,0:T(4,128)S(1)}, u32[]{:S(2)}, u32[]{:S(2)}) collective-permute-start(f32[4,512]{1,0:T(4,128)S(1)} %add.357), channel_id=1, source_target_pairs={{0,32},{8,40},{16,48},{24,56},{32,0},{40,8},{48,16},{56,24},{1,33}... | collective-permute-start | bytes 24584 | tf_op jit(solution)/shard_map/ppermute | solution.py:21
  (3 other events, 18.3 us)
Sparse Core Ops, SparseCore 0:
  60.1 88.7 all-gather.1

commit v5 on v3

--- a/solution.py
+++ b/solution.py
@@ -76,7 +76,7 @@
         mine[:, None] & (rows_of[:, None] == jnp.arange(lines_here)[None, :]), 1.0, 0.0
     )
 
-    row_piece = line_scatter(jnp.dot(pick, ptdf_rows, precision=HI))
+    row_piece = line_scatter(jnp.where(mine[:, None], jnp.take(ptdf_rows, rows_of, axis=0), 0.0))
     piece_width = row_piece.shape[1]
     packed = row_piece.reshape(-1)
     block_width = horizon // snap_count

time: 192 us -> 190 us (0.990)
  matrix products: 32.1 us -> 24.4 us
  local copies, waits for them, and re-layouts: 44.2 us -> 49.1 us
    dot_general x1 -> x0, matrix products: 7.68 us -> none  [body(): row_piece = line_scatter(jnp.dot(pick, ptdf_rows, precision=HI))]
    gather x0 -> x1, local copies, waits for them, and re-layouts: none -> 4.87 us  [body(): jnp.take(ptdf_rows, rows_of, axis=0)]
  transfers between devices with their start and end apart: 20 -> 20, of which waited for: 13 -> 13; matrix products, arithmetic and copies ran while one was open for 31% -> 32% of each run, Pallas kernels for 0% -> 0%
where the time goes in v5:
time: 190 us; the launch traced here: 189 us
  local copies, waits for them, and re-layouts  49.1 us (26%)
  starting transfers between devices  40.8 us (21%)
  between operations  39.7 us (21%)
  waiting for transfers between devices  25 us (13%)
  matrix products  24.4 us (13%)
  other arithmetic  9.76 us (5%)
    ppermute x12, starting transfers between devices, line_total(): x = x + lax.ppermute(x, axis, [(i, i ^ step) for i in range(size)])  20.1 us
    gather x1, local copies, waits for them, and re-layouts, body(): jnp.take(ptdf_rows, order_ids, axis=1)  17.4 us
    ppermute x6, starting transfers between devices, line_scatter(): x = keep + lax.ppermute(give, axis, [(i, i ^ step) for i in range(size)])  15.8 us
    ppermute x12, waiting for transfers between devices, line_total(): x = x + lax.ppermute(x, axis, [(i, i ^ step) for i in range(size)])  14.3 us
    dot_general x1, matrix products, body(): jnp.dot(columns, everyone, preferred_element_type=jnp.float32, precision=HI)  13.1 us
    unnamed x23, local copies, waits for them, and re-layouts  12.6 us
    dot_general x1, matrix products, body(): jnp.dot(ptdf_rows, probes, preferred_element_type=jnp.float32, precision=HI)  10.8 us
    ppermute x6, waiting for transfers between devices, line_scatter(): x = keep + lax.ppermute(give, axis, [(i, i ^ step) for i in range(size)])  10.6 us
  transfers between devices with their start and end apart: 20, of which 13 were waited for; matrix products, arithmetic and copies ran while one was open for 32% of the time, Pallas kernels for 0%

profile of v5, /device:TPU:2, one launch (start us, length us, event | category | flops | bytes accessed | tf_op | source)
XLA Modules:
  0.0 188.7 jit_solution(11366396214548014265)
XLA Ops:
  9.8 4.9 %gather_fusion.3 = f32[4,20480]{1,0:T(4,128)S(1)} fusion(f32[128,20480]{1,0:T(8,128)} %param.13, s32[1024]{0:T(1024)S(1)} %pad_clamp_fusion.1), kind=kCustom, calls=%fused_computation.3 | custom fusion | bytes 655376 | tf_op jit(solution)/shard_map/jit(_take)/gather | solution.py:79
  18.2 2.9 %collective-permute-done.1 = f32[4,5120]{1,0:T(4,128)S(1)} collective-permute-done((f32[4,5120]{1,0:T(4,128)S(1)}, f32[4,5120]{1,0:T(4,128)S(1)}, u32[]{:S(2)}, u32[]{:S(2)}) %collective-permute-start.1) | collective-permute-done | bytes 81952 | tf_op jit(solution)/shard_map/ppermute | solution.py:32
  21.2 3.3 %collective-permute-start.2 = (f32[4,2560]{1,0:T(4,128)S(1)}, f32[4,2560]{1,0:T(4,128)S(1)}, u32[]{:S(2)}, u32[]{:S(2)}) collective-permute-start(f32[4,2560]{1,0:T(4,128)S(1)} %slice_select_fusion.2), channel_id=1, source_target_pairs={{0,4},{2,6},{4,0},{6,2},{1,5},{3,7},{5,1},{7,3},{8,12},{10,14},{12... | collective-permute-start | bytes 122888 | tf_op jit(solution)/shard_map/ppermute | solution.py:32
  24.5 2.3 %collective-permute-done.2 = f32[4,2560]{1,0:T(4,128)S(1)} collective-permute-done((f32[4,2560]{1,0:T(4,128)S(1)}, f32[4,2560]{1,0:T(4,128)S(1)}, u32[]{:S(2)}, u32[]{:S(2)}) %collective-permute-start.2) | collective-permute-done | bytes 40992 | tf_op jit(solution)/shard_map/ppermute | solution.py:32
  26.8 2.0 %collective-permute-start.3 = (f32[4,1280]{1,0:T(4,128)S(1)}, f32[4,1280]{1,0:T(4,128)S(1)}, u32[]{:S(2)}, u32[]{:S(2)}) collective-permute-start(f32[4,1280]{1,0:T(4,128)S(1)} %slice_select_fusion.3), channel_id=1, source_target_pairs={{0,8},{8,0},{16,24},{24,16},{32,40},{40,32},{48,56},{56,48},{1,9},... | collective-permute-start | bytes 61448 | tf_op jit(solution)/shard_map/ppermute | solution.py:32
  28.9 1.8 collective-permute-done.3
  30.7 3.5 %collective-permute-start.4 = (f32[4,640]{1,0:T(4,128)S(1)}, f32[4,640]{1,0:T(4,128)S(1)}, u32[]{:S(2)}, u32[]{:S(2)}) collective-permute-start(f32[4,640]{1,0:T(4,128)S(1)} %slice_select_fusion.4), channel_id=1, source_target_pairs={{0,16},{8,24},{16,0},{24,8},{32,48},{40,56},{48,32},{56,40},{1,17}... | collective-permute-start | bytes 30728 | tf_op jit(solution)/shard_map/ppermute | solution.py:32
  36.6 4.8 %all-to-all-start = ((f32[20,4,512]{2,0,1:T(8,128)}), f32[20,4,512]{2,0,1:T(8,128)S(1)}, u32[]{:S(2)}, u32[]{:S(2)}) async-start(f32[20,4,512]{2,0,1:T(8,128)} %copy.28), calls=%async_computation | async-start | bytes 393216 | tf_op jit(solution)/shard_map/all_to_all | solution.py:96
  41.5 5.3 %collective-permute-start.5 = (f32[4,320]{1,0:T(4,128)S(1)}, f32[4,320]{1,0:T(4,128)S(1)}, u32[]{:S(2)}, u32[]{:S(2)}) collective-permute-start(f32[4,320]{1,0:T(4,128)S(1)} %slice_select_fusion.5), channel_id=1, source_target_pairs={{0,32},{8,40},{16,48},{24,56},{32,0},{40,8},{48,16},{56,24},{1,33}... | collective-permute-start | bytes 15368 | tf_op jit(solution)/shard_map/ppermute | solution.py:32
  46.8 2.2 %collective-permute-done.5 = f32[4,320]{1,0:T(4,128)S(1)} collective-permute-done((f32[4,320]{1,0:T(4,128)S(1)}, f32[4,320]{1,0:T(4,128)S(1)}, u32[]{:S(2)}, u32[]{:S(2)}) %collective-permute-start.5) | collective-permute-done | bytes 5152 | tf_op jit(solution)/shard_map/ppermute | solution.py:32
  50.8 10.8 %fusion = f32[9,128]{1,0:T(8,128)S(1)} fusion(f32[128,20480]{1,0:T(8,128)} %param.13, f32[20480,8]{0,1:T(8,128)S(1)} %fusion.4, f32[20480,1]{0,1:T(1,128)S(1)} %bitcast.64), kind=kOutput, calls=%fused_computation.7 | convolution fusion | flops 283299840 | bytes 11227648 | tf_op jit(solution)/shard_map/dot_general | solution.py:113
  64.6 11.8 %copy.27 = f32[128,20480]{0,1:T(8,128)} copy(f32[128,20480]{1,0:T(8,128)} %param.13) | data formatting | bytes 20971520 | tf_op args[0]
  76.4 3.0 %collective-permute-start.8 = (f32[4,9]{1,0:T(4,128)S(1)}, f32[4,9]{1,0:T(4,128)S(1)}, u32[]{:S(2)}, u32[]{:S(2)}) collective-permute-start(f32[4,9]{1,0:T(4,128)S(1)} %add.364), channel_id=1, source_target_pairs={{0,4},{2,6},{4,0},{6,2},{1,5},{3,7},{5,1},{7,3},{8,12},{10,14},{12... | collective-permute-start | bytes 440 | tf_op jit(solution)/shard_map/ppermute | solution.py:21
  79.5 17.4 %gather_fusion = f32[5120,128]{1,0:T(8,128)S(1)} fusion(f32[128,20480]{0,1:T(8,128)} %copy.27, s32[5120]{0:T(1024)S(1)} %broadcast_clamp_fusion), kind=kCustom, calls=%fused_computation | custom fusion | bytes 5263360 | tf_op jit(solution)/shard_map/jit(_take)/gather | solution.py:103
  97.0 1.8 collective-permute-start.9
  98.8 2.5 %broadcast_select_fusion = f32[128,64,80]{0,2,1:T(8,128)} fusion(f32[128,64,80]{0,2,1:T(8,128)S(1)} %bitcast.57, pred[64,80]{1,0:T(8,128)(4,1)S(1)} %copy.25), kind=kLoop, calls=%fused_computation.11 | loop fusion | flops 655360 | bytes 5248000 | tf_op jit(solution)/shard_map/jit(_take)/select_n | solution.py:103
  102.2 3.8 %collective-permute-done.10 = f32[4,9]{1,0:T(4,128)S(1)} collective-permute-done((f32[4,9]{1,0:T(4,128)S(1)}, f32[4,9]{1,0:T(4,128)S(1)}, u32[]{:S(2)}, u32[]{:S(2)}) %collective-permute-start.10) | collective-permute-done | bytes 176 | tf_op jit(solution)/shard_map/ppermute | solution.py:21
  106.0 4.7 %collective-permute-start.11 = (f32[4,9]{1,0:T(4,128)S(1)}, f32[4,9]{1,0:T(4,128)S(1)}, u32[]{:S(2)}, u32[]{:S(2)}) collective-permute-start(f32[4,9]{1,0:T(4,128)S(1)} %add.367), channel_id=1, source_target_pairs={{0,32},{8,40},{16,48},{24,56},{32,0},{40,8},{48,16},{56,24},{1,33}... | collective-permute-start | bytes 440 | tf_op jit(solution)/shard_map/ppermute | solution.py:21
  111.3 1.9 %pad.12 = f32[128,64,88]{0,2,1:T(8,128)S(1)} pad(f32[128,64,80]{0,2,1:T(8,128)} %broadcast_select_fusion, f32[]{:T(128)} %constant.163.clone.1), padding=0_0x0_0x0_8 | pad | bytes 5505028 | tf_op jit(solution)/shard_map/jit(_pad)/pad | solution.py:104
  139.7 13.1 %convolution_subtract_fusion = f32[128,512]{1,0:T(8,128)S(1)} fusion(f32[128,5632]{0,1:T(8,128)S(1)} %bitcast.56, f32[5632,512]{1,0:T(8,128)} %all-gather.2.cloned.1.call-done, f32[512]{0:T(512)S(1)} %copy-done.5, f32[128]{0:T(128)S(1)} %get-tuple-element.25), kind=kOutput, calls=%fused_computation.12 | convolution fusion | flops 4429316096 | bytes 14682624 | tf_op jit(solution)/shard_map/dot_general | solution.py:150
  154.5 3.5 %collective-permute-done.13 = f32[4,512]{1,0:T(4,128)S(1)} collective-permute-done((f32[4,512]{1,0:T(4,128)S(1)}, f32[4,512]{1,0:T(4,128)S(1)}, u32[]{:S(2)}, u32[]{:S(2)}) %collective-permute-start.13) | collective-permute-done | bytes 8224 | tf_op jit(solution)/shard_map/ppermute | solution.py:21
  170.9 2.4 %collective-permute-done.16 = f32[4,512]{1,0:T(4,128)S(1)} collective-permute-done((f32[4,512]{1,0:T(4,128)S(1)}, f32[4,512]{1,0:T(4,128)S(1)}, u32[]{:S(2)}, u32[]{:S(2)}) %collective-permute-start.16) | collective-permute-done | bytes 8224 | tf_op jit(solution)/shard_map/ppermute | solution.py:21
  173.4 4.6 %collective-permute-start.17 = (f32[4,512]{1,0:T(4,128)S(1)}, f32[4,512]{1,0:T(4,128)S(1)}, u32[]{:S(2)}, u32[]{:S(2)}) collective-permute-start(f32[4,512]{1,0:T(4,128)S(1)} %add.374), channel_id=1, source_target_pairs={{0,32},{8,40},{16,48},{24,56},{32,0},{40,8},{48,16},{56,24},{1,33}... | collective-permute-start | bytes 24584 | tf_op jit(solution)/shard_map/ppermute | solution.py:21
  179.0 1.9 %collective-permute-done.17 = f32[4,512]{1,0:T(4,128)S(1)} collective-permute-done((f32[4,512]{1,0:T(4,128)S(1)}, f32[4,512]{1,0:T(4,128)S(1)}, u32[]{:S(2)}, u32[]{:S(2)}) %collective-permute-start.17) | collective-permute-done | bytes 8224 | tf_op jit(solution)/shard_map/ppermute | solution.py:21
  (130 shorter events, 32.7 us)
Async XLA Ops:
  9.8 24.3 %copy-start.2 = (f32[20,2048]{1,0:T(8,128)S(1)}, f32[20,2048]{1,0:T(8,128)}, u32[]{:S(2)}) copy-start(f32[20,2048]{1,0:T(8,128)} %param.14) | copy-start | bytes 491524
  14.7 35.2 %copy-start.6 = (s32[4,2]{0,1:T(2,128)S(1)}, s32[4,2]{0,1:T(2,128)}, u32[]{:S(2)}) copy-start(s32[4,2]{0,1:T(2,128)} %param.21) | copy-start | bytes 100
  14.9 35.9 %copy-start.3 = (f32[20480]{0:T(1024)S(1)}, f32[20480]{0:T(1024)}, u32[]{:S(2)}) copy-start(f32[20480]{0:T(1024)} %param.18) | copy-start | bytes 245764
  15.0 1.5 collective-permute-start
  16.5 4.6 %collective-permute-start.1 = (f32[4,5120]{1,0:T(4,128)S(1)}, f32[4,5120]{1,0:T(4,128)S(1)}, u32[]{:S(2)}, u32[]{:S(2)}) collective-permute-start(f32[4,5120]{1,0:T(4,128)S(1)} %slice_select_fusion.1), channel_id=1, source_target_pairs={{0,2},{2,0},{4,6},{6,4},{1,3},{3,1},{5,7},{7,5},{8,10},{10,8},{12,... | collective-permute-start | bytes 245768 | tf_op jit(solution)/shard_map/ppermute | solution.py:32
  21.2 5.6 %collective-permute-start.2 = (f32[4,2560]{1,0:T(4,128)S(1)}, f32[4,2560]{1,0:T(4,128)S(1)}, u32[]{:S(2)}, u32[]{:S(2)}) collective-permute-start(f32[4,2560]{1,0:T(4,128)S(1)} %slice_select_fusion.2), channel_id=1, source_target_pairs={{0,4},{2,6},{4,0},{6,2},{1,5},{3,7},{5,1},{7,3},{8,12},{10,14},{12... | collective-permute-start | bytes 122888 | tf_op jit(solution)/shard_map/ppermute | solution.py:32
  26.8 3.9 %collective-permute-start.3 = (f32[4,1280]{1,0:T(4,128)S(1)}, f32[4,1280]{1,0:T(4,128)S(1)}, u32[]{:S(2)}, u32[]{:S(2)}) collective-permute-start(f32[4,1280]{1,0:T(4,128)S(1)} %slice_select_fusion.3), channel_id=1, source_target_pairs={{0,8},{8,0},{16,24},{24,16},{32,40},{40,32},{48,56},{56,48},{1,9},... | collective-permute-start | bytes 61448 | tf_op jit(solution)/shard_map/ppermute | solution.py:32
  30.7 10.7 %collective-permute-start.4 = (f32[4,640]{1,0:T(4,128)S(1)}, f32[4,640]{1,0:T(4,128)S(1)}, u32[]{:S(2)}, u32[]{:S(2)}) collective-permute-start(f32[4,640]{1,0:T(4,128)S(1)} %slice_select_fusion.4), channel_id=1, source_target_pairs={{0,16},{8,24},{16,0},{24,8},{32,48},{40,56},{48,32},{56,40},{1,17}... | collective-permute-start | bytes 30728 | tf_op jit(solution)/shard_map/ppermute | solution.py:32
  36.6 10.2 %all-to-all-start = ((f32[20,4,512]{2,0,1:T(8,128)}), f32[20,4,512]{2,0,1:T(8,128)S(1)}, u32[]{:S(2)}, u32[]{:S(2)}) async-start(f32[20,4,512]{2,0,1:T(8,128)} %copy.28), calls=%async_computation | async-start | bytes 393216 | tf_op jit(solution)/shard_map/all_to_all | solution.py:96
  41.4 98.3 %all-gather.2.cloned.1.call-start = ((), (), s32[]{:S(2)}) async-start(), calls=%async_computation.1 | async-start | bytes 11714560 | tf_op jit(solution)/shard_map/all_gather | solution.py:98
  41.5 7.6 %collective-permute-start.5 = (f32[4,320]{1,0:T(4,128)S(1)}, f32[4,320]{1,0:T(4,128)S(1)}, u32[]{:S(2)}, u32[]{:S(2)}) collective-permute-start(f32[4,320]{1,0:T(4,128)S(1)} %slice_select_fusion.5), channel_id=1, source_target_pairs={{0,32},{8,40},{16,48},{24,56},{32,0},{40,8},{48,16},{56,24},{1,33}... | collective-permute-start | bytes 15368 | tf_op jit(solution)/shard_map/ppermute | solution.py:32
  61.9 1.2 collective-permute-start.6
  63.0 13.4 %collective-permute-start.7 = (f32[4,9]{1,0:T(4,128)S(1)}, f32[4,9]{1,0:T(4,128)S(1)}, u32[]{:S(2)}, u32[]{:S(2)}) collective-permute-start(f32[4,9]{1,0:T(4,128)S(1)} %add.363), channel_id=1, source_target_pairs={{0,2},{2,0},{4,6},{6,4},{1,3},{3,1},{5,7},{7,5},{8,10},{10,8},{12,... | collective-permute-start | bytes 440 | tf_op jit(solution)/shard_map/ppermute | solution.py:21
  76.4 20.5 %collective-permute-start.8 = (f32[4,9]{1,0:T(4,128)S(1)}, f32[4,9]{1,0:T(4,128)S(1)}, u32[]{:S(2)}, u32[]{:S(2)}) collective-permute-start(f32[4,9]{1,0:T(4,128)S(1)} %add.364), channel_id=1, source_target_pairs={{0,4},{2,6},{4,0},{6,2},{1,5},{3,7},{5,1},{7,3},{8,12},{10,14},{12... | collective-permute-start | bytes 440 | tf_op jit(solution)/shard_map/ppermute | solution.py:21
  97.0 4.3 %collective-permute-start.9 = (f32[4,9]{1,0:T(4,128)S(1)}, f32[4,9]{1,0:T(4,128)S(1)}, u32[]{:S(2)}, u32[]{:S(2)}) collective-permute-start(f32[4,9]{1,0:T(4,128)S(1)} %add.365), channel_id=1, source_target_pairs={{0,8},{8,0},{16,24},{24,16},{32,40},{40,32},{48,56},{56,48},{1,9},... | collective-permute-start | bytes 440 | tf_op jit(solution)/shard_map/ppermute | solution.py:21
  101.3 4.7 %collective-permute-start.10 = (f32[4,9]{1,0:T(4,128)S(1)}, f32[4,9]{1,0:T(4,128)S(1)}, u32[]{:S(2)}, u32[]{:S(2)}) collective-permute-start(f32[4,9]{1,0:T(4,128)S(1)} %add.366), channel_id=1, source_target_pairs={{0,16},{8,24},{16,0},{24,8},{32,48},{40,56},{48,32},{56,40},{1,17}... | collective-permute-start | bytes 440 | tf_op jit(solution)/shard_map/ppermute | solution.py:21
  102.1 37.6 %copy-start.5 = (f32[512]{0:T(512)S(1)}, f32[512]{0:T(512)}, u32[]{:S(2)}) copy-start(f32[512]{0:T(512)} %param.19) | copy-start | bytes 6148
  106.0 7.6 %collective-permute-start.11 = (f32[4,9]{1,0:T(4,128)S(1)}, f32[4,9]{1,0:T(4,128)S(1)}, u32[]{:S(2)}, u32[]{:S(2)}) collective-permute-start(f32[4,9]{1,0:T(4,128)S(1)} %add.367), channel_id=1, source_target_pairs={{0,32},{8,40},{16,48},{24,56},{32,0},{40,8},{48,16},{56,24},{1,33}... | collective-permute-start | bytes 440 | tf_op jit(solution)/shard_map/ppermute | solution.py:21
  153.1 1.2 collective-permute-start.12
  154.3 3.7 %collective-permute-start.13 = (f32[4,512]{1,0:T(4,128)S(1)}, f32[4,512]{1,0:T(4,128)S(1)}, u32[]{:S(2)}, u32[]{:S(2)}) collective-permute-start(f32[4,512]{1,0:T(4,128)S(1)} %add.370), channel_id=1, source_target_pairs={{0,2},{2,0},{4,6},{6,4},{1,3},{3,1},{5,7},{7,5},{8,10},{10,8},{12,... | collective-permute-start | bytes 24584 | tf_op jit(solution)/shard_map/ppermute | solution.py:21
  158.0 6.9 %collective-permute-start.14 = (f32[4,512]{1,0:T(4,128)S(1)}, f32[4,512]{1,0:T(4,128)S(1)}, u32[]{:S(2)}, u32[]{:S(2)}) collective-permute-start(f32[4,512]{1,0:T(4,128)S(1)} %add.371), channel_id=1, source_target_pairs={{0,4},{2,6},{4,0},{6,2},{1,5},{3,7},{5,1},{7,3},{8,12},{10,14},{12... | collective-permute-start | bytes 24584 | tf_op jit(solution)/shard_map/ppermute | solution.py:21
  164.8 4.0 %collective-permute-start.15 = (f32[4,512]{1,0:T(4,128)S(1)}, f32[4,512]{1,0:T(4,128)S(1)}, u32[]{:S(2)}, u32[]{:S(2)}) collective-permute-start(f32[4,512]{1,0:T(4,128)S(1)} %add.372), channel_id=1, source_target_pairs={{0,8},{8,0},{16,24},{24,16},{32,40},{40,32},{48,56},{56,48},{1,9},... | collective-permute-start | bytes 24584 | tf_op jit(solution)/shard_map/ppermute | solution.py:21
  168.8 4.5 %collective-permute-start.16 = (f32[4,512]{1,0:T(4,128)S(1)}, f32[4,512]{1,0:T(4,128)S(1)}, u32[]{:S(2)}, u32[]{:S(2)}) collective-permute-start(f32[4,512]{1,0:T(4,128)S(1)} %add.373), channel_id=1, source_target_pairs={{0,16},{8,24},{16,0},{24,8},{32,48},{40,56},{48,32},{56,40},{1,17}... | collective-permute-start | bytes 24584 | tf_op jit(solution)/shard_map/ppermute | solution.py:21
  173.4 7.6 %collective-permute-start.17 = (f32[4,512]{1,0:T(4,128)S(1)}, f32[4,512]{1,0:T(4,128)S(1)}, u32[]{:S(2)}, u32[]{:S(2)}) collective-permute-start(f32[4,512]{1,0:T(4,128)S(1)} %add.374), channel_id=1, source_target_pairs={{0,32},{8,40},{16,48},{24,56},{32,0},{40,8},{48,16},{56,24},{1,33}... | collective-permute-start | bytes 24584 | tf_op jit(solution)/shard_map/ppermute | solution.py:21
  (6 other events, 55.4 us)
Sparse Core Ops, SparseCore 0:
  50.1 88.8 all-gather.1

commit v6 on v5

--- a/solution.py
+++ b/solution.py
@@ -22,29 +22,37 @@
     return x
 
 
+def line_total_wide(x):
+    x = x + lax.ppermute(x, "line_2", [(i, i ^ 1) for i in range(lax.axis_size("line_2"))])
+    chips = ("line_0", "line_1")
+    count = lax.axis_size(chips)
+    rows, width = x.shape
+    parts = x.reshape(rows, count, width // count).transpose(1, 0, 2)
+    mine = lax.all_to_all(parts, chips, 0, 0, tiled=True).sum(axis=0)
+    spread = jnp.broadcast_to(mine[None], (count,) + mine.shape)
+    whole = lax.all_to_all(spread, chips, 0, 0, tiled=True)
+    return whole.transpose(1, 0, 2).reshape(rows, width)
+
+
 def line_scatter(x):
-    for axis, step in STAGES:
-        size = lax.axis_size(axis)
-        upper = (lax.axis_index(axis) // step) % 2 == 1
-        half = x.shape[1] // 2
-        keep = jnp.where(upper, x[:, half:], x[:, :half])
-        give = jnp.where(upper, x[:, :half], x[:, half:])
-        x = keep + lax.ppermute(give, axis, [(i, i ^ step) for i in range(size)])
-    return x
+    upper = lax.axis_index("line_2") == 1
+    half = x.shape[1] // 2
+    keep = jnp.where(upper, x[:, half:], x[:, :half])
+    give = jnp.where(upper, x[:, :half], x[:, half:])
+    x = keep + lax.ppermute(give, "line_2", [(i, i ^ 1) for i in range(lax.axis_size("line_2"))])
+    chips = ("line_0", "line_1")
+    count = lax.axis_size(chips)
+    rows, width = x.shape
+    parts = x.reshape(rows, count, width // count).transpose(1, 0, 2)
+    return lax.all_to_all(parts, chips, 0, 0, tiled=True).sum(axis=0)
 
 
 def piece_order(sizes):
     line_0, line_1, line_2 = sizes
-    slice_of = []
-    for i in range(line_0 * line_1 * line_2):
-        digits = {"line_0": i // (line_1 * line_2), "line_1": (i // line_2) % line_1, "line_2": i % line_2}
-        s = 0
-        for axis, step in STAGES:
-            s = s * 2 + (digits[axis] // step) % 2
-        slice_of.append(s)
-    owner_of = [0] * len(slice_of)
-    for i, s in enumerate(slice_of):
-        owner_of[s] = i
+    owner_of = [0] * (line_0 * line_1 * line_2)
+    for i in range(len(owner_of)):
+        digits = (i // (line_1 * line_2), (i // line_2) % line_1, i % line_2)
+        owner_of[digits[2] * line_0 * line_1 + digits[0] * line_1 + digits[1]] = i
     return owner_of
 
 
@@ -149,7 +157,7 @@
 
     gen_flows = jnp.dot(columns, everyone, preferred_element_type=jnp.float32, precision=HI)
     base = gen_flows - load_flows[:, None] * system_load[None, :]
-    row_base = line_total(jnp.dot(pick, base, precision=HI))
+    row_base = line_total_wide(jnp.dot(pick, base, precision=HI))
 
     pieces = everyone.reshape(line_count, block_units + extra_rows, block_width)[:, block_units:]
     pieces = pieces.reshape(line_count, -1)[:, : NC * piece_width].reshape(line_count, NC, piece_width)

time: 190 us -> 201 us (1.058)
  waiting for transfers between devices: 25 us -> 43.1 us
  starting transfers between devices: 40.8 us -> 31.2 us
  local copies, waits for them, and re-layouts: 49.1 us -> 51.8 us
    all_to_all x0 -> x3, waiting for transfers between devices: none -> 29.8 us  [the longest x1 11.2 us: line_scatter(): return lax.all_to_all(parts, chips, 0, 0, tiled=True).sum(axis=0)]
    all_to_all x0 -> x3, starting transfers between devices: none -> 18.9 us  [the longest x1 10.5 us: line_scatter(): return lax.all_to_all(parts, chips, 0, 0, tiled=True).sum(axis=0)]
    ppermute x6 -> x2, starting transfers between devices: 15.8 us -> 0.1 us  [the longest x1 0.09 us: line_scatter(): lax.ppermute(give, 'line_2', [(i, i ^ 1) for i in range(lax.axis_size('li...]
    ppermute x12 -> x6, starting transfers between devices: 20.1 us -> 6.58 us  [line_total(): x = x + lax.ppermute(x, axis, [(i, i ^ step) for i in range(size)])]
    ppermute x6 -> x2, waiting for transfers between devices: 10.6 us -> 0.01 us  [the longest x1 0.01 us: line_scatter(): lax.ppermute(give, 'line_2', [(i, i ^ 1) for i in range(lax.axis_size('li...]
    ppermute x12 -> x6, waiting for transfers between devices: 14.3 us -> 8.81 us  [line_total(): x = x + lax.ppermute(x, axis, [(i, i ^ step) for i in range(size)])]
    all_to_all x1, waiting for transfers between devices: 0.01 us -> 4.43 us  [body(): lax.all_to_all(dispatch, 'snap', split_axis=1, concat_axis=0, tiled=True)]
  transfers between devices with their start and end apart: 20 -> 13, of which waited for: 13 -> 8; matrix products, arithmetic and copies ran while one was open for 32% -> 31% of each run, Pallas kernels for 0% -> 0%
where the time goes in v6:
time: 201 us; the launch traced here: 200 us
  local copies, waits for them, and re-layouts  51.8 us (26%)
  waiting for transfers between devices  43.1 us (21%)
  between operations  39.6 us (20%)
  starting transfers between devices  31.2 us (16%)
  matrix products  24.4 us (12%)
  other arithmetic  9.85 us (5%)
    gather x1, local copies, waits for them, and re-layouts, body(): jnp.take(ptdf_rows, order_ids, axis=1)  17.4 us
    dot_general x1, matrix products, body(): jnp.dot(columns, everyone, preferred_element_type=jnp.float32, precision=HI)  13.1 us
    unnamed x23, local copies, waits for them, and re-layouts  12.5 us
    all_to_all x1, waiting for transfers between devices, line_scatter(): return lax.all_to_all(parts, chips, 0, 0, tiled=True).sum(axis=0)  11.2 us
    dot_general x1, matrix products, body(): jnp.dot(ptdf_rows, probes, preferred_element_type=jnp.float32, precision=HI)  10.8 us
    all_to_all x1, starting transfers between devices, line_scatter(): return lax.all_to_all(parts, chips, 0, 0, tiled=True).sum(axis=0)  10.5 us
    all_to_all x1, waiting for transfers between devices, line_total_wide(): mine = lax.all_to_all(parts, chips, 0, 0, tiled=True).sum(axis=0)  9.63 us
    all_to_all x1, waiting for transfers between devices, line_total_wide(): whole = lax.all_to_all(spread, chips, 0, 0, tiled=True)  8.98 us
  transfers between devices with their start and end apart: 13, of which 8 were waited for; matrix products, arithmetic and copies ran while one was open for 31% of the time, Pallas kernels for 0%

profile of v6, /device:TPU:2, one launch (start us, length us, event | category | flops | bytes accessed | tf_op | source)
XLA Modules:
  0.0 199.9 jit_solution(14114007844623924864)
XLA Ops:
  8.6 1.3 gather_fusion.1
  9.9 4.8 %gather_fusion.3 = f32[4,20480]{1,0:T(4,128)S(1)} fusion(f32[128,20480]{1,0:T(8,128)} %param.13, s32[1024]{0:T(1024)S(1)} %pad_clamp_fusion.1), kind=kCustom, calls=%fused_computation.3 | custom fusion | bytes 655376 | tf_op jit(solution)/shard_map/jit(_take)/gather | solution.py:87
  15.2 1.6 multiply_add_fusion
  17.6 5.6 %all-to-all-start = ((f32[20,4,512]{2,0,1:T(8,128)}), f32[20,4,512]{2,0,1:T(8,128)S(1)}, u32[]{:S(2)}, u32[]{:S(2)}) async-start(f32[20,4,512]{2,0,1:T(8,128)} %copy.28), calls=%async_computation | async-start | bytes 393216 | tf_op jit(solution)/shard_map/all_to_all | solution.py:104
  24.2 4.4 %all-to-all-done = f32[20,4,512]{2,0,1:T(8,128)S(1)} async-done(((f32[20,4,512]{2,0,1:T(8,128)}), f32[20,4,512]{2,0,1:T(8,128)S(1)}, u32[]{:S(2)}, u32[]{:S(2)}) %all-to-all-start) | async-done | bytes 163872 | tf_op jit(solution)/shard_map/all_to_all | solution.py:104
  28.6 10.5 %all-to-all-start.1 = ((f32[32,4,320]{2,1,0:T(4,128)}), f32[32,4,320]{2,1,0:T(4,128)S(1)}, u32[]{:S(2)}, u32[]{:S(2)}) async-start(f32[32,4,320]{2,1,0:T(4,128)} %bitcast.55), calls=%async_computation.1 | async-start | bytes 393216 | tf_op jit(solution)/shard_map/all_to_all | solution.py:47
  39.1 11.2 %all-to-all-done.1 = f32[32,4,320]{2,1,0:T(4,128)S(1)} async-done(((f32[32,4,320]{2,1,0:T(4,128)}), f32[32,4,320]{2,1,0:T(4,128)S(1)}, u32[]{:S(2)}, u32[]{:S(2)}) %all-to-all-start.1) | async-done | bytes 163872 | tf_op jit(solution)/shard_map/all_to_all | solution.py:47
  52.1 10.8 %fusion = f32[9,128]{1,0:T(8,128)S(1)} fusion(f32[128,20480]{1,0:T(8,128)} %param.13, f32[20480,8]{0,1:T(8,128)S(1)} %fusion.4, f32[20480,1]{0,1:T(1,128)S(1)} %bitcast.67), kind=kOutput, calls=%fused_computation.7 | convolution fusion | flops 283299840 | bytes 11227648 | tf_op jit(solution)/shard_map/dot_general | solution.py:121
  63.8 11.8 %copy.27 = f32[128,20480]{0,1:T(8,128)} copy(f32[128,20480]{1,0:T(8,128)} %param.13) | data formatting | bytes 20971520 | tf_op args[0]
  75.8 17.4 %gather_fusion = f32[5120,128]{1,0:T(8,128)S(1)} fusion(f32[128,20480]{0,1:T(8,128)} %copy.27, s32[5120]{0:T(1024)S(1)} %broadcast_clamp_fusion), kind=kCustom, calls=%fused_computation | custom fusion | bytes 5263360 | tf_op jit(solution)/shard_map/jit(_take)/gather | solution.py:111
  93.2 2.7 %collective-permute-start.3 = (f32[4,9]{1,0:T(4,128)S(1)}, f32[4,9]{1,0:T(4,128)S(1)}, u32[]{:S(2)}, u32[]{:S(2)}) collective-permute-start(f32[4,9]{1,0:T(4,128)S(1)} %add.298), channel_id=1, source_target_pairs={{0,4},{2,6},{4,0},{6,2},{1,5},{3,7},{5,1},{7,3},{8,12},{10,14},{12... | collective-permute-start | bytes 440 | tf_op jit(solution)/shard_map/ppermute | solution.py:21
  96.0 2.4 %broadcast_select_fusion = f32[128,64,80]{0,2,1:T(8,128)} fusion(f32[128,64,80]{0,2,1:T(8,128)S(1)} %bitcast.58, pred[64,80]{1,0:T(8,128)(4,1)S(1)} %copy.25), kind=kLoop, calls=%fused_computation.11 | loop fusion | flops 655360 | bytes 5248000 | tf_op jit(solution)/shard_map/jit(_take)/select_n | solution.py:111
  100.3 1.9 collective-permute-done.4
  102.1 1.3 collective-permute-start.5
  104.1 2.6 %collective-permute-done.5 = f32[4,9]{1,0:T(4,128)S(1)} collective-permute-done((f32[4,9]{1,0:T(4,128)S(1)}, f32[4,9]{1,0:T(4,128)S(1)}, u32[]{:S(2)}, u32[]{:S(2)}) %collective-permute-start.5) | collective-permute-done | bytes 176 | tf_op jit(solution)/shard_map/ppermute | solution.py:21
  106.7 1.4 collective-permute-start.6
  108.1 2.0 pad.12
  110.1 4.2 %collective-permute-done.6 = f32[4,9]{1,0:T(4,128)S(1)} collective-permute-done((f32[4,9]{1,0:T(4,128)S(1)}, f32[4,9]{1,0:T(4,128)S(1)}, u32[]{:S(2)}, u32[]{:S(2)}) %collective-permute-start.6) | collective-permute-done | bytes 176 | tf_op jit(solution)/shard_map/ppermute | solution.py:21
  143.6 13.1 %convolution_subtract_fusion = f32[128,512]{1,0:T(8,128)S(1)} fusion(f32[128,5632]{0,1:T(8,128)S(1)} %bitcast.57, f32[5632,512]{1,0:T(8,128)} %all-gather.2.cloned.1.call-done, f32[512]{0:T(512)S(1)} %copy-done.5, f32[128]{0:T(128)S(1)} %get-tuple-element.28), kind=kOutput, calls=%fused_computation.12 | convolution fusion | flops 4429316096 | bytes 14682624 | tf_op jit(solution)/shard_map/dot_general | solution.py:158
  157.0 1.3 slice.456
  162.5 4.6 %all-to-all-start.2 = ((f32[32,4,16]{2,1,0:T(4,128)}), f32[32,4,16]{2,1,0:T(4,128)S(1)}, u32[]{:S(2)}, u32[]{:S(2)}) async-start(f32[32,4,16]{2,1,0:T(4,128)} %copy.31), calls=%async_computation.2 | async-start | bytes 131072 | tf_op jit(solution)/shard_map/all_to_all | solution.py:31
  167.5 9.6 %all-to-all-done.2 = f32[32,4,16]{2,1,0:T(4,128)S(1)} async-done(((f32[32,4,16]{2,1,0:T(4,128)}), f32[32,4,16]{2,1,0:T(4,128)S(1)}, u32[]{:S(2)}, u32[]{:S(2)}) %all-to-all-start.2) | async-done | bytes 8224 | tf_op jit(solution)/shard_map/all_to_all | solution.py:31
  177.8 3.9 %all-to-all-start.3 = ((f32[32,4,16]{2,1,0:T(4,128)}), f32[32,4,16]{2,1,0:T(4,128)S(1)}, u32[]{:S(2)}, u32[]{:S(2)}) async-start(f32[32,4,16]{2,1,0:T(4,128)} %broadcast_in_dim.106), calls=%async_computation.3 | async-start | bytes 131072 | tf_op jit(solution)/shard_map/all_to_all | solution.py:33
  182.7 9.0 %all-to-all-done.3 = f32[32,4,16]{2,1,0:T(4,128)S(1)} async-done(((f32[32,4,16]{2,1,0:T(4,128)}), f32[32,4,16]{2,1,0:T(4,128)S(1)}, u32[]{:S(2)}, u32[]{:S(2)}) %all-to-all-start.3) | async-done | bytes 8224 | tf_op jit(solution)/shard_map/all_to_all | solution.py:33
  (113 shorter events, 20.9 us)
Async XLA Ops:
  7.2 0.8 copy-start
  7.2 7.9 %copy-start.7 = (s32[20]{0:T(128)S(1)}, s32[20]{0:T(128)}, u32[]{:S(2)}) copy-start(s32[20]{0:T(128)} %param.17) | copy-start | bytes 244
  7.2 7.9 %copy-start.8 = (s32[20]{0:T(128)S(1)}, s32[20]{0:T(128)}, u32[]{:S(2)}) copy-start(s32[20]{0:T(128)} %param.16) | copy-start | bytes 244
  7.2 8.0 %copy-start.2 = (f32[20,2048]{1,0:T(8,128)S(1)}, f32[20,2048]{1,0:T(8,128)}, u32[]{:S(2)}) copy-start(f32[20,2048]{1,0:T(8,128)} %param.14) | copy-start | bytes 491524
  14.7 36.5 %copy-start.6 = (s32[4,2]{0,1:T(2,128)S(1)}, s32[4,2]{0,1:T(2,128)}, u32[]{:S(2)}) copy-start(s32[4,2]{0,1:T(2,128)} %param.21) | copy-start | bytes 100
  14.9 37.2 %copy-start.3 = (f32[20480]{0:T(1024)S(1)}, f32[20480]{0:T(1024)}, u32[]{:S(2)}) copy-start(f32[20480]{0:T(1024)} %param.18) | copy-start | bytes 245764
  15.0 8.2 %collective-permute-start = (f32[4,10240]{1,0:T(4,128)S(1)}, f32[4,10240]{1,0:T(4,128)S(1)}, u32[]{:S(2)}, u32[]{:S(2)}) collective-permute-start(f32[4,10240]{1,0:T(4,128)S(1)} %slice_select_fusion), channel_id=1, source_target_pairs={{0,1},{1,0},{2,3},{3,2},{4,5},{5,4},{6,7},{7,6},{8,9},{9,8},{10,11... | collective-permute-start | bytes 491528 | tf_op jit(solution)/shard_map/ppermute | solution.py:42
  17.6 11.0 %all-to-all-start = ((f32[20,4,512]{2,0,1:T(8,128)}), f32[20,4,512]{2,0,1:T(8,128)S(1)}, u32[]{:S(2)}, u32[]{:S(2)}) async-start(f32[20,4,512]{2,0,1:T(8,128)} %copy.28), calls=%async_computation | async-start | bytes 393216 | tf_op jit(solution)/shard_map/all_to_all | solution.py:104
  28.6 21.7 %all-to-all-start.1 = ((f32[32,4,320]{2,1,0:T(4,128)}), f32[32,4,320]{2,1,0:T(4,128)S(1)}, u32[]{:S(2)}, u32[]{:S(2)}) async-start(f32[32,4,320]{2,1,0:T(4,128)} %bitcast.55), calls=%async_computation.1 | async-start | bytes 393216 | tf_op jit(solution)/shard_map/all_to_all | solution.py:47
  39.1 104.5 %all-gather.2.cloned.1.call-start = ((), (), s32[]{:S(2)}) async-start(), calls=%async_computation.4 | async-start | bytes 11714560 | tf_op jit(solution)/shard_map/all_gather | solution.py:106
  52.1 11.0 %copy-start.4 = (s32[5120]{0:T(1024)S(1)}, s32[5120]{0:T(1024)}, u32[]{:S(2)}) copy-start(s32[5120]{0:T(1024)} %param.15) | copy-start | bytes 61444
  63.1 12.4 %collective-permute-start.1 = (f32[4,9]{1,0:T(4,128)S(1)}, f32[4,9]{1,0:T(4,128)S(1)}, u32[]{:S(2)}, u32[]{:S(2)}) collective-permute-start(f32[4,9]{1,0:T(4,128)S(1)} %fusion.9), channel_id=1, source_target_pairs={{0,1},{1,0},{2,3},{3,2},{4,5},{5,4},{6,7},{7,6},{8,9},{9,8},{10,11... | collective-permute-start | bytes 440 | tf_op jit(solution)/shard_map/ppermute | solution.py:21
  75.6 17.6 %collective-permute-start.2 = (f32[4,9]{1,0:T(4,128)S(1)}, f32[4,9]{1,0:T(4,128)S(1)}, u32[]{:S(2)}, u32[]{:S(2)}) collective-permute-start(f32[4,9]{1,0:T(4,128)S(1)} %add.297), channel_id=1, source_target_pairs={{0,2},{2,0},{4,6},{6,4},{1,3},{3,1},{5,7},{7,5},{8,10},{10,8},{12,... | collective-permute-start | bytes 440 | tf_op jit(solution)/shard_map/ppermute | solution.py:21
  93.2 6.4 %copy-start.1 = (f32[4]{0:T(128)S(1)}, f32[4]{0:T(128)}, u32[]{:S(2)}) copy-start(f32[4]{0:T(128)} %param.24) | copy-start | bytes 52
  93.2 5.3 %collective-permute-start.3 = (f32[4,9]{1,0:T(4,128)S(1)}, f32[4,9]{1,0:T(4,128)S(1)}, u32[]{:S(2)}, u32[]{:S(2)}) collective-permute-start(f32[4,9]{1,0:T(4,128)S(1)} %add.298), channel_id=1, source_target_pairs={{0,4},{2,6},{4,0},{6,2},{1,5},{3,7},{5,1},{7,3},{8,12},{10,14},{12... | collective-permute-start | bytes 440 | tf_op jit(solution)/shard_map/ppermute | solution.py:21
  96.0 12.1 %copy-start.9 = (s32[64]{0:T(128)S(1)}, s32[64]{0:T(128)}, u32[]{:S(2)}) copy-start(s32[64]{0:T(128)} %constant.137) | copy-start | bytes 772
  98.5 3.6 %collective-permute-start.4 = (f32[4,9]{1,0:T(4,128)S(1)}, f32[4,9]{1,0:T(4,128)S(1)}, u32[]{:S(2)}, u32[]{:S(2)}) collective-permute-start(f32[4,9]{1,0:T(4,128)S(1)} %add.299), channel_id=1, source_target_pairs={{0,8},{8,0},{16,24},{24,16},{32,40},{40,32},{48,56},{56,48},{1,9},... | collective-permute-start | bytes 440 | tf_op jit(solution)/shard_map/ppermute | solution.py:21
  102.1 4.6 %collective-permute-start.5 = (f32[4,9]{1,0:T(4,128)S(1)}, f32[4,9]{1,0:T(4,128)S(1)}, u32[]{:S(2)}, u32[]{:S(2)}) collective-permute-start(f32[4,9]{1,0:T(4,128)S(1)} %add.300), channel_id=1, source_target_pairs={{0,16},{8,24},{16,0},{24,8},{32,48},{40,56},{48,32},{56,40},{1,17}... | collective-permute-start | bytes 440 | tf_op jit(solution)/shard_map/ppermute | solution.py:21
  106.7 7.6 %collective-permute-start.6 = (f32[4,9]{1,0:T(4,128)S(1)}, f32[4,9]{1,0:T(4,128)S(1)}, u32[]{:S(2)}, u32[]{:S(2)}) collective-permute-start(f32[4,9]{1,0:T(4,128)S(1)} %add.301), channel_id=1, source_target_pairs={{0,32},{8,40},{16,48},{24,56},{32,0},{40,8},{48,16},{56,24},{1,33}... | collective-permute-start | bytes 440 | tf_op jit(solution)/shard_map/ppermute | solution.py:21
  108.1 35.5 %copy-start.5 = (f32[512]{0:T(512)S(1)}, f32[512]{0:T(512)}, u32[]{:S(2)}) copy-start(f32[512]{0:T(512)} %param.19) | copy-start | bytes 6148
  157.0 4.7 %collective-permute-start.7 = (f32[4,512]{1,0:T(4,128)S(1)}, f32[4,512]{1,0:T(4,128)S(1)}, u32[]{:S(2)}, u32[]{:S(2)}) collective-permute-start(f32[4,512]{1,0:T(4,128)S(1)} %fusion.7), channel_id=1, source_target_pairs={{0,1},{1,0},{2,3},{3,2},{4,5},{5,4},{6,7},{7,6},{8,9},{9,8},{10,11... | collective-permute-start | bytes 24584 | tf_op jit(solution)/shard_map/ppermute | solution.py:26
  162.5 14.6 %all-to-all-start.2 = ((f32[32,4,16]{2,1,0:T(4,128)}), f32[32,4,16]{2,1,0:T(4,128)S(1)}, u32[]{:S(2)}, u32[]{:S(2)}) async-start(f32[32,4,16]{2,1,0:T(4,128)} %copy.31), calls=%async_computation.2 | async-start | bytes 131072 | tf_op jit(solution)/shard_map/all_to_all | solution.py:31
  177.8 13.9 %all-to-all-start.3 = ((f32[32,4,16]{2,1,0:T(4,128)}), f32[32,4,16]{2,1,0:T(4,128)S(1)}, u32[]{:S(2)}, u32[]{:S(2)}) async-start(f32[32,4,16]{2,1,0:T(4,128)} %broadcast_in_dim.106), calls=%async_computation.3 | async-start | bytes 131072 | tf_op jit(solution)/shard_map/all_to_all | solution.py:33
Sparse Core Ops, SparseCore 0:
  51.3 81.6 all-gather.1

commit v7 on v5

--- a/solution.py
+++ b/solution.py
@@ -23,7 +23,7 @@
 
 
 def line_scatter(x):
-    for axis, step in STAGES:
+    for axis, step in STAGES[1:]:
         size = lax.axis_size(axis)
         upper = (lax.axis_index(axis) // step) % 2 == 1
         half = x.shape[1] // 2
@@ -34,17 +34,14 @@
 
 
 def piece_order(sizes):
-    line_0, line_1, line_2 = sizes
-    slice_of = []
-    for i in range(line_0 * line_1 * line_2):
-        digits = {"line_0": i // (line_1 * line_2), "line_1": (i // line_2) % line_1, "line_2": i % line_2}
+    line_0, line_1 = sizes
+    owner_of = [0] * (line_0 * line_1)
+    for chip in range(len(owner_of)):
+        digits = {"line_0": chip // line_1, "line_1": chip % line_1}
         s = 0
-        for axis, step in STAGES:
+        for axis, step in STAGES[1:]:
             s = s * 2 + (digits[axis] // step) % 2
-        slice_of.append(s)
-    owner_of = [0] * len(slice_of)
-    for i, s in enumerate(slice_of):
-        owner_of[s] = i
+        owner_of[s] = chip
     return owner_of
 
 
@@ -152,8 +149,9 @@
     row_base = line_total(jnp.dot(pick, base, precision=HI))
 
     pieces = everyone.reshape(line_count, block_units + extra_rows, block_width)[:, block_units:]
-    pieces = pieces.reshape(line_count, -1)[:, : NC * piece_width].reshape(line_count, NC, piece_width)
-    pieces = jnp.take(pieces, jnp.array(piece_order([lax.axis_size(a) for a in LINE])), axis=0)
+    pieces = pieces.reshape(line_count, -1)[:, : NC * piece_width].reshape(-1, 2, NC, piece_width)
+    pieces = pieces[:, 0] + pieces[:, 1]
+    pieces = jnp.take(pieces, jnp.array(piece_order([lax.axis_size(a) for a in LINE[:2]])), axis=0)
     all_rows = pieces.transpose(1, 0, 2).reshape(NC, buses)
 
     sens_list = []

time: 190 us -> 190 us (level)
    ppermute x6 -> x5, waiting for transfers between devices: 10.6 us -> 11.4 us  [line_scatter(): x = keep + lax.ppermute(give, axis, [(i, i ^ step) for i in range(size)])]
    ppermute x6 -> x5, starting transfers between devices: 15.8 us -> 15.9 us  [line_scatter(): x = keep + lax.ppermute(give, axis, [(i, i ^ step) for i in range(size)])]
  transfers between devices with their start and end apart: 20 -> 19, of which waited for: 13 -> 12; matrix products, arithmetic and copies ran while one was open for 32% -> 31% of each run, Pallas kernels for 0% -> 0%
where the time goes in v7:
time: 190 us; the launch traced here: 188 us
  local copies, waits for them, and re-layouts  48.3 us (25%)
  starting transfers between devices  42.2 us (22%)
  between operations  39 us (21%)
  waiting for transfers between devices  25.7 us (14%)
  matrix products  24.4 us (13%)
  other arithmetic  8.8 us (5%)
    ppermute x12, starting transfers between devices, line_total(): x = x + lax.ppermute(x, axis, [(i, i ^ step) for i in range(size)])  21.5 us
    gather x1, local copies, waits for them, and re-layouts, body(): jnp.take(ptdf_rows, order_ids, axis=1)  17.4 us
    ppermute x5, starting transfers between devices, line_scatter(): x = keep + lax.ppermute(give, axis, [(i, i ^ step) for i in range(size)])  15.9 us
    ppermute x12, waiting for transfers between devices, line_total(): x = x + lax.ppermute(x, axis, [(i, i ^ step) for i in range(size)])  14.3 us
    dot_general x1, matrix products, body(): jnp.dot(columns, everyone, preferred_element_type=jnp.float32, precision=HI)  13.1 us
    unnamed x23, local copies, waits for them, and re-layouts  12.6 us
    ppermute x5, waiting for transfers between devices, line_scatter(): x = keep + lax.ppermute(give, axis, [(i, i ^ step) for i in range(size)])  11.4 us
    dot_general x1, matrix products, body(): jnp.dot(ptdf_rows, probes, preferred_element_type=jnp.float32, precision=HI)  10.8 us
  transfers between devices with their start and end apart: 19, of which 12 were waited for; matrix products, arithmetic and copies ran while one was open for 31% of the time, Pallas kernels for 0%

profile of v7, /device:TPU:2, one launch (start us, length us, event | category | flops | bytes accessed | tf_op | source)
XLA Modules:
  0.0 188.5 jit_solution(6239071125857536852)
XLA Ops:
  9.9 4.9 %gather_fusion.3 = f32[4,20480]{1,0:T(4,128)S(1)} fusion(f32[128,20480]{1,0:T(8,128)} %param.13, s32[1024]{0:T(1024)S(1)} %pad_clamp_fusion.1), kind=kCustom, calls=%fused_computation.3 | custom fusion | bytes 655376 | tf_op jit(solution)/shard_map/jit(_take)/gather | solution.py:76
  16.7 4.3 %collective-permute-done = f32[4,10240]{1,0:T(4,128)S(1)} collective-permute-done((f32[4,10240]{1,0:T(4,128)S(1)}, f32[4,10240]{1,0:T(4,128)S(1)}, u32[]{:S(2)}, u32[]{:S(2)}) %collective-permute-start) | collective-permute-done | bytes 163872 | tf_op jit(solution)/shard_map/ppermute | solution.py:32
  21.1 3.3 %collective-permute-start.1 = (f32[4,5120]{1,0:T(4,128)S(1)}, f32[4,5120]{1,0:T(4,128)S(1)}, u32[]{:S(2)}, u32[]{:S(2)}) collective-permute-start(f32[4,5120]{1,0:T(4,128)S(1)} %slice_select_fusion.1), channel_id=1, source_target_pairs={{0,4},{2,6},{4,0},{6,2},{1,5},{3,7},{5,1},{7,3},{8,12},{10,14},{12... | collective-permute-start | bytes 245768 | tf_op jit(solution)/shard_map/ppermute | solution.py:32
  24.4 2.7 %collective-permute-done.1 = f32[4,5120]{1,0:T(4,128)S(1)} collective-permute-done((f32[4,5120]{1,0:T(4,128)S(1)}, f32[4,5120]{1,0:T(4,128)S(1)}, u32[]{:S(2)}, u32[]{:S(2)}) %collective-permute-start.1) | collective-permute-done | bytes 81952 | tf_op jit(solution)/shard_map/ppermute | solution.py:32
  27.2 2.0 %collective-permute-start.2 = (f32[4,2560]{1,0:T(4,128)S(1)}, f32[4,2560]{1,0:T(4,128)S(1)}, u32[]{:S(2)}, u32[]{:S(2)}) collective-permute-start(f32[4,2560]{1,0:T(4,128)S(1)} %slice_select_fusion.2), channel_id=1, source_target_pairs={{0,8},{8,0},{16,24},{24,16},{32,40},{40,32},{48,56},{56,48},{1,9},... | collective-permute-start | bytes 122888 | tf_op jit(solution)/shard_map/ppermute | solution.py:32
  29.2 2.0 %collective-permute-done.2 = f32[4,2560]{1,0:T(4,128)S(1)} collective-permute-done((f32[4,2560]{1,0:T(4,128)S(1)}, f32[4,2560]{1,0:T(4,128)S(1)}, u32[]{:S(2)}, u32[]{:S(2)}) %collective-permute-start.2) | collective-permute-done | bytes 40992 | tf_op jit(solution)/shard_map/ppermute | solution.py:32
  31.3 3.6 %collective-permute-start.3 = (f32[4,1280]{1,0:T(4,128)S(1)}, f32[4,1280]{1,0:T(4,128)S(1)}, u32[]{:S(2)}, u32[]{:S(2)}) collective-permute-start(f32[4,1280]{1,0:T(4,128)S(1)} %slice_select_fusion.3), channel_id=1, source_target_pairs={{0,16},{8,24},{16,0},{24,8},{32,48},{40,56},{48,32},{56,40},{1,17}... | collective-permute-start | bytes 61448 | tf_op jit(solution)/shard_map/ppermute | solution.py:32
  37.3 4.8 %all-to-all-start = ((f32[20,4,512]{2,0,1:T(8,128)}), f32[20,4,512]{2,0,1:T(8,128)S(1)}, u32[]{:S(2)}, u32[]{:S(2)}) async-start(f32[20,4,512]{2,0,1:T(8,128)} %copy.37), calls=%async_computation | async-start | bytes 393216 | tf_op jit(solution)/shard_map/all_to_all | solution.py:93
  42.2 5.4 %collective-permute-start.4 = (f32[4,640]{1,0:T(4,128)S(1)}, f32[4,640]{1,0:T(4,128)S(1)}, u32[]{:S(2)}, u32[]{:S(2)}) collective-permute-start(f32[4,640]{1,0:T(4,128)S(1)} %slice_select_fusion.4), channel_id=1, source_target_pairs={{0,32},{8,40},{16,48},{24,56},{32,0},{40,8},{48,16},{56,24},{1,33}... | collective-permute-start | bytes 30728 | tf_op jit(solution)/shard_map/ppermute | solution.py:32
  47.6 2.2 %collective-permute-done.4 = f32[4,640]{1,0:T(4,128)S(1)} collective-permute-done((f32[4,640]{1,0:T(4,128)S(1)}, f32[4,640]{1,0:T(4,128)S(1)}, u32[]{:S(2)}, u32[]{:S(2)}) %collective-permute-start.4) | collective-permute-done | bytes 10272 | tf_op jit(solution)/shard_map/ppermute | solution.py:32
  51.5 10.8 %fusion = f32[9,128]{1,0:T(8,128)S(1)} fusion(f32[128,20480]{1,0:T(8,128)} %param.13, f32[20480,8]{0,1:T(8,128)S(1)} %fusion.4, f32[20480,1]{0,1:T(1,128)S(1)} %bitcast.85), kind=kOutput, calls=%fused_computation.7 | convolution fusion | flops 283299840 | bytes 11227648 | tf_op jit(solution)/shard_map/dot_general | solution.py:110
  65.3 11.8 %copy.36 = f32[128,20480]{0,1:T(8,128)} copy(f32[128,20480]{1,0:T(8,128)} %param.13) | data formatting | bytes 20971520 | tf_op args[0]
  77.1 3.0 %collective-permute-start.7 = (f32[4,9]{1,0:T(4,128)S(1)}, f32[4,9]{1,0:T(4,128)S(1)}, u32[]{:S(2)}, u32[]{:S(2)}) collective-permute-start(f32[4,9]{1,0:T(4,128)S(1)} %add.361), channel_id=1, source_target_pairs={{0,4},{2,6},{4,0},{6,2},{1,5},{3,7},{5,1},{7,3},{8,12},{10,14},{12... | collective-permute-start | bytes 440 | tf_op jit(solution)/shard_map/ppermute | solution.py:21
  80.2 17.4 %gather_fusion = f32[5120,128]{1,0:T(8,128)S(1)} fusion(f32[128,20480]{0,1:T(8,128)} %copy.36, s32[5120]{0:T(1024)S(1)} %broadcast_clamp_fusion), kind=kCustom, calls=%fused_computation | custom fusion | bytes 5263360 | tf_op jit(solution)/shard_map/jit(_take)/gather | solution.py:100
  99.4 2.5 %broadcast_select_fusion = f32[128,64,80]{0,2,1:T(8,128)} fusion(f32[128,64,80]{0,2,1:T(8,128)S(1)} %bitcast.73, pred[64,80]{1,0:T(8,128)(4,1)S(1)} %copy.34), kind=kLoop, calls=%fused_computation.11 | loop fusion | flops 655360 | bytes 5248000 | tf_op jit(solution)/shard_map/jit(_take)/select_n | solution.py:100
  102.7 3.8 %collective-permute-done.9 = f32[4,9]{1,0:T(4,128)S(1)} collective-permute-done((f32[4,9]{1,0:T(4,128)S(1)}, f32[4,9]{1,0:T(4,128)S(1)}, u32[]{:S(2)}, u32[]{:S(2)}) %collective-permute-start.9) | collective-permute-done | bytes 176 | tf_op jit(solution)/shard_map/ppermute | solution.py:21
  106.5 4.9 %collective-permute-start.10 = (f32[4,9]{1,0:T(4,128)S(1)}, f32[4,9]{1,0:T(4,128)S(1)}, u32[]{:S(2)}, u32[]{:S(2)}) collective-permute-start(f32[4,9]{1,0:T(4,128)S(1)} %add.364), channel_id=1, source_target_pairs={{0,32},{8,40},{16,48},{24,56},{32,0},{40,8},{48,16},{56,24},{1,33}... | collective-permute-start | bytes 440 | tf_op jit(solution)/shard_map/ppermute | solution.py:21
  112.0 1.9 %pad.12 = f32[128,64,88]{0,2,1:T(8,128)S(1)} pad(f32[128,64,80]{0,2,1:T(8,128)} %broadcast_select_fusion, f32[]{:T(128)} %constant.152.clone.1), padding=0_0x0_0x0_8 | pad | bytes 5505028 | tf_op jit(solution)/shard_map/jit(_pad)/pad | solution.py:101
  139.7 13.1 %convolution_subtract_fusion = f32[128,512]{1,0:T(8,128)S(1)} fusion(f32[128,5632]{0,1:T(8,128)S(1)} %bitcast.72, f32[5632,512]{1,0:T(8,128)} %all-gather.2.cloned.1.call-done, f32[512]{0:T(512)S(1)} %copy-done.5, f32[128]{0:T(128)S(1)} %get-tuple-element.25), kind=kOutput, calls=%fused_computation.12 | convolution fusion | flops 4429316096 | bytes 14682624 | tf_op jit(solution)/shard_map/dot_general | solution.py:147
  159.8 2.0 %collective-permute-start.13 = (f32[4,512]{1,0:T(4,128)S(1)}, f32[4,512]{1,0:T(4,128)S(1)}, u32[]{:S(2)}, u32[]{:S(2)}) collective-permute-start(f32[4,512]{1,0:T(4,128)S(1)} %add.368), channel_id=1, source_target_pairs={{0,4},{2,6},{4,0},{6,2},{1,5},{3,7},{5,1},{7,3},{8,12},{10,14},{12... | collective-permute-start | bytes 24584 | tf_op jit(solution)/shard_map/ppermute | solution.py:21
  162.7 2.3 %collective-permute-done.13 = f32[4,512]{1,0:T(4,128)S(1)} collective-permute-done((f32[4,512]{1,0:T(4,128)S(1)}, f32[4,512]{1,0:T(4,128)S(1)}, u32[]{:S(2)}, u32[]{:S(2)}) %collective-permute-start.13) | collective-permute-done | bytes 8224 | tf_op jit(solution)/shard_map/ppermute | solution.py:21
  166.5 2.1 %collective-permute-done.14 = f32[4,512]{1,0:T(4,128)S(1)} collective-permute-done((f32[4,512]{1,0:T(4,128)S(1)}, f32[4,512]{1,0:T(4,128)S(1)}, u32[]{:S(2)}, u32[]{:S(2)}) %collective-permute-start.14) | collective-permute-done | bytes 8224 | tf_op jit(solution)/shard_map/ppermute | solution.py:21
  170.6 2.6 %collective-permute-done.15 = f32[4,512]{1,0:T(4,128)S(1)} collective-permute-done((f32[4,512]{1,0:T(4,128)S(1)}, f32[4,512]{1,0:T(4,128)S(1)}, u32[]{:S(2)}, u32[]{:S(2)}) %collective-permute-start.15) | collective-permute-done | bytes 8224 | tf_op jit(solution)/shard_map/ppermute | solution.py:21
  173.2 4.6 %collective-permute-start.16 = (f32[4,512]{1,0:T(4,128)S(1)}, f32[4,512]{1,0:T(4,128)S(1)}, u32[]{:S(2)}, u32[]{:S(2)}) collective-permute-start(f32[4,512]{1,0:T(4,128)S(1)} %add.371), channel_id=1, source_target_pairs={{0,32},{8,40},{16,48},{24,56},{32,0},{40,8},{48,16},{56,24},{1,33}... | collective-permute-start | bytes 24584 | tf_op jit(solution)/shard_map/ppermute | solution.py:21
  (123 shorter events, 31.3 us)
Async XLA Ops:
  8.5 15.9 %copy-start.8 = (s32[20]{0:T(128)S(1)}, s32[20]{0:T(128)}, u32[]{:S(2)}) copy-start(s32[20]{0:T(128)} %param.16) | copy-start | bytes 244
  9.8 25.0 %copy-start.2 = (f32[20,2048]{1,0:T(8,128)S(1)}, f32[20,2048]{1,0:T(8,128)}, u32[]{:S(2)}) copy-start(f32[20,2048]{1,0:T(8,128)} %param.14) | copy-start | bytes 491524
  14.7 35.8 %copy-start.6 = (s32[4,2]{0,1:T(2,128)S(1)}, s32[4,2]{0,1:T(2,128)}, u32[]{:S(2)}) copy-start(s32[4,2]{0,1:T(2,128)} %param.21) | copy-start | bytes 100
  14.9 36.5 %copy-start.3 = (f32[20480]{0:T(1024)S(1)}, f32[20480]{0:T(1024)}, u32[]{:S(2)}) copy-start(f32[20480]{0:T(1024)} %param.18) | copy-start | bytes 245764
  15.0 6.0 %collective-permute-start = (f32[4,10240]{1,0:T(4,128)S(1)}, f32[4,10240]{1,0:T(4,128)S(1)}, u32[]{:S(2)}, u32[]{:S(2)}) collective-permute-start(f32[4,10240]{1,0:T(4,128)S(1)} %slice_select_fusion), channel_id=1, source_target_pairs={{0,2},{2,0},{4,6},{6,4},{1,3},{3,1},{5,7},{7,5},{8,10},{10,8},{12,... | collective-permute-start | bytes 491528 | tf_op jit(solution)/shard_map/ppermute | solution.py:32
  21.1 6.0 %collective-permute-start.1 = (f32[4,5120]{1,0:T(4,128)S(1)}, f32[4,5120]{1,0:T(4,128)S(1)}, u32[]{:S(2)}, u32[]{:S(2)}) collective-permute-start(f32[4,5120]{1,0:T(4,128)S(1)} %slice_select_fusion.1), channel_id=1, source_target_pairs={{0,4},{2,6},{4,0},{6,2},{1,5},{3,7},{5,1},{7,3},{8,12},{10,14},{12... | collective-permute-start | bytes 245768 | tf_op jit(solution)/shard_map/ppermute | solution.py:32
  27.2 4.1 %collective-permute-start.2 = (f32[4,2560]{1,0:T(4,128)S(1)}, f32[4,2560]{1,0:T(4,128)S(1)}, u32[]{:S(2)}, u32[]{:S(2)}) collective-permute-start(f32[4,2560]{1,0:T(4,128)S(1)} %slice_select_fusion.2), channel_id=1, source_target_pairs={{0,8},{8,0},{16,24},{24,16},{32,40},{40,32},{48,56},{56,48},{1,9},... | collective-permute-start | bytes 122888 | tf_op jit(solution)/shard_map/ppermute | solution.py:32
  31.3 10.8 %collective-permute-start.3 = (f32[4,1280]{1,0:T(4,128)S(1)}, f32[4,1280]{1,0:T(4,128)S(1)}, u32[]{:S(2)}, u32[]{:S(2)}) collective-permute-start(f32[4,1280]{1,0:T(4,128)S(1)} %slice_select_fusion.3), channel_id=1, source_target_pairs={{0,16},{8,24},{16,0},{24,8},{32,48},{40,56},{48,32},{56,40},{1,17}... | collective-permute-start | bytes 61448 | tf_op jit(solution)/shard_map/ppermute | solution.py:32
  37.3 10.3 %all-to-all-start = ((f32[20,4,512]{2,0,1:T(8,128)}), f32[20,4,512]{2,0,1:T(8,128)S(1)}, u32[]{:S(2)}, u32[]{:S(2)}) async-start(f32[20,4,512]{2,0,1:T(8,128)} %copy.37), calls=%async_computation | async-start | bytes 393216 | tf_op jit(solution)/shard_map/all_to_all | solution.py:93
  42.1 97.5 %all-gather.2.cloned.1.call-start = ((), (), s32[]{:S(2)}) async-start(), calls=%async_computation.1 | async-start | bytes 11714560 | tf_op jit(solution)/shard_map/all_gather | solution.py:95
  42.2 7.7 %collective-permute-start.4 = (f32[4,640]{1,0:T(4,128)S(1)}, f32[4,640]{1,0:T(4,128)S(1)}, u32[]{:S(2)}, u32[]{:S(2)}) collective-permute-start(f32[4,640]{1,0:T(4,128)S(1)} %slice_select_fusion.4), channel_id=1, source_target_pairs={{0,32},{8,40},{16,48},{24,56},{32,0},{40,8},{48,16},{56,24},{1,33}... | collective-permute-start | bytes 30728 | tf_op jit(solution)/shard_map/ppermute | solution.py:32
  62.5 1.2 collective-permute-start.5
  63.7 13.4 %collective-permute-start.6 = (f32[4,9]{1,0:T(4,128)S(1)}, f32[4,9]{1,0:T(4,128)S(1)}, u32[]{:S(2)}, u32[]{:S(2)}) collective-permute-start(f32[4,9]{1,0:T(4,128)S(1)} %add.360), channel_id=1, source_target_pairs={{0,2},{2,0},{4,6},{6,4},{1,3},{3,1},{5,7},{7,5},{8,10},{10,8},{12,... | collective-permute-start | bytes 440 | tf_op jit(solution)/shard_map/ppermute | solution.py:21
  77.1 20.6 %collective-permute-start.7 = (f32[4,9]{1,0:T(4,128)S(1)}, f32[4,9]{1,0:T(4,128)S(1)}, u32[]{:S(2)}, u32[]{:S(2)}) collective-permute-start(f32[4,9]{1,0:T(4,128)S(1)} %add.361), channel_id=1, source_target_pairs={{0,4},{2,6},{4,0},{6,2},{1,5},{3,7},{5,1},{7,3},{8,12},{10,14},{12... | collective-permute-start | bytes 440 | tf_op jit(solution)/shard_map/ppermute | solution.py:21
  97.7 4.2 %collective-permute-start.8 = (f32[4,9]{1,0:T(4,128)S(1)}, f32[4,9]{1,0:T(4,128)S(1)}, u32[]{:S(2)}, u32[]{:S(2)}) collective-permute-start(f32[4,9]{1,0:T(4,128)S(1)} %add.362), channel_id=1, source_target_pairs={{0,8},{8,0},{16,24},{24,16},{32,40},{40,32},{48,56},{56,48},{1,9},... | collective-permute-start | bytes 440 | tf_op jit(solution)/shard_map/ppermute | solution.py:21
  101.9 4.6 %collective-permute-start.9 = (f32[4,9]{1,0:T(4,128)S(1)}, f32[4,9]{1,0:T(4,128)S(1)}, u32[]{:S(2)}, u32[]{:S(2)}) collective-permute-start(f32[4,9]{1,0:T(4,128)S(1)} %add.363), channel_id=1, source_target_pairs={{0,16},{8,24},{16,0},{24,8},{32,48},{40,56},{48,32},{56,40},{1,17}... | collective-permute-start | bytes 440 | tf_op jit(solution)/shard_map/ppermute | solution.py:21
  102.7 37.0 %copy-start.5 = (f32[512]{0:T(512)S(1)}, f32[512]{0:T(512)}, u32[]{:S(2)}) copy-start(f32[512]{0:T(512)} %param.19) | copy-start | bytes 6148
  106.5 7.6 %collective-permute-start.10 = (f32[4,9]{1,0:T(4,128)S(1)}, f32[4,9]{1,0:T(4,128)S(1)}, u32[]{:S(2)}, u32[]{:S(2)}) collective-permute-start(f32[4,9]{1,0:T(4,128)S(1)} %add.364), channel_id=1, source_target_pairs={{0,32},{8,40},{16,48},{24,56},{32,0},{40,8},{48,16},{56,24},{1,33}... | collective-permute-start | bytes 440 | tf_op jit(solution)/shard_map/ppermute | solution.py:21
  153.1 1.2 collective-permute-start.11
  154.3 5.5 %collective-permute-start.12 = (f32[4,512]{1,0:T(4,128)S(1)}, f32[4,512]{1,0:T(4,128)S(1)}, u32[]{:S(2)}, u32[]{:S(2)}) collective-permute-start(f32[4,512]{1,0:T(4,128)S(1)} %add.367), channel_id=1, source_target_pairs={{0,2},{2,0},{4,6},{6,4},{1,3},{3,1},{5,7},{7,5},{8,10},{10,8},{12,... | collective-permute-start | bytes 24584 | tf_op jit(solution)/shard_map/ppermute | solution.py:21
  159.8 5.2 %collective-permute-start.13 = (f32[4,512]{1,0:T(4,128)S(1)}, f32[4,512]{1,0:T(4,128)S(1)}, u32[]{:S(2)}, u32[]{:S(2)}) collective-permute-start(f32[4,512]{1,0:T(4,128)S(1)} %add.368), channel_id=1, source_target_pairs={{0,4},{2,6},{4,0},{6,2},{1,5},{3,7},{5,1},{7,3},{8,12},{10,14},{12... | collective-permute-start | bytes 24584 | tf_op jit(solution)/shard_map/ppermute | solution.py:21
  165.0 3.7 %collective-permute-start.14 = (f32[4,512]{1,0:T(4,128)S(1)}, f32[4,512]{1,0:T(4,128)S(1)}, u32[]{:S(2)}, u32[]{:S(2)}) collective-permute-start(f32[4,512]{1,0:T(4,128)S(1)} %add.369), channel_id=1, source_target_pairs={{0,8},{8,0},{16,24},{24,16},{32,40},{40,32},{48,56},{56,48},{1,9},... | collective-permute-start | bytes 24584 | tf_op jit(solution)/shard_map/ppermute | solution.py:21
  168.7 4.5 %collective-permute-start.15 = (f32[4,512]{1,0:T(4,128)S(1)}, f32[4,512]{1,0:T(4,128)S(1)}, u32[]{:S(2)}, u32[]{:S(2)}) collective-permute-start(f32[4,512]{1,0:T(4,128)S(1)} %add.370), channel_id=1, source_target_pairs={{0,16},{8,24},{16,0},{24,8},{32,48},{40,56},{48,32},{56,40},{1,17}... | collective-permute-start | bytes 24584 | tf_op jit(solution)/shard_map/ppermute | solution.py:21
  173.2 7.6 %collective-permute-start.16 = (f32[4,512]{1,0:T(4,128)S(1)}, f32[4,512]{1,0:T(4,128)S(1)}, u32[]{:S(2)}, u32[]{:S(2)}) collective-permute-start(f32[4,512]{1,0:T(4,128)S(1)} %add.371), channel_id=1, source_target_pairs={{0,32},{8,40},{16,48},{24,56},{32,0},{40,8},{48,16},{56,24},{1,33}... | collective-permute-start | bytes 24584 | tf_op jit(solution)/shard_map/ppermute | solution.py:21
  (5 other events, 39.3 us)
Sparse Core Ops, SparseCore 0:
  50.7 88.8 all-gather.1

commit v8 on v7

--- a/solution.py
+++ b/solution.py
@@ -10,6 +10,7 @@
 SNAP_LINE = ("snap", "line_0", "line_1", "line_2")
 HI = lax.Precision.HIGHEST
 STAGES = (("line_2", 1), ("line_1", 1), ("line_1", 2), ("line_0", 1), ("line_0", 2), ("line_0", 4))
+SCATTER = STAGES[1:5]
 
 
 ramp_gain = 0.5
@@ -23,7 +24,7 @@
 
 
 def line_scatter(x):
-    for axis, step in STAGES[1:]:
+    for axis, step in SCATTER:
         size = lax.axis_size(axis)
         upper = (lax.axis_index(axis) // step) % 2 == 1
         half = x.shape[1] // 2
@@ -34,14 +35,14 @@
 
 
 def piece_order(sizes):
-    line_0, line_1 = sizes
-    owner_of = [0] * (line_0 * line_1)
-    for chip in range(len(owner_of)):
-        digits = {"line_0": chip // line_1, "line_1": chip % line_1}
+    near_0, line_1 = sizes
+    owner_of = [0] * (near_0 * line_1)
+    for group in range(len(owner_of)):
+        digits = {"line_0": group // line_1, "line_1": group % line_1}
         s = 0
-        for axis, step in STAGES[1:]:
+        for axis, step in SCATTER:
             s = s * 2 + (digits[axis] // step) % 2
-        owner_of[s] = chip
+        owner_of[s] = group
     return owner_of
 
 
@@ -149,9 +150,11 @@
     row_base = line_total(jnp.dot(pick, base, precision=HI))
 
     pieces = everyone.reshape(line_count, block_units + extra_rows, block_width)[:, block_units:]
-    pieces = pieces.reshape(line_count, -1)[:, : NC * piece_width].reshape(-1, 2, NC, piece_width)
-    pieces = pieces[:, 0] + pieces[:, 1]
-    pieces = jnp.take(pieces, jnp.array(piece_order([lax.axis_size(a) for a in LINE[:2]])), axis=0)
+    line_0, line_1, line_2 = (lax.axis_size(a) for a in LINE)
+    pieces = pieces.reshape(line_count, -1)[:, : NC * piece_width]
+    pieces = pieces.reshape(2, line_0 // 2, line_1, line_2, NC, piece_width).sum(axis=(0, 3))
+    pieces = pieces.reshape(-1, NC, piece_width)
+    pieces = jnp.take(pieces, jnp.array(piece_order([line_0 // 2, line_1])), axis=0)
     all_rows = pieces.transpose(1, 0, 2).reshape(NC, buses)
 
     sens_list = []

time: 190 us -> 187 us (0.984)
  starting transfers between devices: 42.2 us -> 37.4 us
  local copies, waits for them, and re-layouts: 48.3 us -> 50.3 us
    ppermute x5 -> x4, starting transfers between devices: 15.9 us -> 10.3 us  [line_scatter(): x = keep + lax.ppermute(give, axis, [(i, i ^ step) for i in range(size)])]
    ppermute x5 -> x4, waiting for transfers between devices: 11.4 us -> 7.32 us  [line_scatter(): x = keep + lax.ppermute(give, axis, [(i, i ^ step) for i in range(size)])]
  transfers between devices with their start and end apart: 19 -> 18, of which waited for: 12 -> 13; matrix products, arithmetic and copies ran while one was open for 31% -> 33% of each run, Pallas kernels for 0% -> 0%
where the time goes in v8:
time: 187 us; the launch traced here: 186 us
  local copies, waits for them, and re-layouts  50.3 us (27%)
  between operations  39.4 us (21%)
  starting transfers between devices  37.4 us (20%)
  matrix products  25.3 us (14%)
  waiting for transfers between devices  24.5 us (13%)
  other arithmetic  9.08 us (5%)
    ppermute x12, starting transfers between devices, line_total(): x = x + lax.ppermute(x, axis, [(i, i ^ step) for i in range(size)])  22.3 us
    gather x1, local copies, waits for them, and re-layouts, body(): jnp.take(ptdf_rows, order_ids, axis=1)  17.4 us
    ppermute x12, waiting for transfers between devices, line_total(): x = x + lax.ppermute(x, axis, [(i, i ^ step) for i in range(size)])  14.8 us
    dot_general x1, matrix products, body(): jnp.dot(columns, everyone, preferred_element_type=jnp.float32, precision=HI)  14.1 us
    unnamed x23, local copies, waits for them, and re-layouts  13.2 us
    dot_general x1, matrix products, body(): jnp.dot(ptdf_rows, probes, preferred_element_type=jnp.float32, precision=HI)  10.8 us
    ppermute x4, starting transfers between devices, line_scatter(): x = keep + lax.ppermute(give, axis, [(i, i ^ step) for i in range(size)])  10.3 us
    ppermute x4, waiting for transfers between devices, line_scatter(): x = keep + lax.ppermute(give, axis, [(i, i ^ step) for i in range(size)])  7.32 us
  transfers between devices with their start and end apart: 18, of which 13 were waited for; matrix products, arithmetic and copies ran while one was open for 33% of the time, Pallas kernels for 0%

profile of v8, /device:TPU:2, one launch (start us, length us, event | category | flops | bytes accessed | tf_op | source)
XLA Modules:
  0.0 185.9 jit_solution(1465410946706462647)
XLA Ops:
  9.9 4.9 %gather_fusion.3 = f32[4,20480]{1,0:T(4,128)S(1)} fusion(f32[128,20480]{1,0:T(8,128)} %param.13, s32[1024]{0:T(1024)S(1)} %pad_clamp_fusion.1), kind=kCustom, calls=%fused_computation.3 | custom fusion | bytes 655376 | tf_op jit(solution)/shard_map/jit(_take)/gather | solution.py:77
  15.0 1.7 collective-permute-start
  16.7 4.3 %collective-permute-done = f32[4,10240]{1,0:T(4,128)S(1)} collective-permute-done((f32[4,10240]{1,0:T(4,128)S(1)}, f32[4,10240]{1,0:T(4,128)S(1)}, u32[]{:S(2)}, u32[]{:S(2)}) %collective-permute-start) | collective-permute-done | bytes 163872 | tf_op jit(solution)/shard_map/ppermute | solution.py:33
  21.1 3.3 %collective-permute-start.1 = (f32[4,5120]{1,0:T(4,128)S(1)}, f32[4,5120]{1,0:T(4,128)S(1)}, u32[]{:S(2)}, u32[]{:S(2)}) collective-permute-start(f32[4,5120]{1,0:T(4,128)S(1)} %slice_select_fusion.1), channel_id=1, source_target_pairs={{0,4},{2,6},{4,0},{6,2},{1,5},{3,7},{5,1},{7,3},{8,12},{10,14},{12... | collective-permute-start | bytes 245768 | tf_op jit(solution)/shard_map/ppermute | solution.py:33
  24.4 2.7 %collective-permute-done.1 = f32[4,5120]{1,0:T(4,128)S(1)} collective-permute-done((f32[4,5120]{1,0:T(4,128)S(1)}, f32[4,5120]{1,0:T(4,128)S(1)}, u32[]{:S(2)}, u32[]{:S(2)}) %collective-permute-start.1) | collective-permute-done | bytes 81952 | tf_op jit(solution)/shard_map/ppermute | solution.py:33
  27.2 2.0 %collective-permute-start.2 = (f32[4,2560]{1,0:T(4,128)S(1)}, f32[4,2560]{1,0:T(4,128)S(1)}, u32[]{:S(2)}, u32[]{:S(2)}) collective-permute-start(f32[4,2560]{1,0:T(4,128)S(1)} %slice_select_fusion.2), channel_id=1, source_target_pairs={{0,8},{8,0},{16,24},{24,16},{32,40},{40,32},{48,56},{56,48},{1,9},... | collective-permute-start | bytes 122888 | tf_op jit(solution)/shard_map/ppermute | solution.py:33
  31.6 4.8 %all-to-all-start = ((f32[20,4,512]{2,0,1:T(8,128)}), f32[20,4,512]{2,0,1:T(8,128)S(1)}, u32[]{:S(2)}, u32[]{:S(2)}) async-start(f32[20,4,512]{2,0,1:T(8,128)} %copy.28), calls=%async_computation | async-start | bytes 393216 | tf_op jit(solution)/shard_map/all_to_all | solution.py:94
  36.5 3.4 %collective-permute-start.3 = (f32[4,1280]{1,0:T(4,128)S(1)}, f32[4,1280]{1,0:T(4,128)S(1)}, u32[]{:S(2)}, u32[]{:S(2)}) collective-permute-start(f32[4,1280]{1,0:T(4,128)S(1)} %slice_select_fusion.3), channel_id=1, source_target_pairs={{0,16},{8,24},{16,0},{24,8},{32,48},{40,56},{48,32},{56,40},{1,17}... | collective-permute-start | bytes 61448 | tf_op jit(solution)/shard_map/ppermute | solution.py:33
  43.3 10.8 %fusion = f32[9,128]{1,0:T(8,128)S(1)} fusion(f32[128,20480]{1,0:T(8,128)} %param.13, f32[20480,8]{0,1:T(8,128)S(1)} %fusion.4, f32[20480,1]{0,1:T(1,128)S(1)} %bitcast.75), kind=kOutput, calls=%fused_computation.7 | convolution fusion | flops 283299840 | bytes 11227648 | tf_op jit(solution)/shard_map/dot_general | solution.py:111
  57.1 11.8 %copy.27 = f32[128,20480]{0,1:T(8,128)} copy(f32[128,20480]{1,0:T(8,128)} %param.13) | data formatting | bytes 20971520 | tf_op args[0]
  68.9 3.2 %collective-permute-start.6 = (f32[4,9]{1,0:T(4,128)S(1)}, f32[4,9]{1,0:T(4,128)S(1)}, u32[]{:S(2)}, u32[]{:S(2)}) collective-permute-start(f32[4,9]{1,0:T(4,128)S(1)} %add.342), channel_id=1, source_target_pairs={{0,4},{2,6},{4,0},{6,2},{1,5},{3,7},{5,1},{7,3},{8,12},{10,14},{12... | collective-permute-start | bytes 440 | tf_op jit(solution)/shard_map/ppermute | solution.py:22
  72.2 17.4 %gather_fusion = f32[5120,128]{1,0:T(8,128)S(1)} fusion(f32[128,20480]{0,1:T(8,128)} %copy.27, s32[5120]{0:T(1024)S(1)} %broadcast_clamp_fusion), kind=kCustom, calls=%fused_computation | custom fusion | bytes 5263360 | tf_op jit(solution)/shard_map/jit(_take)/gather | solution.py:101
  89.8 2.4 %broadcast_select_fusion = f32[128,64,80]{0,2,1:T(8,128)} fusion(f32[128,64,80]{0,2,1:T(8,128)S(1)} %bitcast.62, pred[64,80]{1,0:T(8,128)(4,1)S(1)} %copy.25), kind=kLoop, calls=%fused_computation.11 | loop fusion | flops 655360 | bytes 5248000 | tf_op jit(solution)/shard_map/jit(_take)/select_n | solution.py:101
  93.3 3.0 %collective-permute-start.8 = (f32[4,9]{1,0:T(4,128)S(1)}, f32[4,9]{1,0:T(4,128)S(1)}, u32[]{:S(2)}, u32[]{:S(2)}) collective-permute-start(f32[4,9]{1,0:T(4,128)S(1)} %add.344), channel_id=1, source_target_pairs={{0,16},{8,24},{16,0},{24,8},{32,48},{40,56},{48,32},{56,40},{1,17}... | collective-permute-start | bytes 440 | tf_op jit(solution)/shard_map/ppermute | solution.py:22
  98.0 6.0 %collective-permute-start.9 = (f32[4,9]{1,0:T(4,128)S(1)}, f32[4,9]{1,0:T(4,128)S(1)}, u32[]{:S(2)}, u32[]{:S(2)}) collective-permute-start(f32[4,9]{1,0:T(4,128)S(1)} %add.345), channel_id=1, source_target_pairs={{0,32},{8,40},{16,48},{24,56},{32,0},{40,8},{48,16},{56,24},{1,33}... | collective-permute-start | bytes 440 | tf_op jit(solution)/shard_map/ppermute | solution.py:22
  104.6 2.2 %pad.12 = f32[128,64,96]{0,2,1:T(8,128)S(1)} pad(f32[128,64,80]{0,2,1:T(8,128)} %broadcast_select_fusion, f32[]{:T(128)} %constant.139.clone.1), padding=0_0x0_0x0_16 | pad | bytes 5767172 | tf_op jit(solution)/shard_map/jit(_pad)/pad | solution.py:102
  133.7 14.1 %convolution_subtract_fusion = f32[128,512]{1,0:T(8,128)S(1)} fusion(f32[128,6144]{0,1:T(8,128)S(1)} %bitcast.61, f32[6144,512]{1,0:T(8,128)} %all-gather.2.cloned.1.call-done, f32[512]{0:T(512)S(1)} %copy-done.5, f32[128]{0:T(128)S(1)} %get-tuple-element.25), kind=kOutput, calls=%fused_computation.12 | convolution fusion | flops 4831969280 | bytes 15993344 | tf_op jit(solution)/shard_map/dot_general | solution.py:148
  149.4 3.5 %collective-permute-done.11 = f32[4,512]{1,0:T(4,128)S(1)} collective-permute-done((f32[4,512]{1,0:T(4,128)S(1)}, f32[4,512]{1,0:T(4,128)S(1)}, u32[]{:S(2)}, u32[]{:S(2)}) %collective-permute-start.11) | collective-permute-done | bytes 8224 | tf_op jit(solution)/shard_map/ppermute | solution.py:22
  157.3 1.9 slice.488
  164.1 2.0 %collective-permute-done.13 = f32[4,512]{1,0:T(4,128)S(1)} collective-permute-done((f32[4,512]{1,0:T(4,128)S(1)}, f32[4,512]{1,0:T(4,128)S(1)}, u32[]{:S(2)}, u32[]{:S(2)}) %collective-permute-start.13) | collective-permute-done | bytes 8224 | tf_op jit(solution)/shard_map/ppermute | solution.py:22
  166.1 1.9 %collective-permute-start.14 = (f32[4,512]{1,0:T(4,128)S(1)}, f32[4,512]{1,0:T(4,128)S(1)}, u32[]{:S(2)}, u32[]{:S(2)}) collective-permute-start(f32[4,512]{1,0:T(4,128)S(1)} %add.351), channel_id=1, source_target_pairs={{0,16},{8,24},{16,0},{24,8},{32,48},{40,56},{48,32},{56,40},{1,17}... | collective-permute-start | bytes 24584 | tf_op jit(solution)/shard_map/ppermute | solution.py:22
  168.3 2.4 %collective-permute-done.14 = f32[4,512]{1,0:T(4,128)S(1)} collective-permute-done((f32[4,512]{1,0:T(4,128)S(1)}, f32[4,512]{1,0:T(4,128)S(1)}, u32[]{:S(2)}, u32[]{:S(2)}) %collective-permute-start.14) | collective-permute-done | bytes 8224 | tf_op jit(solution)/shard_map/ppermute | solution.py:22
  170.7 3.2 %collective-permute-start.15 = (f32[4,512]{1,0:T(4,128)S(1)}, f32[4,512]{1,0:T(4,128)S(1)}, u32[]{:S(2)}, u32[]{:S(2)}) collective-permute-start(f32[4,512]{1,0:T(4,128)S(1)} %add.352), channel_id=1, source_target_pairs={{0,32},{8,40},{16,48},{24,56},{32,0},{40,8},{48,16},{56,24},{1,33}... | collective-permute-start | bytes 24584 | tf_op jit(solution)/shard_map/ppermute | solution.py:22
  174.8 3.4 %collective-permute-done.15 = f32[4,512]{1,0:T(4,128)S(1)} collective-permute-done((f32[4,512]{1,0:T(4,128)S(1)}, f32[4,512]{1,0:T(4,128)S(1)}, u32[]{:S(2)}, u32[]{:S(2)}) %collective-permute-start.15) | collective-permute-done | bytes 8224 | tf_op jit(solution)/shard_map/ppermute | solution.py:22
  (119 shorter events, 30.5 us)
Async XLA Ops:
  9.9 19.3 %copy-start.2 = (f32[20,2048]{1,0:T(8,128)S(1)}, f32[20,2048]{1,0:T(8,128)}, u32[]{:S(2)}) copy-start(f32[20,2048]{1,0:T(8,128)} %param.14) | copy-start | bytes 491524
  14.9 27.5 %copy-start.6 = (s32[4,2]{0,1:T(2,128)S(1)}, s32[4,2]{0,1:T(2,128)}, u32[]{:S(2)}) copy-start(s32[4,2]{0,1:T(2,128)} %param.21) | copy-start | bytes 100
  15.0 28.3 %copy-start.3 = (f32[20480]{0:T(1024)S(1)}, f32[20480]{0:T(1024)}, u32[]{:S(2)}) copy-start(f32[20480]{0:T(1024)} %param.18) | copy-start | bytes 245764
  15.0 6.0 %collective-permute-start = (f32[4,10240]{1,0:T(4,128)S(1)}, f32[4,10240]{1,0:T(4,128)S(1)}, u32[]{:S(2)}, u32[]{:S(2)}) collective-permute-start(f32[4,10240]{1,0:T(4,128)S(1)} %slice_select_fusion), channel_id=1, source_target_pairs={{0,2},{2,0},{4,6},{6,4},{1,3},{3,1},{5,7},{7,5},{8,10},{10,8},{12,... | collective-permute-start | bytes 491528 | tf_op jit(solution)/shard_map/ppermute | solution.py:33
  21.1 6.0 %collective-permute-start.1 = (f32[4,5120]{1,0:T(4,128)S(1)}, f32[4,5120]{1,0:T(4,128)S(1)}, u32[]{:S(2)}, u32[]{:S(2)}) collective-permute-start(f32[4,5120]{1,0:T(4,128)S(1)} %slice_select_fusion.1), channel_id=1, source_target_pairs={{0,4},{2,6},{4,0},{6,2},{1,5},{3,7},{5,1},{7,3},{8,12},{10,14},{12... | collective-permute-start | bytes 245768 | tf_op jit(solution)/shard_map/ppermute | solution.py:33
  27.2 9.2 %collective-permute-start.2 = (f32[4,2560]{1,0:T(4,128)S(1)}, f32[4,2560]{1,0:T(4,128)S(1)}, u32[]{:S(2)}, u32[]{:S(2)}) collective-permute-start(f32[4,2560]{1,0:T(4,128)S(1)} %slice_select_fusion.2), channel_id=1, source_target_pairs={{0,8},{8,0},{16,24},{24,16},{32,40},{40,32},{48,56},{56,48},{1,9},... | collective-permute-start | bytes 122888 | tf_op jit(solution)/shard_map/ppermute | solution.py:33
  31.6 9.7 %all-to-all-start = ((f32[20,4,512]{2,0,1:T(8,128)}), f32[20,4,512]{2,0,1:T(8,128)S(1)}, u32[]{:S(2)}, u32[]{:S(2)}) async-start(f32[20,4,512]{2,0,1:T(8,128)} %copy.28), calls=%async_computation | async-start | bytes 393216 | tf_op jit(solution)/shard_map/all_to_all | solution.py:94
  36.4 97.2 %all-gather.2.cloned.1.call-start = ((), (), s32[]{:S(2)}) async-start(), calls=%async_computation.1 | async-start | bytes 12779520 | tf_op jit(solution)/shard_map/all_gather | solution.py:96
  36.5 5.1 %collective-permute-start.3 = (f32[4,1280]{1,0:T(4,128)S(1)}, f32[4,1280]{1,0:T(4,128)S(1)}, u32[]{:S(2)}, u32[]{:S(2)}) collective-permute-start(f32[4,1280]{1,0:T(4,128)S(1)} %slice_select_fusion.3), channel_id=1, source_target_pairs={{0,16},{8,24},{16,0},{24,8},{32,48},{40,56},{48,32},{56,40},{1,17}... | collective-permute-start | bytes 61448 | tf_op jit(solution)/shard_map/ppermute | solution.py:33
  43.3 11.0 %copy-start.4 = (s32[5120]{0:T(1024)S(1)}, s32[5120]{0:T(1024)}, u32[]{:S(2)}) copy-start(s32[5120]{0:T(1024)} %param.15) | copy-start | bytes 61444
  54.3 1.2 collective-permute-start.4
  55.5 13.4 %collective-permute-start.5 = (f32[4,9]{1,0:T(4,128)S(1)}, f32[4,9]{1,0:T(4,128)S(1)}, u32[]{:S(2)}, u32[]{:S(2)}) collective-permute-start(f32[4,9]{1,0:T(4,128)S(1)} %add.341), channel_id=1, source_target_pairs={{0,2},{2,0},{4,6},{6,4},{1,3},{3,1},{5,7},{7,5},{8,10},{10,8},{12,... | collective-permute-start | bytes 440 | tf_op jit(solution)/shard_map/ppermute | solution.py:22
  68.9 20.7 %collective-permute-start.6 = (f32[4,9]{1,0:T(4,128)S(1)}, f32[4,9]{1,0:T(4,128)S(1)}, u32[]{:S(2)}, u32[]{:S(2)}) collective-permute-start(f32[4,9]{1,0:T(4,128)S(1)} %add.342), channel_id=1, source_target_pairs={{0,4},{2,6},{4,0},{6,2},{1,5},{3,7},{5,1},{7,3},{8,12},{10,14},{12... | collective-permute-start | bytes 440 | tf_op jit(solution)/shard_map/ppermute | solution.py:22
  89.6 3.7 %collective-permute-start.7 = (f32[4,9]{1,0:T(4,128)S(1)}, f32[4,9]{1,0:T(4,128)S(1)}, u32[]{:S(2)}, u32[]{:S(2)}) collective-permute-start(f32[4,9]{1,0:T(4,128)S(1)} %add.343), channel_id=1, source_target_pairs={{0,8},{8,0},{16,24},{24,16},{32,40},{40,32},{48,56},{56,48},{1,9},... | collective-permute-start | bytes 440 | tf_op jit(solution)/shard_map/ppermute | solution.py:22
  93.3 4.6 %collective-permute-start.8 = (f32[4,9]{1,0:T(4,128)S(1)}, f32[4,9]{1,0:T(4,128)S(1)}, u32[]{:S(2)}, u32[]{:S(2)}) collective-permute-start(f32[4,9]{1,0:T(4,128)S(1)} %add.344), channel_id=1, source_target_pairs={{0,16},{8,24},{16,0},{24,8},{32,48},{40,56},{48,32},{56,40},{1,17}... | collective-permute-start | bytes 440 | tf_op jit(solution)/shard_map/ppermute | solution.py:22
  98.0 8.8 %collective-permute-start.9 = (f32[4,9]{1,0:T(4,128)S(1)}, f32[4,9]{1,0:T(4,128)S(1)}, u32[]{:S(2)}, u32[]{:S(2)}) collective-permute-start(f32[4,9]{1,0:T(4,128)S(1)} %add.345), channel_id=1, source_target_pairs={{0,32},{8,40},{16,48},{24,56},{32,0},{40,8},{48,16},{56,24},{1,33}... | collective-permute-start | bytes 440 | tf_op jit(solution)/shard_map/ppermute | solution.py:22
  104.6 29.1 %copy-start.5 = (f32[512]{0:T(512)S(1)}, f32[512]{0:T(512)}, u32[]{:S(2)}) copy-start(f32[512]{0:T(512)} %param.19) | copy-start | bytes 6148
  133.7 15.7 %copy-start.9 = (s32[16]{0:T(128)S(1)}, s32[16]{0:T(128)}, u32[]{:S(2)}) copy-start(s32[16]{0:T(128)} %constant.189) | copy-start | bytes 196
  148.0 1.2 collective-permute-start.10
  149.2 3.7 %collective-permute-start.11 = (f32[4,512]{1,0:T(4,128)S(1)}, f32[4,512]{1,0:T(4,128)S(1)}, u32[]{:S(2)}, u32[]{:S(2)}) collective-permute-start(f32[4,512]{1,0:T(4,128)S(1)} %add.348), channel_id=1, source_target_pairs={{0,2},{2,0},{4,6},{6,4},{1,3},{3,1},{5,7},{7,5},{8,10},{10,8},{12,... | collective-permute-start | bytes 24584 | tf_op jit(solution)/shard_map/ppermute | solution.py:22
  152.9 9.5 %collective-permute-start.12 = (f32[4,512]{1,0:T(4,128)S(1)}, f32[4,512]{1,0:T(4,128)S(1)}, u32[]{:S(2)}, u32[]{:S(2)}) collective-permute-start(f32[4,512]{1,0:T(4,128)S(1)} %add.349), channel_id=1, source_target_pairs={{0,4},{2,6},{4,0},{6,2},{1,5},{3,7},{5,1},{7,3},{8,12},{10,14},{12... | collective-permute-start | bytes 24584 | tf_op jit(solution)/shard_map/ppermute | solution.py:22
  162.4 3.7 %collective-permute-start.13 = (f32[4,512]{1,0:T(4,128)S(1)}, f32[4,512]{1,0:T(4,128)S(1)}, u32[]{:S(2)}, u32[]{:S(2)}) collective-permute-start(f32[4,512]{1,0:T(4,128)S(1)} %add.350), channel_id=1, source_target_pairs={{0,8},{8,0},{16,24},{24,16},{32,40},{40,32},{48,56},{56,48},{1,9},... | collective-permute-start | bytes 24584 | tf_op jit(solution)/shard_map/ppermute | solution.py:22
  166.1 4.5 %collective-permute-start.14 = (f32[4,512]{1,0:T(4,128)S(1)}, f32[4,512]{1,0:T(4,128)S(1)}, u32[]{:S(2)}, u32[]{:S(2)}) collective-permute-start(f32[4,512]{1,0:T(4,128)S(1)} %add.351), channel_id=1, source_target_pairs={{0,16},{8,24},{16,0},{24,8},{32,48},{40,56},{48,32},{56,40},{1,17}... | collective-permute-start | bytes 24584 | tf_op jit(solution)/shard_map/ppermute | solution.py:22
  170.7 7.6 %collective-permute-start.15 = (f32[4,512]{1,0:T(4,128)S(1)}, f32[4,512]{1,0:T(4,128)S(1)}, u32[]{:S(2)}, u32[]{:S(2)}) collective-permute-start(f32[4,512]{1,0:T(4,128)S(1)} %add.352), channel_id=1, source_target_pairs={{0,32},{8,40},{16,48},{24,56},{32,0},{40,8},{48,16},{56,24},{1,33}... | collective-permute-start | bytes 24584 | tf_op jit(solution)/shard_map/ppermute | solution.py:22
  (4 other events, 24.8 us)
Sparse Core Ops, SparseCore 0:
  42.5 91.1 all-gather.1

commit v9 on v8

--- a/solution.py
+++ b/solution.py
@@ -10,7 +10,7 @@
 SNAP_LINE = ("snap", "line_0", "line_1", "line_2")
 HI = lax.Precision.HIGHEST
 STAGES = (("line_2", 1), ("line_1", 1), ("line_1", 2), ("line_0", 1), ("line_0", 2), ("line_0", 4))
-SCATTER = STAGES[1:5]
+SCATTER = STAGES[1:4]
 
 
 ramp_gain = 0.5
@@ -152,9 +152,9 @@
     pieces = everyone.reshape(line_count, block_units + extra_rows, block_width)[:, block_units:]
     line_0, line_1, line_2 = (lax.axis_size(a) for a in LINE)
     pieces = pieces.reshape(line_count, -1)[:, : NC * piece_width]
-    pieces = pieces.reshape(2, line_0 // 2, line_1, line_2, NC, piece_width).sum(axis=(0, 3))
+    pieces = pieces.reshape(4, line_0 // 4, line_1, line_2, NC, piece_width).sum(axis=(0, 3))
     pieces = pieces.reshape(-1, NC, piece_width)
-    pieces = jnp.take(pieces, jnp.array(piece_order([line_0 // 2, line_1])), axis=0)
+    pieces = jnp.take(pieces, jnp.array(piece_order([line_0 // 4, line_1])), axis=0)
     all_rows = pieces.transpose(1, 0, 2).reshape(NC, buses)
 
     sens_list = []

time: 187 us -> 190 us (1.016)
  local copies, waits for them, and re-layouts: 50.3 us -> 55.7 us
  starting transfers between devices: 37.4 us -> 34 us
    ppermute x4 -> x3, starting transfers between devices: 10.3 us -> 6.95 us  [line_scatter(): x = keep + lax.ppermute(give, axis, [(i, i ^ step) for i in range(size)])]
    ppermute x4 -> x3, waiting for transfers between devices: 7.32 us -> 4.31 us  [line_scatter(): x = keep + lax.ppermute(give, axis, [(i, i ^ step) for i in range(size)])]
    reshape x1, local copies, waits for them, and re-layouts: 0.65 us -> 3.12 us  [body(): pieces.reshape(4, line_0 // 4, line_1, line_2, NC, piece_width)]
    unnamed x23 -> x27, local copies, waits for them, and re-layouts: 13.2 us -> 14.4 us
  transfers between devices with their start and end apart: 18 -> 17, of which waited for: 13 -> 10; matrix products, arithmetic and copies ran while one was open for 33% -> 35% of each run, Pallas kernels for 0% -> 0%
where the time goes in v9:
time: 190 us; the launch traced here: 189 us
  local copies, waits for them, and re-layouts  55.7 us (29%)
  between operations  40.1 us (21%)
  starting transfers between devices  34 us (18%)
  matrix products  26.4 us (14%)
  waiting for transfers between devices  23 us (12%)
  other arithmetic  9.41 us (5%)
    ppermute x12, starting transfers between devices, line_total(): x = x + lax.ppermute(x, axis, [(i, i ^ step) for i in range(size)])  22.2 us
    gather x1, local copies, waits for them, and re-layouts, body(): jnp.take(ptdf_rows, order_ids, axis=1)  17.4 us
    dot_general x1, matrix products, body(): jnp.dot(columns, everyone, preferred_element_type=jnp.float32, precision=HI)  15.2 us
    unnamed x27, local copies, waits for them, and re-layouts  14.4 us
    ppermute x12, waiting for transfers between devices, line_total(): x = x + lax.ppermute(x, axis, [(i, i ^ step) for i in range(size)])  14.1 us
    dot_general x1, matrix products, body(): jnp.dot(ptdf_rows, probes, preferred_element_type=jnp.float32, precision=HI)  10.8 us
    ppermute x3, starting transfers between devices, line_scatter(): x = keep + lax.ppermute(give, axis, [(i, i ^ step) for i in range(size)])  6.95 us
    gather x1, local copies, waits for them, and re-layouts, body(): jnp.take(ptdf_rows, rows_of, axis=0)  4.83 us
  transfers between devices with their start and end apart: 17, of which 10 were waited for; matrix products, arithmetic and copies ran while one was open for 35% of the time, Pallas kernels for 0%

profile of v9, /device:TPU:2, one launch (start us, length us, event | category | flops | bytes accessed | tf_op | source)
XLA Modules:
  0.0 188.7 jit_solution(16315755196071900228)
XLA Ops:
  9.9 4.8 %gather_fusion.3 = f32[4,20480]{1,0:T(4,128)S(1)} fusion(f32[128,20480]{1,0:T(8,128)} %param.13, s32[1024]{0:T(1024)S(1)} %pad_clamp_fusion.1), kind=kCustom, calls=%fused_computation.3 | custom fusion | bytes 655376 | tf_op jit(solution)/shard_map/jit(_take)/gather | solution.py:77
  16.7 4.3 %collective-permute-done = f32[4,10240]{1,0:T(4,128)S(1)} collective-permute-done((f32[4,10240]{1,0:T(4,128)S(1)}, f32[4,10240]{1,0:T(4,128)S(1)}, u32[]{:S(2)}, u32[]{:S(2)}) %collective-permute-start) | collective-permute-done | bytes 163872 | tf_op jit(solution)/shard_map/ppermute | solution.py:33
  21.1 3.3 %collective-permute-start.1 = (f32[4,5120]{1,0:T(4,128)S(1)}, f32[4,5120]{1,0:T(4,128)S(1)}, u32[]{:S(2)}, u32[]{:S(2)}) collective-permute-start(f32[4,5120]{1,0:T(4,128)S(1)} %slice_select_fusion.1), channel_id=1, source_target_pairs={{0,4},{2,6},{4,0},{6,2},{1,5},{3,7},{5,1},{7,3},{8,12},{10,14},{12... | collective-permute-start | bytes 245768 | tf_op jit(solution)/shard_map/ppermute | solution.py:33
  26.8 4.8 %all-to-all-start = ((f32[20,4,512]{2,0,1:T(8,128)}), f32[20,4,512]{2,0,1:T(8,128)S(1)}, u32[]{:S(2)}, u32[]{:S(2)}) async-start(f32[20,4,512]{2,0,1:T(8,128)} %copy.28), calls=%async_computation | async-start | bytes 393216 | tf_op jit(solution)/shard_map/all_to_all | solution.py:94
  31.7 2.0 %collective-permute-start.2 = (f32[4,2560]{1,0:T(4,128)S(1)}, f32[4,2560]{1,0:T(4,128)S(1)}, u32[]{:S(2)}, u32[]{:S(2)}) collective-permute-start(f32[4,2560]{1,0:T(4,128)S(1)} %slice_select_fusion.2), channel_id=1, source_target_pairs={{0,8},{8,0},{16,24},{24,16},{32,40},{40,32},{48,56},{56,48},{1,9},... | collective-permute-start | bytes 122888 | tf_op jit(solution)/shard_map/ppermute | solution.py:33
  33.7 2.8 %all-to-all-done = f32[20,4,512]{2,0,1:T(8,128)S(1)} async-done(((f32[20,4,512]{2,0,1:T(8,128)}), f32[20,4,512]{2,0,1:T(8,128)S(1)}, u32[]{:S(2)}, u32[]{:S(2)}) %all-to-all-start) | async-done | bytes 163872 | tf_op jit(solution)/shard_map/all_to_all | solution.py:94
  38.2 10.8 %fusion = f32[9,128]{1,0:T(8,128)S(1)} fusion(f32[128,20480]{1,0:T(8,128)} %param.13, f32[20480,8]{0,1:T(8,128)S(1)} %fusion.4, f32[20480,1]{0,1:T(1,128)S(1)} %bitcast.75), kind=kOutput, calls=%fused_computation.7 | convolution fusion | flops 283299840 | bytes 11227648 | tf_op jit(solution)/shard_map/dot_general | solution.py:111
  51.1 11.8 %copy.27 = f32[128,20480]{0,1:T(8,128)} copy(f32[128,20480]{1,0:T(8,128)} %param.13) | data formatting | bytes 20971520 | tf_op args[0]
  62.9 2.0 %collective-permute-start.5 = (f32[4,9]{1,0:T(4,128)S(1)}, f32[4,9]{1,0:T(4,128)S(1)}, u32[]{:S(2)}, u32[]{:S(2)}) collective-permute-start(f32[4,9]{1,0:T(4,128)S(1)} %add.333), channel_id=1, source_target_pairs={{0,4},{2,6},{4,0},{6,2},{1,5},{3,7},{5,1},{7,3},{8,12},{10,14},{12... | collective-permute-start | bytes 440 | tf_op jit(solution)/shard_map/ppermute | solution.py:22
  65.0 17.4 %gather_fusion = f32[5120,128]{1,0:T(8,128)S(1)} fusion(f32[128,20480]{0,1:T(8,128)} %copy.27, s32[5120]{0:T(1024)S(1)} %broadcast_clamp_fusion), kind=kCustom, calls=%fused_computation | custom fusion | bytes 5263360 | tf_op jit(solution)/shard_map/jit(_take)/gather | solution.py:101
  82.4 2.2 %collective-permute-start.6 = (f32[4,9]{1,0:T(4,128)S(1)}, f32[4,9]{1,0:T(4,128)S(1)}, u32[]{:S(2)}, u32[]{:S(2)}) collective-permute-start(f32[4,9]{1,0:T(4,128)S(1)} %add.334), channel_id=1, source_target_pairs={{0,8},{8,0},{16,24},{24,16},{32,40},{40,32},{48,56},{56,48},{1,9},... | collective-permute-start | bytes 440 | tf_op jit(solution)/shard_map/ppermute | solution.py:22
  84.7 2.4 %broadcast_select_fusion = f32[128,64,80]{0,2,1:T(8,128)} fusion(f32[128,64,80]{0,2,1:T(8,128)S(1)} %bitcast.64, pred[64,80]{1,0:T(8,128)(4,1)S(1)} %copy.25), kind=kLoop, calls=%fused_computation.11 | loop fusion | flops 655360 | bytes 5248000 | tf_op jit(solution)/shard_map/jit(_take)/select_n | solution.py:101
  87.1 3.2 %collective-permute-start.7 = (f32[4,9]{1,0:T(4,128)S(1)}, f32[4,9]{1,0:T(4,128)S(1)}, u32[]{:S(2)}, u32[]{:S(2)}) collective-permute-start(f32[4,9]{1,0:T(4,128)S(1)} %add.335), channel_id=1, source_target_pairs={{0,16},{8,24},{16,0},{24,8},{32,48},{40,56},{48,32},{56,40},{1,17}... | collective-permute-start | bytes 440 | tf_op jit(solution)/shard_map/ppermute | solution.py:22
  91.9 6.1 %collective-permute-start.8 = (f32[4,9]{1,0:T(4,128)S(1)}, f32[4,9]{1,0:T(4,128)S(1)}, u32[]{:S(2)}, u32[]{:S(2)}) collective-permute-start(f32[4,9]{1,0:T(4,128)S(1)} %add.336), channel_id=1, source_target_pairs={{0,32},{8,40},{16,48},{24,56},{32,0},{40,8},{48,16},{56,24},{1,33}... | collective-permute-start | bytes 440 | tf_op jit(solution)/shard_map/ppermute | solution.py:22
  98.7 2.0 %pad.12 = f32[128,64,104]{0,2,1:T(8,128)S(1)} pad(f32[128,64,80]{0,2,1:T(8,128)} %broadcast_select_fusion, f32[]{:T(128)} %constant.128.clone.1), padding=0_0x0_0x0_24 | pad | bytes 6029316 | tf_op jit(solution)/shard_map/jit(_pad)/pad | solution.py:102
  129.3 15.2 %convolution_subtract_fusion = f32[128,512]{1,0:T(8,128)S(1)} fusion(f32[128,6656]{0,1:T(8,128)S(1)} %bitcast.61, f32[6656,512]{1,0:T(8,128)} %all-gather.2.cloned.1.call-done, f32[512]{0:T(512)S(1)} %copy-done.7, f32[128]{0:T(128)S(1)} %get-tuple-element.25), kind=kOutput, calls=%fused_computation.12 | convolution fusion | flops 5234622464 | bytes 17304064 | tf_op jit(solution)/shard_map/dot_general | solution.py:148
  146.9 3.4 %collective-permute-done.10 = f32[4,512]{1,0:T(4,128)S(1)} collective-permute-done((f32[4,512]{1,0:T(4,128)S(1)}, f32[4,512]{1,0:T(4,128)S(1)}, u32[]{:S(2)}, u32[]{:S(2)}) %collective-permute-start.10) | collective-permute-done | bytes 8224 | tf_op jit(solution)/shard_map/ppermute | solution.py:22
  154.8 2.2 %slice.476 = f32[64,24,512]{2,1,0:T(8,128)S(1)} slice(f32[64,104,512]{2,1,0:T(8,128)} %bitcast.60), slice={[0:64], [80:104], [0:512]} | slice | bytes 6291456 | tf_op jit(solution)/shard_map/slice | solution.py:152
  157.0 1.8 copy.30
  160.5 3.1 %reshape.353 = f32[4,2,4,2,4,2560]{5,4,3,2,1,0:T(4,128)S(1)} reshape(f32[64,10240]{1,0:T(8,128)} %slice.477) | data formatting | bytes 5242880 | tf_op jit(solution)/shard_map/reshape | solution.py:155
  166.5 2.3 %collective-permute-done.12 = f32[4,512]{1,0:T(4,128)S(1)} collective-permute-done((f32[4,512]{1,0:T(4,128)S(1)}, f32[4,512]{1,0:T(4,128)S(1)}, u32[]{:S(2)}, u32[]{:S(2)}) %collective-permute-start.12) | collective-permute-done | bytes 8224 | tf_op jit(solution)/shard_map/ppermute | solution.py:22
  170.6 2.8 %collective-permute-done.13 = f32[4,512]{1,0:T(4,128)S(1)} collective-permute-done((f32[4,512]{1,0:T(4,128)S(1)}, f32[4,512]{1,0:T(4,128)S(1)}, u32[]{:S(2)}, u32[]{:S(2)}) %collective-permute-start.13) | collective-permute-done | bytes 8224 | tf_op jit(solution)/shard_map/ppermute | solution.py:22
  173.4 3.4 %collective-permute-start.14 = (f32[4,512]{1,0:T(4,128)S(1)}, f32[4,512]{1,0:T(4,128)S(1)}, u32[]{:S(2)}, u32[]{:S(2)}) collective-permute-start(f32[4,512]{1,0:T(4,128)S(1)} %add.343), channel_id=1, source_target_pairs={{0,32},{8,40},{16,48},{24,56},{32,0},{40,8},{48,16},{56,24},{1,33}... | collective-permute-start | bytes 24584 | tf_op jit(solution)/shard_map/ppermute | solution.py:22
  177.9 3.1 %collective-permute-done.14 = f32[4,512]{1,0:T(4,128)S(1)} collective-permute-done((f32[4,512]{1,0:T(4,128)S(1)}, f32[4,512]{1,0:T(4,128)S(1)}, u32[]{:S(2)}, u32[]{:S(2)}) %collective-permute-start.14) | collective-permute-done | bytes 8224 | tf_op jit(solution)/shard_map/ppermute | solution.py:22
  (119 shorter events, 31.2 us)
Async XLA Ops:
  7.2 17.2 %copy-start.4 = (f32[20,2048]{1,0:T(8,128)S(1)}, f32[20,2048]{1,0:T(8,128)}, u32[]{:S(2)}) copy-start(f32[20,2048]{1,0:T(8,128)} %param.14) | copy-start | bytes 491524
  14.7 22.6 %copy-start.8 = (s32[4,2]{0,1:T(2,128)S(1)}, s32[4,2]{0,1:T(2,128)}, u32[]{:S(2)}) copy-start(s32[4,2]{0,1:T(2,128)} %param.21) | copy-start | bytes 100
  14.8 23.4 %copy-start.5 = (f32[20480]{0:T(1024)S(1)}, f32[20480]{0:T(1024)}, u32[]{:S(2)}) copy-start(f32[20480]{0:T(1024)} %param.18) | copy-start | bytes 245764
  15.0 6.0 %collective-permute-start = (f32[4,10240]{1,0:T(4,128)S(1)}, f32[4,10240]{1,0:T(4,128)S(1)}, u32[]{:S(2)}, u32[]{:S(2)}) collective-permute-start(f32[4,10240]{1,0:T(4,128)S(1)} %slice_select_fusion), channel_id=1, source_target_pairs={{0,2},{2,0},{4,6},{6,4},{1,3},{3,1},{5,7},{7,5},{8,10},{10,8},{12,... | collective-permute-start | bytes 491528 | tf_op jit(solution)/shard_map/ppermute | solution.py:33
  21.1 10.5 %collective-permute-start.1 = (f32[4,5120]{1,0:T(4,128)S(1)}, f32[4,5120]{1,0:T(4,128)S(1)}, u32[]{:S(2)}, u32[]{:S(2)}) collective-permute-start(f32[4,5120]{1,0:T(4,128)S(1)} %slice_select_fusion.1), channel_id=1, source_target_pairs={{0,4},{2,6},{4,0},{6,2},{1,5},{3,7},{5,1},{7,3},{8,12},{10,14},{12... | collective-permute-start | bytes 245768 | tf_op jit(solution)/shard_map/ppermute | solution.py:33
  26.8 9.7 %all-to-all-start = ((f32[20,4,512]{2,0,1:T(8,128)}), f32[20,4,512]{2,0,1:T(8,128)S(1)}, u32[]{:S(2)}, u32[]{:S(2)}) async-start(f32[20,4,512]{2,0,1:T(8,128)} %copy.28), calls=%async_computation | async-start | bytes 393216 | tf_op jit(solution)/shard_map/all_to_all | solution.py:94
  31.6 97.7 %all-gather.2.cloned.1.call-start = ((), (), s32[]{:S(2)}) async-start(), calls=%async_computation.1 | async-start | bytes 13844480 | tf_op jit(solution)/shard_map/all_gather | solution.py:96
  31.7 4.8 %collective-permute-start.2 = (f32[4,2560]{1,0:T(4,128)S(1)}, f32[4,2560]{1,0:T(4,128)S(1)}, u32[]{:S(2)}, u32[]{:S(2)}) collective-permute-start(f32[4,2560]{1,0:T(4,128)S(1)} %slice_select_fusion.2), channel_id=1, source_target_pairs={{0,8},{8,0},{16,24},{24,16},{32,40},{40,32},{48,56},{56,48},{1,9},... | collective-permute-start | bytes 122888 | tf_op jit(solution)/shard_map/ppermute | solution.py:33
  38.2 11.0 %copy-start.6 = (s32[5120]{0:T(1024)S(1)}, s32[5120]{0:T(1024)}, u32[]{:S(2)}) copy-start(s32[5120]{0:T(1024)} %param.15) | copy-start | bytes 61444
  49.2 1.2 collective-permute-start.3
  50.4 12.5 %collective-permute-start.4 = (f32[4,9]{1,0:T(4,128)S(1)}, f32[4,9]{1,0:T(4,128)S(1)}, u32[]{:S(2)}, u32[]{:S(2)}) collective-permute-start(f32[4,9]{1,0:T(4,128)S(1)} %add.332), channel_id=1, source_target_pairs={{0,2},{2,0},{4,6},{6,4},{1,3},{3,1},{5,7},{7,5},{8,10},{10,8},{12,... | collective-permute-start | bytes 440 | tf_op jit(solution)/shard_map/ppermute | solution.py:22
  62.9 19.5 %collective-permute-start.5 = (f32[4,9]{1,0:T(4,128)S(1)}, f32[4,9]{1,0:T(4,128)S(1)}, u32[]{:S(2)}, u32[]{:S(2)}) collective-permute-start(f32[4,9]{1,0:T(4,128)S(1)} %add.333), channel_id=1, source_target_pairs={{0,4},{2,6},{4,0},{6,2},{1,5},{3,7},{5,1},{7,3},{8,12},{10,14},{12... | collective-permute-start | bytes 440 | tf_op jit(solution)/shard_map/ppermute | solution.py:22
  82.4 4.7 %collective-permute-start.6 = (f32[4,9]{1,0:T(4,128)S(1)}, f32[4,9]{1,0:T(4,128)S(1)}, u32[]{:S(2)}, u32[]{:S(2)}) collective-permute-start(f32[4,9]{1,0:T(4,128)S(1)} %add.334), channel_id=1, source_target_pairs={{0,8},{8,0},{16,24},{24,16},{32,40},{40,32},{48,56},{56,48},{1,9},... | collective-permute-start | bytes 440 | tf_op jit(solution)/shard_map/ppermute | solution.py:22
  87.1 4.9 %collective-permute-start.7 = (f32[4,9]{1,0:T(4,128)S(1)}, f32[4,9]{1,0:T(4,128)S(1)}, u32[]{:S(2)}, u32[]{:S(2)}) collective-permute-start(f32[4,9]{1,0:T(4,128)S(1)} %add.335), channel_id=1, source_target_pairs={{0,16},{8,24},{16,0},{24,8},{32,48},{40,56},{48,32},{56,40},{1,17}... | collective-permute-start | bytes 440 | tf_op jit(solution)/shard_map/ppermute | solution.py:22
  90.9 38.4 %copy-start.7 = (f32[512]{0:T(512)S(1)}, f32[512]{0:T(512)}, u32[]{:S(2)}) copy-start(f32[512]{0:T(512)} %param.19) | copy-start | bytes 6148
  91.9 8.8 %collective-permute-start.8 = (f32[4,9]{1,0:T(4,128)S(1)}, f32[4,9]{1,0:T(4,128)S(1)}, u32[]{:S(2)}, u32[]{:S(2)}) collective-permute-start(f32[4,9]{1,0:T(4,128)S(1)} %add.336), channel_id=1, source_target_pairs={{0,32},{8,40},{16,48},{24,56},{32,0},{40,8},{48,16},{56,24},{1,33}... | collective-permute-start | bytes 440 | tf_op jit(solution)/shard_map/ppermute | solution.py:22
  129.3 17.6 %copy-start.11 = (s32[8]{0:T(128)S(1)}, s32[8]{0:T(128)}, u32[]{:S(2)}) copy-start(s32[8]{0:T(128)} %constant.178) | copy-start | bytes 100
  145.5 1.2 collective-permute-start.9
  146.7 3.7 %collective-permute-start.10 = (f32[4,512]{1,0:T(4,128)S(1)}, f32[4,512]{1,0:T(4,128)S(1)}, u32[]{:S(2)}, u32[]{:S(2)}) collective-permute-start(f32[4,512]{1,0:T(4,128)S(1)} %add.339), channel_id=1, source_target_pairs={{0,2},{2,0},{4,6},{6,4},{1,3},{3,1},{5,7},{7,5},{8,10},{10,8},{12,... | collective-permute-start | bytes 24584 | tf_op jit(solution)/shard_map/ppermute | solution.py:22
  150.3 14.8 %collective-permute-start.11 = (f32[4,512]{1,0:T(4,128)S(1)}, f32[4,512]{1,0:T(4,128)S(1)}, u32[]{:S(2)}, u32[]{:S(2)}) collective-permute-start(f32[4,512]{1,0:T(4,128)S(1)} %add.340), channel_id=1, source_target_pairs={{0,4},{2,6},{4,0},{6,2},{1,5},{3,7},{5,1},{7,3},{8,12},{10,14},{12... | collective-permute-start | bytes 24584 | tf_op jit(solution)/shard_map/ppermute | solution.py:22
  163.6 17.4 %copy-start.3 = (f32[128,512]{1,0:T(8,128)S(1)}, f32[128,512]{1,0:T(8,128)}, u32[]{:S(2)}) copy-start(f32[128,512]{1,0:T(8,128)} %copy-done.2) | copy-start | bytes 786436
  165.1 3.7 %collective-permute-start.12 = (f32[4,512]{1,0:T(4,128)S(1)}, f32[4,512]{1,0:T(4,128)S(1)}, u32[]{:S(2)}, u32[]{:S(2)}) collective-permute-start(f32[4,512]{1,0:T(4,128)S(1)} %add.341), channel_id=1, source_target_pairs={{0,8},{8,0},{16,24},{24,16},{32,40},{40,32},{48,56},{56,48},{1,9},... | collective-permute-start | bytes 24584 | tf_op jit(solution)/shard_map/ppermute | solution.py:22
  168.8 4.5 %collective-permute-start.13 = (f32[4,512]{1,0:T(4,128)S(1)}, f32[4,512]{1,0:T(4,128)S(1)}, u32[]{:S(2)}, u32[]{:S(2)}) collective-permute-start(f32[4,512]{1,0:T(4,128)S(1)} %add.342), channel_id=1, source_target_pairs={{0,16},{8,24},{16,0},{24,8},{32,48},{40,56},{48,32},{56,40},{1,17}... | collective-permute-start | bytes 24584 | tf_op jit(solution)/shard_map/ppermute | solution.py:22
  173.4 7.6 %collective-permute-start.14 = (f32[4,512]{1,0:T(4,128)S(1)}, f32[4,512]{1,0:T(4,128)S(1)}, u32[]{:S(2)}, u32[]{:S(2)}) collective-permute-start(f32[4,512]{1,0:T(4,128)S(1)} %add.343), channel_id=1, source_target_pairs={{0,32},{8,40},{16,48},{24,56},{32,0},{40,8},{48,16},{56,24},{1,33}... | collective-permute-start | bytes 24584 | tf_op jit(solution)/shard_map/ppermute | solution.py:22
  (5 other events, 28.3 us)
Sparse Core Ops, SparseCore 0:
  37.4 91.8 all-gather.1
